TPU v7x, 32 devices: a whole 2x2x4 slice. The times are simulated.
32 devices in a mesh: groups: 2 (over y), brick: 4 (over z), split: 2 (over x), sub: 2 (over core).
Axes of the slice: x: 2, y: 2, z: 4, core: 2. Of those that a mesh axis runs over, the one named last changes fastest.
Arguments:
- grad_out: bfloat16 [128, 32, 512], P(('groups', 'brick', 'split', 'sub')), parts along dimension 0, may hold values from -6 to 6
- features: bfloat16 [128, 32, 512], P(('groups', 'brick', 'split', 'sub')), parts along dimension 0, may hold values from -6 to 6
- kernel: bfloat16 [27, 32, 32], replicated, may hold values from -0.21875 to 0.21875
- block_count: int32 [32], P(('groups', 'brick', 'split', 'sub')), parts along dimension 0, may hold values from 1 to 4, as said below
- neighbours: int32 [128, 26], P(('groups', 'brick', 'split', 'sub')), parts along dimension 0, may hold values from 0 to 16, as said below
Outputs:
- grad_features: bfloat16 [128, 32, 512], P(('groups', 'brick', 'split', 'sub')), parts along dimension 0
- kernel_grad: float32 [54, 32, 32], P('groups'), parts along dimension 0
There are 2 independent parts, one for each index of `groups`. A program takes and returns all parts, laid end to end along the dimension named above; an argument that names none is the same for every part. Nothing has to cross between parts.
Inputs may be any that keep to these rules, and one draw needn't show every extreme that they name: `block_count`: in every brick one device holds exactly 4 live blocks. `neighbours`: entry (q, k) is the slot, within the brick at block height offset c of direction k (periodic), of the active block at the neighbouring position (periodic in the first two dimensions), or 16 if that position is inactive; rows of slots that are not live hold 16; every active block has one slot.
All inputs are finite; a program needn't handle non-finite values.
Results may differ from a plain program's by a relative error of at most 0.001.
Values may be sent and summed in bfloat16 or wider, within the bound.
No kernel may reach another device: no remote copies, remote signals or barrier semaphores. Data moves between devices by JAX's collectives and lax.ppermute only.
A program may use at most 64 MiB of HBM per device.

v0:
```python
import math

import jax
import jax.numpy as jnp
from jax import lax
from jax.sharding import PartitionSpec as P

DIRECTIONS = [(a, b, c) for a in (-1, 0, 1) for b in (-1, 0, 1) for c in (-1, 0, 1)]
NEIGHBOURS = [d for d in DIRECTIONS if d != (0, 0, 0)]


def from_behind(block, axis, distance):
    devices = range(lax.axis_size(axis))
    route = [((i - distance) % len(devices), i) for i in devices]
    return lax.ppermute(block, axis, route)


def window(offset):
    if offset < 0:
        return slice(7, 8)
    if offset > 0:
        return slice(0, 1)
    return slice(0, 8)


def assemble(pieces):
    planes = []
    for a in (-1, 0, 1):
        row_list = []
        for b in (-1, 0, 1):
            row_list.append(jnp.concatenate([pieces[a, b, c] for c in (-1, 0, 1)], axis=4))
        planes.append(jnp.concatenate(row_list, axis=3))
    return jnp.concatenate(planes, axis=2)


def contract(padded, source, kernel):
    blocks_here, channels = (source.shape[0], source.shape[1])
    input_grad = jnp.zeros((blocks_here, channels, 512), jnp.float32)
    weight_grads = {}
    for c in (-1, 0, 1):
        shifted = jnp.concatenate(
            [
                padded[:, :, 1 - a : 9 - a, 1 - b : 9 - b, 1 - c : 9 - c].reshape(
                    blocks_here, channels, 512
                )
                for a in (-1, 0, 1)
                for b in (-1, 0, 1)
            ],
            axis=1,
        )
        offset_ids = [(a + 1) * 9 + (b + 1) * 3 + (c + 1) for a in (-1, 0, 1) for b in (-1, 0, 1)]
        stacked = jnp.stack([kernel[i] for i in offset_ids], axis=0)
        mixing = jnp.transpose(stacked, (1, 0, 2)).reshape(channels, 9 * channels)
        input_grad = input_grad + jnp.einsum(
            "ik,bkv->biv", mixing, shifted, preferred_element_type=jnp.float32
        )
        weight_part = jnp.einsum(
            "biv,bkv->ik", source, shifted, preferred_element_type=jnp.float32
        ).reshape(channels, 9, channels)
        for j, i in enumerate(offset_ids):
            weight_grads[i] = weight_part[:, j]
    return (input_grad, jnp.stack([weight_grads[i] for i in range(27)], axis=0))


def with_zero(fetched_rows):
    return jnp.concatenate(
        [fetched_rows, jnp.zeros((1,) + fetched_rows.shape[1:], fetched_rows.dtype)], axis=0
    )


def on_device(grad_out, features, kernel, block_count, neighbours):
    blocks_here, channels = (grad_out.shape[0], grad_out.shape[1])
    cubes_here = grad_out.reshape(blocks_here, channels, 8, 8, 8)
    shell_rows = jnp.concatenate(
        [cubes_here[:, :, 0], cubes_here[:, :, 7], cubes_here[:, :, :, 0], cubes_here[:, :, :, 7]],
        axis=2,
    ).reshape(blocks_here, channels, 256)
    lower_layer = cubes_here[:, :, :, :, 0].reshape(blocks_here, channels * 64)
    upper_layer = cubes_here[:, :, :, :, 7].reshape(blocks_here, channels * 64)
    shell_all, lower_all, upper_all = (
        lax.all_gather(shell_rows, ("split", "sub"), axis=0, tiled=True),
        lax.all_gather(lower_layer, ("split", "sub"), axis=0, tiled=True),
        lax.all_gather(upper_layer, ("split", "sub"), axis=0, tiled=True),
    )
    from_below = from_behind(upper_all, "brick", 1)
    from_above = from_behind(lower_all, "brick", -1)
    shell_table = with_zero(shell_all)
    layer_tables = {-1: with_zero(from_below), 1: with_zero(from_above)}
    pieces = {(0, 0, 0): cubes_here}
    for k, (a, b, c) in enumerate(NEIGHBOURS):
        slot_index = neighbours[:, k]
        if c == 0:
            fetched = jnp.take(shell_table, slot_index, axis=0).reshape(
                blocks_here, channels, 4, 8, 8
            )
            if a != 0:
                face_rows = fetched[:, :, 1 if a < 0 else 0]
                pieces[a, b, c] = face_rows[:, :, None, window(b), :]
            else:
                face_rows = fetched[:, :, 3 if b < 0 else 2]
                pieces[a, b, c] = face_rows[:, :, :, None, :]
        else:
            layer_rows = jnp.take(layer_tables[c], slot_index, axis=0).reshape(
                blocks_here, channels, 8, 8
            )
            pieces[a, b, c] = layer_rows[:, :, window(a), window(b)][:, :, :, :, None]
    padded = assemble(pieces)
    live_mask = (jnp.arange(blocks_here) < block_count[0])[:, None, None]
    masked = jnp.where(live_mask, features, jnp.zeros_like(features))
    input_grad, weight_grads = contract(padded, masked, kernel)
    grad_features = jnp.where(live_mask, input_grad, jnp.zeros_like(input_grad)).astype(
        jnp.bfloat16
    )
    totals = lax.psum(weight_grads, ("brick", "split", "sub"))
    scaling = 1.0 / math.sqrt(
        lax.axis_size("brick") * lax.axis_size("split") * lax.axis_size("sub") * blocks_here * 512
    )
    return (grad_features, totals * scaling)


def solution(mesh):
    placed = (
        P(("groups", "brick", "split", "sub"), None, None),
        P(("groups", "brick", "split", "sub"), None, None),
        P(),
        P(("groups", "brick", "split", "sub")),
        P(("groups", "brick", "split", "sub"), None),
    )
    return jax.shard_map(
        on_device,
        mesh=mesh,
        in_specs=placed,
        out_specs=(P(("groups", "brick", "split", "sub"), None, None), P("groups", None, None)),
        check_vma=False,
    )
```

profile of v0, /device:TPU:0, one launch (start us, length us, event | category | flops | bytes accessed | tf_op | source)
XLA Modules:
  0.0 252.1 jit_solution(10741603956274095577)
XLA Ops:
  9.1 6.2 %all-gather = bf16[4,4,2048]{2,1,0:T(4,128)(2,1)S(1)} all-gather(bf16[1,4,2048]{2,1,0:T(4,128)(2,1)S(1)} %reshape.484), channel_id=1, replica_groups=mesh['groups'=2,'brick'=4,'split'=2,'sub'=2] {'split','sub'}, dimensions={0}, use_global_device_ids=true | all-gather | bytes 81920 | tf_op jit(solution)/shard_map/all_gather | solution.py:83
  15.3 2.2 collective-permute-start
  18.0 5.2 %all-gather.1 = bf16[4,4,2048]{2,1,0:T(4,128)(2,1)S(1)} all-gather(bf16[1,4,2048]{2,1,0:T(4,128)(2,1)S(1)} %reshape.486), channel_id=1, replica_groups=mesh['groups'=2,'brick'=4,'split'=2,'sub'=2] {'split','sub'}, dimensions={0}, use_global_device_ids=true | all-gather | bytes 81920 | tf_op jit(solution)/shard_map/all_gather | solution.py:82
  23.2 2.1 collective-permute-start.1
  36.5 6.1 %all_gather.10 = bf16[16,32,256]{2,1,0:T(8,128)(2,1)S(1)} all-gather(bf16[4,32,256]{2,1,0:T(8,128)(2,1)S(1)} %copy.281), channel_id=1, replica_groups=mesh['groups'=2,'brick'=4,'split'=2,'sub'=2] {'split','sub'}, dimensions={0}, use_global_device_ids=true | all-gather | bytes 327680 | tf_op jit(solution)/shard_map/all_gather | solution.py:81
  89.7 1.9 copy.344
  94.3 1.9 copy.342
  97.3 3.7 %maximum_maximum_fusion = bf16[4,32,9,10,10]{1,4,3,2,0:T(8,128)(2,1)S(1)} fusion(bf16[4,32,1,1,1]{1,4,3,2,0:T(2,128)(2,1)S(1)} %copy-done.33, bf16[4,32,1,1,8]{1,4,3,2,0:T(8,128)(2,1)S(1)} %copy-done.28, bf16[4,32,1,1,1]{1,4,3,2,0:T(2,128)(2,1)S(1)} %copy-done.31, bf16[4,32,1,8,1]{1,4,3,2,0:T(2,128)(2,1)S(1)} %copy-done.26, ...), kind=kLoop, calls=%fused_computation.26 | loop fusion | flops 4147200 | bytes 460800 | tf_op jit(solution)/shard_map/concatenate | solution.py:33
  101.0 2.2 fusion.7
  103.3 1.9 copy.341
  105.1 1.9 copy.340
  107.0 1.9 copy.339
  108.9 1.9 copy.330
  110.7 1.9 copy.329
  122.3 3.3 %maximum_maximum_fusion.1 = bf16[4,32,9,10,10]{1,4,3,2,0:T(8,128)(2,1)S(1)} fusion(bf16[4,32,8,1,1]{1,4,3,2,0:T(2,128)(2,1)} %copy-done.25, bf16[4,32,8,1,8]{1,4,3,2,0:T(8,128)(2,1)S(1)} %slice_bitcast_fusion.4, bf16[4,32,8,1,1]{1,4,3,2,0:T(2,128)(2,1)} %copy-done.23, bf16[4,32,8,8,1]{1,4,3,2,0:T(2,128)(2,1)S(1)} %copy.288, ...), kind=kLoop, calls=%fused_computation.27 | loop fusion | flops 4147200 | bytes 460800 | tf_op jit(solution)/shard_map/concatenate | solution.py:33
  125.5 2.5 fusion.6
  128.0 1.9 copy.347
  129.9 1.9 copy.346
  131.8 1.9 copy.345
  133.6 1.9 copy.335
  135.5 1.9 copy.334
  137.4 1.9 copy.333
  139.3 1.9 copy.325
  155.9 87.3 %all-reduce.5.cloned.1.call-done = f32[27,32,32]{1,2,0:T(8,128)} async-done(((f32[27,32,32]{1,2,0:T(8,128)}), f32[27,32,32]{1,2,0:T(8,128)}) %all-reduce.5.cloned.1.call-update) | async-done | bytes 110608 | tf_op jit(solution)/shard_map/psum | solution.py:114
  (364 shorter events, 88.7 us)
Async XLA Ops:
  7.2 18.1 %copy-start = (s32[4,26]{1,0:T(4,128)S(1)}, s32[4,26]{1,0:T(4,128)}, u32[]{:S(2)}) copy-start(s32[4,26]{1,0:T(4,128)} %param.13) | copy-start | bytes 1252
  7.2 236.1 %all-reduce.5.cloned.1.call-start = ((), (), s32[]{:S(2)}) async-start(), calls=%async_computation | async-start | bytes 884736 | tf_op jit(solution)/shard_map/psum | solution.py:114
  15.3 37.6 %collective-permute-start = (bf16[16,2048]{1,0:T(8,128)(2,1)S(1)}, bf16[16,2048]{1,0:T(8,128)(2,1)S(1)}, u32[]{:S(2)}, u32[]{:S(2)}) collective-permute-start(bf16[16,2048]{1,0:T(8,128)(2,1)S(1)} %reshape.485), channel_id=1, source_target_pairs={{12,0},{0,4},{4,8},{8,12},{13,1},{1,5},{5,9},{9,13},{14,2},{2,6},{... | collective-permute-start | bytes 196616 | tf_op jit(solution)/shard_map/ppermute | solution.py:15
  23.2 45.5 %collective-permute-start.1 = (bf16[16,2048]{1,0:T(8,128)(2,1)S(1)}, bf16[16,2048]{1,0:T(8,128)(2,1)S(1)}, u32[]{:S(2)}, u32[]{:S(2)}) collective-permute-start(bf16[16,2048]{1,0:T(8,128)(2,1)S(1)} %reshape.487), channel_id=1, source_target_pairs={{4,0},{8,4},{12,8},{0,12},{5,1},{9,5},{13,9},{1,13},{6,2},{10,6},{... | collective-permute-start | bytes 196616 | tf_op jit(solution)/shard_map/ppermute | solution.py:15
  60.5 36.8 %copy-start.23 = (bf16[4,32,8,1,1]{1,4,3,2,0:T(2,128)(2,1)}, bf16[4,32,8,1,1]{1,4,3,2,0:T(2,128)(2,1)S(1)}, u32[]{:S(2)}) copy-start(bf16[4,32,8,1,1]{1,4,3,2,0:T(2,128)(2,1)S(1)} %copy.292) | copy-start | bytes 6148
  75.5 21.8 %copy-start.24 = (bf16[4,32,8,1,1]{1,4,3,2,0:T(2,128)(2,1)}, bf16[4,32,8,1,1]{1,4,3,2,0:T(2,128)(2,1)S(1)}, u32[]{:S(2)}) copy-start(bf16[4,32,8,1,1]{1,4,3,2,0:T(2,128)(2,1)S(1)} %copy.286) | copy-start | bytes 6148
  76.2 21.0 %copy-start.25 = (bf16[4,32,8,1,1]{1,4,3,2,0:T(2,128)(2,1)}, bf16[4,32,8,1,1]{1,4,3,2,0:T(2,128)(2,1)S(1)}, u32[]{:S(2)}) copy-start(bf16[4,32,8,1,1]{1,4,3,2,0:T(2,128)(2,1)S(1)} %copy.293) | copy-start | bytes 6148
  94.3 3.0 %copy-start.27 = (bf16[4,32,1,1,8]{1,4,3,2,0:T(8,128)(2,1)S(1)}, bf16[4,32,1,1,8]{1,4,3,2,0:T(8,128)(2,1)}, u32[]{:S(2)}) copy-start(bf16[4,32,1,1,8]{1,4,3,2,0:T(8,128)(2,1)} %slice_bitcast_fusion.40) | copy-start | bytes 6148
  94.3 3.0 %copy-start.28 = (bf16[4,32,1,1,8]{1,4,3,2,0:T(8,128)(2,1)S(1)}, bf16[4,32,1,1,8]{1,4,3,2,0:T(8,128)(2,1)}, u32[]{:S(2)}) copy-start(bf16[4,32,1,1,8]{1,4,3,2,0:T(8,128)(2,1)} %slice_bitcast_fusion.39) | copy-start | bytes 6148
  94.3 3.0 %copy-start.30 = (bf16[4,32,1,1,1]{1,4,3,2,0:T(2,128)(2,1)S(1)}, bf16[4,32,1,1,1]{1,4,3,2,0:T(2,128)(2,1)}, u32[]{:S(2)}) copy-start(bf16[4,32,1,1,1]{1,4,3,2,0:T(2,128)(2,1)} %broadcast_in_dim.250) | copy-start | bytes 772
  94.3 3.0 %copy-start.31 = (bf16[4,32,1,1,1]{1,4,3,2,0:T(2,128)(2,1)S(1)}, bf16[4,32,1,1,1]{1,4,3,2,0:T(2,128)(2,1)}, u32[]{:S(2)}) copy-start(bf16[4,32,1,1,1]{1,4,3,2,0:T(2,128)(2,1)} %broadcast_in_dim.252) | copy-start | bytes 772
  94.3 3.0 %copy-start.32 = (bf16[4,32,1,1,1]{1,4,3,2,0:T(2,128)(2,1)S(1)}, bf16[4,32,1,1,1]{1,4,3,2,0:T(2,128)(2,1)}, u32[]{:S(2)}) copy-start(bf16[4,32,1,1,1]{1,4,3,2,0:T(2,128)(2,1)} %broadcast_in_dim.251) | copy-start | bytes 772
  94.3 3.0 %copy-start.33 = (bf16[4,32,1,1,1]{1,4,3,2,0:T(2,128)(2,1)S(1)}, bf16[4,32,1,1,1]{1,4,3,2,0:T(2,128)(2,1)}, u32[]{:S(2)}) copy-start(bf16[4,32,1,1,1]{1,4,3,2,0:T(2,128)(2,1)} %broadcast_in_dim.253) | copy-start | bytes 772
  114.3 6.4 %copy-start.2 = (bf16[4,32,512]{2,1,0:T(8,128)(2,1)S(1)}, bf16[4,32,512]{2,1,0:T(8,128)(2,1)}, u32[]{:S(2)}) copy-start(bf16[4,32,512]{2,1,0:T(8,128)(2,1)} %param.9) | copy-start | bytes 393220
  142.0 3.7 %copy-start.5 = (bf16[4,32,512]{2,1,0:T(8,128)(2,1)S(1)}, bf16[4,32,512]{2,1,0:T(8,128)(2,1)}, u32[]{:S(2)}) copy-start(bf16[4,32,512]{2,1,0:T(8,128)(2,1)} %copy.321) | copy-start | bytes 393220
  142.0 3.8 %copy-start.7 = (bf16[4,32,512]{2,1,0:T(8,128)(2,1)S(1)}, bf16[4,32,512]{2,1,0:T(8,128)(2,1)}, u32[]{:S(2)}) copy-start(bf16[4,32,512]{2,1,0:T(8,128)(2,1)} %copy.322) | copy-start | bytes 393220
  142.0 3.8 %copy-start.6 = (bf16[4,32,512]{2,1,0:T(8,128)(2,1)S(1)}, bf16[4,32,512]{2,1,0:T(8,128)(2,1)}, u32[]{:S(2)}) copy-start(bf16[4,32,512]{2,1,0:T(8,128)(2,1)} %copy.332) | copy-start | bytes 393220
  142.8 3.6 %copy-start.18 = (bf16[4,32,512]{2,1,0:T(8,128)(2,1)S(1)}, bf16[4,32,512]{2,1,0:T(8,128)(2,1)}, u32[]{:S(2)}) copy-start(bf16[4,32,512]{2,1,0:T(8,128)(2,1)} %copy.333) | copy-start | bytes 393220
  142.8 4.3 %copy-start.16 = (bf16[4,32,512]{2,1,0:T(8,128)(2,1)S(1)}, bf16[4,32,512]{2,1,0:T(8,128)(2,1)}, u32[]{:S(2)}) copy-start(bf16[4,32,512]{2,1,0:T(8,128)(2,1)} %copy.334) | copy-start | bytes 393220
  142.8 5.0 %copy-start.14 = (bf16[4,32,512]{2,1,0:T(8,128)(2,1)S(1)}, bf16[4,32,512]{2,1,0:T(8,128)(2,1)}, u32[]{:S(2)}) copy-start(bf16[4,32,512]{2,1,0:T(8,128)(2,1)} %copy.335) | copy-start | bytes 393220
  142.8 5.6 %copy-start.17 = (bf16[4,32,512]{2,1,0:T(8,128)(2,1)S(1)}, bf16[4,32,512]{2,1,0:T(8,128)(2,1)}, u32[]{:S(2)}) copy-start(bf16[4,32,512]{2,1,0:T(8,128)(2,1)} %copy.323) | copy-start | bytes 393220
  142.8 5.6 %copy-start.15 = (bf16[4,32,512]{2,1,0:T(8,128)(2,1)S(1)}, bf16[4,32,512]{2,1,0:T(8,128)(2,1)}, u32[]{:S(2)}) copy-start(bf16[4,32,512]{2,1,0:T(8,128)(2,1)} %copy.324) | copy-start | bytes 393220
  142.8 5.7 %copy-start.13 = (bf16[4,32,512]{2,1,0:T(8,128)(2,1)S(1)}, bf16[4,32,512]{2,1,0:T(8,128)(2,1)}, u32[]{:S(2)}) copy-start(bf16[4,32,512]{2,1,0:T(8,128)(2,1)} %copy.325) | copy-start | bytes 393220
  143.8 4.7 %copy-start.22 = (bf16[32,9,32]{0,2,1:T(8,128)(2,1)S(1)}, bf16[32,9,32]{0,2,1:T(8,128)(2,1)}, u32[]{:S(2)}) copy-start(bf16[32,9,32]{0,2,1:T(8,128)(2,1)} %copy.326) | copy-start | bytes 55300
  (13 other events, 27.2 us)
Sparse Core Ops, SparseCore 0:
  153.3 89.8 all-reduce.4
where the time goes:
time: 254 us; the launch traced here: 252 us
  local copies, waits for them, and re-layouts  107 us (42%)
  waiting for transfers between devices  87.4 us (34%)
  blocking collectives  17.5 us (7%)
  between operations  16.4 us (6%)
  other arithmetic  13.6 us (5%)
  matrix products  5.92 us (2%)
  starting transfers between devices  4.28 us (2%)
    psum x1, waiting for transfers between devices, on_device(): totals = lax.psum(weight_grads, ('brick', 'split', 'sub'))  87.3 us
    reshape x26, local copies, waits for them, and re-layouts, contract(): padded[:, :, 1 - a:9 - a, 1 - b:9 - b, 1 - c:9 - c]  34.4 us
    unnamed x132, local copies, waits for them, and re-layouts  21.5 us
    gather x18, local copies, waits for them, and re-layouts, on_device(): jnp.take(layer_tables[c], slot_index, axis=0)  10.3 us
    concatenate x2, other arithmetic, assemble(): return jnp.concatenate(planes, axis=2)  6.94 us
    slice x4, local copies, waits for them, and re-layouts, contract(): padded[:, :, 1 - a:9 - a, 1 - b:9 - b, 1 - c:9 - c]  6.8 us
    slice x22, local copies, waits for them, and re-layouts, on_device(): pieces[a, b, c] = layer_rows[:, :, window(a), window(b)][:, :, :, :, None]  6.71 us
    broadcast_in_dim x16, local copies, waits for them, and re-layouts, on_device(): pieces[a, b, c] = layer_rows[:, :, window(a), window(b)][:, :, :, :, None]  6.67 us
  transfers between devices with their start and end apart: 3, of which 1 were waited for; matrix products, arithmetic and copies ran while one was open for 15% of the time, Pallas kernels for 0%

commit v1 on v0

v1 whole, which is shorter than its diff:
```python
import math

import jax
import jax.numpy as jnp
from jax import lax
from jax.experimental import pallas as pl
from jax.experimental.pallas import tpu as pltpu
from jax.sharding import PartitionSpec as P

DIRECTIONS = [(a, b, c) for a in (-1, 0, 1) for b in (-1, 0, 1) for c in (-1, 0, 1)]
NEIGHBOURS = [d for d in DIRECTIONS if d != (0, 0, 0)]
VOX = 512


def from_behind(block, axis, distance):
    devices = range(lax.axis_size(axis))
    route = [((i - distance) % len(devices), i) for i in devices]
    return lax.ppermute(block, axis, route)


def butterfly_sum(x, axes):
    for axis in axes:
        n = lax.axis_size(axis)
        if n & (n - 1):
            x = lax.psum(x, axis)
            continue
        bit = 1
        while bit < n:
            x = x + lax.ppermute(x, axis, [(i, i ^ bit) for i in range(n)])
            bit *= 2
    return x


def sources_of(d):
    a, b, c = d
    found = []
    for ex in sorted({0, -a}):
        for ey in sorted({0, -b}):
            for ez in sorted({0, -c}):
                if (ex, ey, ez) != (0, 0, 0):
                    found.append((ex, ey, ez))
    return sorted(found, key=lambda e: sum(1 for t in e if t != 0))


def make_kernel(blocks, channels, slots):
    def kernel(nbr_ref, cnt_ref, g_ref, f_ref, gath_ref, kmix_ref, gf_ref, wg_ref,
               same_ref, lay_ref, stack_ref):
        lane = lax.broadcasted_iota(jnp.int32, (channels, VOX), 1)
        coord = (lane // 64, (lane // 8) % 8, lane % 8)

        def boundary(axis, sign):
            return coord[axis] == (7 if sign < 0 else 0)

        rows = lax.broadcasted_iota(jnp.int32, (64, VOX), 0)
        cols = lax.broadcasted_iota(jnp.int32, (64, VOX), 1)
        spread = (cols // 8 == rows).astype(jnp.bfloat16)
        same_ref[slots] = jnp.zeros((channels, VOX), jnp.bfloat16)
        lay_ref[0, slots] = jnp.zeros((channels, VOX), jnp.bfloat16)
        lay_ref[1, slots] = jnp.zeros((channels, VOX), jnp.bfloat16)

        def fill(q, carry):
            row = gath_ref[q]
            same_ref[q] = row[:, 0:VOX]
            for t in range(2):
                layer = row[:, VOX + 64 * t:VOX + 64 * (t + 1)]
                wide = jnp.dot(layer, spread, preferred_element_type=jnp.float32)
                lay_ref[t, q] = wide.astype(jnp.bfloat16)
            return carry

        lax.fori_loop(0, slots, fill, 0)

        gf_ref[...] = jnp.zeros_like(gf_ref)
        wg_ref[...] = jnp.zeros_like(wg_ref)

        def body(s, carry):
            own = g_ref[s].astype(jnp.float32)

            def neighbour(e):
                q = jnp.minimum(nbr_ref[s, NEIGHBOURS.index(e)], slots)
                if e[2] == 0:
                    return same_ref[q].astype(jnp.float32)
                return lay_ref[0 if e[2] < 0 else 1, q].astype(jnp.float32)

            for di, d in enumerate(DIRECTIONS):
                z = own
                for e in sources_of(d):
                    region = None
                    for axis in range(3):
                        if e[axis] != 0:
                            part = boundary(axis, e[axis])
                            region = part if region is None else (region & part)
                    z = jnp.where(region, neighbour(e), z)
                a, b, c = d
                if c != 0:
                    z = jnp.where(coord[2] == (0 if c > 0 else 7),
                                  pltpu.roll(z, (-7 * c) % VOX, 1),
                                  pltpu.roll(z, c % VOX, 1))
                if b != 0:
                    z = jnp.where(coord[1] == (0 if b > 0 else 7),
                                  pltpu.roll(z, (-56 * b) % VOX, 1),
                                  pltpu.roll(z, (8 * b) % VOX, 1))
                if a != 0:
                    z = pltpu.roll(z, (64 * a) % VOX, 1)
                stack_ref[di * channels:(di + 1) * channels, :] = z.astype(jnp.bfloat16)
            st = stack_ref[...]
            gf = jnp.dot(kmix_ref[...], st, preferred_element_type=jnp.float32)
            gf_ref[s] = gf.astype(jnp.bfloat16)
            wg_ref[...] += lax.dot_general(
                f_ref[s], st, (((1,), (1,)), ((), ())), preferred_element_type=jnp.float32
            )
            return carry

        lax.fori_loop(0, jnp.minimum(cnt_ref[0], blocks), body, 0)

    return kernel


def local_conv(neighbours, block_count, grad_out, features, gathered, kmix):
    blocks, channels = grad_out.shape[0], grad_out.shape[1]
    slots = gathered.shape[0]
    smem = pl.BlockSpec(memory_space=pltpu.SMEM)
    vmem = pl.BlockSpec(memory_space=pltpu.VMEM)
    return pl.pallas_call(
        make_kernel(blocks, channels, slots),
        out_shape=(
            jax.ShapeDtypeStruct((blocks, channels, VOX), jnp.bfloat16),
            jax.ShapeDtypeStruct((channels, 27 * channels), jnp.float32),
        ),
        in_specs=[smem, smem, vmem, vmem, vmem, vmem],
        out_specs=(vmem, vmem),
        scratch_shapes=[
            pltpu.VMEM((slots + 1, channels, VOX), jnp.bfloat16),
            pltpu.VMEM((2, slots + 1, channels, VOX), jnp.bfloat16),
            pltpu.VMEM((27 * channels, VOX), jnp.bfloat16),
        ],
    )(neighbours, block_count, grad_out, features, gathered, kmix)


def on_device(grad_out, features, kernel, block_count, neighbours):
    blocks, channels = grad_out.shape[0], grad_out.shape[1]
    cubes = grad_out.reshape(blocks, channels, 8, 8, 8)
    lowest = cubes[:, :, :, :, 0].reshape(blocks, channels, 64)
    highest = cubes[:, :, :, :, 7].reshape(blocks, channels, 64)
    from_below = from_behind(highest, "brick", 1)
    from_above = from_behind(lowest, "brick", -1)
    packed = jnp.concatenate([grad_out, from_below, from_above], axis=2)
    gathered = lax.all_gather(packed, ("split", "sub"), axis=0, tiled=True)
    kmix = jnp.transpose(kernel, (1, 0, 2)).reshape(channels, 27 * channels)
    grad_features, wg = local_conv(neighbours, block_count, grad_out, features, gathered, kmix)
    wg = butterfly_sum(wg, ("sub", "split", "brick"))
    scaling = 1.0 / math.sqrt(
        lax.axis_size("brick") * lax.axis_size("split") * lax.axis_size("sub") * blocks * VOX
    )
    totals = jnp.transpose(wg.reshape(channels, 27, channels), (1, 0, 2)) * scaling
    return (grad_features, totals)


def solution(mesh):
    placed = (
        P(("groups", "brick", "split", "sub"), None, None),
        P(("groups", "brick", "split", "sub"), None, None),
        P(),
        P(("groups", "brick", "split", "sub")),
        P(("groups", "brick", "split", "sub"), None),
    )
    return jax.shard_map(
        on_device,
        mesh=mesh,
        in_specs=placed,
        out_specs=(P(("groups", "brick", "split", "sub"), None, None), P("groups", None, None)),
        check_vma=False,
    )
```

time: 254 us -> 55.9 us (0.22)
  local copies, waits for them, and re-layouts: 107 us -> 3.72 us
  waiting for transfers between devices: 87.4 us -> 22.2 us
  between operations: 16.4 us -> 1.4 us
  Pallas kernels: 0 us -> 13.6 us
  other arithmetic: 13.6 us -> 1.05 us
  blocking collectives: 17.5 us -> 8.33 us
  matrix products: 5.92 us -> 0 us
    psum x1 -> x0, waiting for transfers between devices: 87.3 us -> none  [on_device(): totals = lax.psum(weight_grads, ('brick', 'split', 'sub'))]
    reshape x43 -> x1, local copies, waits for them, and re-layouts: 39.9 us -> 0.86 us  [on_device(): kmix = jnp.transpose(kernel, (1, 0, 2)).reshape(channels, 27 * channels)]
    unnamed x132 -> x8, local copies, waits for them, and re-layouts: 21.5 us -> 2.24 us
    ppermute x0 -> x4, waiting for transfers between devices: none -> 17.8 us  [butterfly_sum(): x = x + lax.ppermute(x, axis, [(i, i ^ bit) for i in range(n)])]
    slice x33 -> x1, local copies, waits for them, and re-layouts: 15.5 us -> 0.17 us  [on_device(): highest = cubes[:, :, :, :, 7].reshape(blocks, channels, 64)]
    gather x26 -> x0, local copies, waits for them, and re-layouts: 14.7 us -> none  [the longest x18 10.3 us: on_device(): jnp.take(layer_tables[c], slot_index, axis=0)]
    pallas_call x0 -> x1, Pallas kernels: none -> 13.6 us  [local_conv(): pl.pallas_call(make_kernel(blocks, channels, slots), out_shape=(jax.Shape...]
    concatenate x4 -> x1, other arithmetic: 9.47 us -> 0.09 us  [on_device(): packed = jnp.concatenate([grad_out, from_below, from_above], axis=2)]
  transfers between devices with their start and end apart: 3 -> 6, of which waited for: 1 -> 6; matrix products, arithmetic and copies ran while one was open for 15% -> 2% of each run, Pallas kernels for 0% -> 0%
where the time goes in v1:
time: 55.9 us; the launch traced here: 55.7 us
  waiting for transfers between devices  22.2 us (40%)
  Pallas kernels  13.6 us (24%)
  blocking collectives  8.33 us (15%)
  starting transfers between devices  5.4 us (10%)
  local copies, waits for them, and re-layouts  3.72 us (7%)
  between operations  1.4 us (3%)
  other arithmetic  1.05 us (2%)
    ppermute x4, waiting for transfers between devices, butterfly_sum(): x = x + lax.ppermute(x, axis, [(i, i ^ bit) for i in range(n)])  17.8 us
    pallas_call x1, Pallas kernels, local_conv(): pl.pallas_call(make_kernel(blocks, channels, slots), out_shape=(jax.Shape...  13.6 us
    all_gather x1, blocking collectives, on_device(): gathered = lax.all_gather(packed, ('split', 'sub'), axis=0, tiled=True)  8.33 us
    ppermute x2, starting transfers between devices, from_behind(): return lax.ppermute(block, axis, route)  5.19 us
    ppermute x2, waiting for transfers between devices, from_behind(): return lax.ppermute(block, axis, route)  4.33 us
    unnamed x8, local copies, waits for them, and re-layouts  2.24 us
  transfers between devices with their start and end apart: 6, of which 6 were waited for; matrix products, arithmetic and copies ran while one was open for 2% of the time, Pallas kernels for 0%

profile of v1, /device:TPU:0, one launch (start us, length us, event | category | flops | bytes accessed | tf_op | source)
XLA Modules:
  0.0 55.7 jit_solution(478014940607562068)
XLA Ops:
  0.6 1.2 %copy.16 = bf16[4,32,512]{1,2,0:T(8,128)(2,1)S(1)} copy(bf16[4,32,512]{2,1,0:T(8,128)(2,1)} %g_ref.1) | data formatting | bytes 262144 | tf_op args[0]
  1.8 0.2 fusion
  2.0 0.0 copy-start.1
  2.0 5.1 %collective-permute-start.1 = (bf16[4,32,64]{1,2,0:T(8,128)(2,1)S(1)}, bf16[4,32,64]{1,2,0:T(8,128)(2,1)S(1)}, u32[]{:S(2)}, u32[]{:S(2)}) collective-permute-start(bf16[4,32,64]{1,2,0:T(8,128)(2,1)S(1)} %bitcast.12), channel_id=1, source_target_pairs={{4,0},{8,4},{12,8},{0,12},{5,1},{9,5},{13,9},{1,13},{6,2},{10,6},{... | collective-permute-start | bytes 49160 | tf_op jit(solution)/shard_map/ppermute | solution.py:18
  7.2 0.1 collective-permute-start
  7.9 0.1 copy.19
  8.0 0.9 %reshape.14.kmix_ref = bf16[32,864]{1,0:T(8,128)(2,1)} reshape(bf16[32,27,32]{2,1,0:T(8,128)(2,1)S(1)} %copy.19) | data formatting | bytes 110592 | tf_op jit(solution)/shard_map/reshape | solution.py:148
  8.9 0.3 collective-permute-done.1
  9.2 0.1 copy.18
  9.3 4.0 %collective-permute-done = bf16[4,32,64]{1,2,0:T(8,128)(2,1)S(1)} collective-permute-done((bf16[4,32,64]{1,2,0:T(8,128)(2,1)S(1)}, bf16[4,32,64]{1,2,0:T(8,128)(2,1)S(1)}, u32[]{:S(2)}, u32[]{:S(2)}) %collective-permute-start) | collective-permute-done | bytes 16416 | tf_op jit(solution)/shard_map/ppermute | solution.py:18
  13.3 0.1 copy.17
  13.4 0.1 pad_maximum_fusion
  13.5 8.3 %all_gather.3.gath_ref = bf16[16,32,640]{2,1,0:T(8,128)(2,1)} all-gather(bf16[4,32,640]{2,1,0:T(8,128)(2,1)S(1)} %pad_maximum_fusion), channel_id=1, replica_groups=mesh['groups'=2,'brick'=4,'split'=2,'sub'=2] {'split','sub'}, dimensions={0}, use_global_device_ids=true | all-gather | bytes 819200 | tf_op jit(solution)/shard_map/all_gather | solution.py:147
  21.8 13.6 %shard_map.68 = (bf16[4,32,512]{2,1,0:T(8,128)(2,1)}, f32[32,864]{1,0:T(8,128)}) custom-call(s32[4,26]{1,0:T(4,128)} %nbr_ref.1, s32[1]{0:T(128)S(6)} %copy.27.cnt_ref, bf16[4,32,512]{2,1,0:T(8,128)(2,1)} %g_ref.1, bf16[4,32,512]{2,1,0:T(8,128)(2,1)} %f_ref.1, bf16[16,32,640]{2,1,0:T(8,128)(2,1)} %all_gather.3.gath_ref, bf16[32,864]{1,0:T(8,128)(2,1)} %reshape.14.kmix_ref), custom_call_target="tpu_custom_call" | custom-call | tf_op jit(solution)/shard_map/pallas_call | solution.py:123
  35.4 1.5 %collective-permute-done.2 = f32[32,864]{1,0:T(8,128)S(1)} collective-permute-done((f32[32,864]{1,0:T(8,128)}, f32[32,864]{1,0:T(8,128)S(1)}, u32[]{:S(2)}, u32[]{:S(2)}) %collective-permute-start.2) | collective-permute-done | bytes 110624 | tf_op jit(solution)/shard_map/ppermute | solution.py:29
  37.0 0.9 %add.12 = f32[32,864]{1,0:T(8,128)S(1)} add(f32[32,864]{1,0:T(8,128)} %get-tuple-element.5, f32[32,864]{1,0:T(8,128)S(1)} %collective-permute-done.2) | non-fusion elementwise | flops 27648 | bytes 331776 | tf_op jit(solution)/shard_map/add | solution.py:29
  37.9 0.1 collective-permute-start.3
  38.0 5.2 %collective-permute-done.3 = f32[32,864]{1,0:T(8,128)S(1)} collective-permute-done((f32[32,864]{1,0:T(8,128)S(1)}, f32[32,864]{1,0:T(8,128)S(1)}, u32[]{:S(2)}, u32[]{:S(2)}) %collective-permute-start.3) | collective-permute-done | bytes 110624 | tf_op jit(solution)/shard_map/ppermute | solution.py:29
  43.2 0.1 collective-permute-start.4
  43.3 4.8 %collective-permute-done.4 = f32[32,864]{1,0:T(8,128)S(1)} collective-permute-done((f32[32,864]{1,0:T(8,128)S(1)}, f32[32,864]{1,0:T(8,128)S(1)}, u32[]{:S(2)}, u32[]{:S(2)}) %collective-permute-start.4) | collective-permute-done | bytes 110624 | tf_op jit(solution)/shard_map/ppermute | solution.py:29
  48.0 0.1 collective-permute-start.5
  48.1 6.3 %collective-permute-done.5 = f32[32,864]{1,0:T(8,128)S(1)} collective-permute-done((f32[32,864]{1,0:T(8,128)S(1)}, f32[32,864]{1,0:T(8,128)S(1)}, u32[]{:S(2)}, u32[]{:S(2)}) %collective-permute-start.5) | collective-permute-done | bytes 110624 | tf_op jit(solution)/shard_map/ppermute | solution.py:29
  54.5 0.2 mul.14
  54.7 1.0 %copy.20 = f32[27,32,32]{2,1,0:T(8,128)} copy(f32[27,32,32]{2,0,1:T(8,128)S(1)} %bitcast.9) | data formatting | bytes 221184
  (9 shorter events, 0.1 us)
Async XLA Ops:
  2.0 5.9 %copy-start.1 = (bf16[27,32,32]{2,1,0:T(8,128)(2,1)S(1)}, bf16[27,32,32]{2,1,0:T(8,128)(2,1)}, u32[]{:S(2)}) copy-start(bf16[27,32,32]{2,1,0:T(8,128)(2,1)} %param.7) | copy-start | bytes 165892
  2.0 7.2 %collective-permute-start.1 = (bf16[4,32,64]{1,2,0:T(8,128)(2,1)S(1)}, bf16[4,32,64]{1,2,0:T(8,128)(2,1)S(1)}, u32[]{:S(2)}, u32[]{:S(2)}) collective-permute-start(bf16[4,32,64]{1,2,0:T(8,128)(2,1)S(1)} %bitcast.12), channel_id=1, source_target_pairs={{4,0},{8,4},{12,8},{0,12},{5,1},{9,5},{13,9},{1,13},{6,2},{10,6},{... | collective-permute-start | bytes 49160 | tf_op jit(solution)/shard_map/ppermute | solution.py:18
  7.2 6.1 %collective-permute-start = (bf16[4,32,64]{1,2,0:T(8,128)(2,1)S(1)}, bf16[4,32,64]{1,2,0:T(8,128)(2,1)S(1)}, u32[]{:S(2)}, u32[]{:S(2)}) collective-permute-start(bf16[4,32,64]{1,2,0:T(8,128)(2,1)S(1)} %bitcast.13), channel_id=1, source_target_pairs={{12,0},{0,4},{4,8},{8,12},{13,1},{1,5},{5,9},{9,13},{14,2},{2,6},{... | collective-permute-start | bytes 49160 | tf_op jit(solution)/shard_map/ppermute | solution.py:18
  8.9 4.5 %copy-start = (bf16[4,32,512]{2,1,0:T(8,128)(2,1)S(1)}, bf16[4,32,512]{2,1,0:T(8,128)(2,1)}, u32[]{:S(2)}) copy-start(bf16[4,32,512]{2,1,0:T(8,128)(2,1)} %g_ref.1) | copy-start | bytes 393220
  35.4 1.5 %collective-permute-start.2 = (f32[32,864]{1,0:T(8,128)}, f32[32,864]{1,0:T(8,128)S(1)}, u32[]{:S(2)}, u32[]{:S(2)}) collective-permute-start(f32[32,864]{1,0:T(8,128)} %get-tuple-element.5), channel_id=1, source_target_pairs={{0,1},{1,0},{2,3},{3,2},{4,5},{5,4},{6,7},{7,6},{8,9},{9,8},{10,11... | collective-permute-start | bytes 331784 | tf_op jit(solution)/shard_map/ppermute | solution.py:29
  37.9 5.3 %collective-permute-start.3 = (f32[32,864]{1,0:T(8,128)S(1)}, f32[32,864]{1,0:T(8,128)S(1)}, u32[]{:S(2)}, u32[]{:S(2)}) collective-permute-start(f32[32,864]{1,0:T(8,128)S(1)} %add.12), channel_id=1, source_target_pairs={{0,2},{2,0},{1,3},{3,1},{4,6},{6,4},{5,7},{7,5},{8,10},{10,8},{9,1... | collective-permute-start | bytes 331784 | tf_op jit(solution)/shard_map/ppermute | solution.py:29
  43.2 4.9 %collective-permute-start.4 = (f32[32,864]{1,0:T(8,128)S(1)}, f32[32,864]{1,0:T(8,128)S(1)}, u32[]{:S(2)}, u32[]{:S(2)}) collective-permute-start(f32[32,864]{1,0:T(8,128)S(1)} %add.13), channel_id=1, source_target_pairs={{0,4},{4,0},{8,12},{12,8},{1,5},{5,1},{9,13},{13,9},{2,6},{6,2},{1... | collective-permute-start | bytes 331784 | tf_op jit(solution)/shard_map/ppermute | solution.py:29
  48.0 6.4 %collective-permute-start.5 = (f32[32,864]{1,0:T(8,128)S(1)}, f32[32,864]{1,0:T(8,128)S(1)}, u32[]{:S(2)}, u32[]{:S(2)}) collective-permute-start(f32[32,864]{1,0:T(8,128)S(1)} %add.14), channel_id=1, source_target_pairs={{0,8},{4,12},{8,0},{12,4},{1,9},{5,13},{9,1},{13,5},{2,10},{6,14},... | collective-permute-start | bytes 331784 | tf_op jit(solution)/shard_map/ppermute | solution.py:29

commit v2 on v1

--- a/solution.py
+++ b/solution.py
@@ -73,35 +73,48 @@
         wg_ref[...] = jnp.zeros_like(wg_ref)
 
         def body(s, carry):
-            own = g_ref[s].astype(jnp.float32)
+            own = g_ref[s]
 
             def neighbour(e):
                 q = jnp.minimum(nbr_ref[s, NEIGHBOURS.index(e)], slots)
                 if e[2] == 0:
-                    return same_ref[q].astype(jnp.float32)
-                return lay_ref[0 if e[2] < 0 else 1, q].astype(jnp.float32)
+                    return same_ref[q]
+                return lay_ref[0 if e[2] < 0 else 1, q]
 
-            for di, d in enumerate(DIRECTIONS):
-                z = own
-                for e in sources_of(d):
-                    region = None
-                    for axis in range(3):
-                        if e[axis] != 0:
-                            part = boundary(axis, e[axis])
-                            region = part if region is None else (region & part)
-                    z = jnp.where(region, neighbour(e), z)
-                a, b, c = d
-                if c != 0:
-                    z = jnp.where(coord[2] == (0 if c > 0 else 7),
-                                  pltpu.roll(z, (-7 * c) % VOX, 1),
-                                  pltpu.roll(z, c % VOX, 1))
-                if b != 0:
-                    z = jnp.where(coord[1] == (0 if b > 0 else 7),
-                                  pltpu.roll(z, (-56 * b) % VOX, 1),
-                                  pltpu.roll(z, (8 * b) % VOX, 1))
-                if a != 0:
-                    z = pltpu.roll(z, (64 * a) % VOX, 1)
-                stack_ref[di * channels:(di + 1) * channels, :] = z.astype(jnp.bfloat16)
+            for a in (-1, 0, 1):
+                for b in (-1, 0, 1):
+                    rx = boundary(0, -a) if a != 0 else None
+                    ry = boundary(1, -b) if b != 0 else None
+                    flat = own
+                    if a != 0:
+                        flat = jnp.where(rx, neighbour((-a, 0, 0)), flat)
+                    if b != 0:
+                        flat = jnp.where(ry, neighbour((0, -b, 0)), flat)
+                    if a != 0 and b != 0:
+                        flat = jnp.where(rx & ry, neighbour((-a, -b, 0)), flat)
+                    for c in (-1, 0, 1):
+                        z = flat
+                        if c != 0:
+                            y = neighbour((0, 0, -c))
+                            if a != 0:
+                                y = jnp.where(rx, neighbour((-a, 0, -c)), y)
+                            if b != 0:
+                                y = jnp.where(ry, neighbour((0, -b, -c)), y)
+                            if a != 0 and b != 0:
+                                y = jnp.where(rx & ry, neighbour((-a, -b, -c)), y)
+                            z = jnp.where(boundary(2, -c), y, flat)
+                        if c != 0:
+                            z = jnp.where(coord[2] == (0 if c > 0 else 7),
+                                          pltpu.roll(z, (-7 * c) % VOX, 1),
+                                          pltpu.roll(z, c % VOX, 1))
+                        if b != 0:
+                            z = jnp.where(coord[1] == (0 if b > 0 else 7),
+                                          pltpu.roll(z, (-56 * b) % VOX, 1),
+                                          pltpu.roll(z, (8 * b) % VOX, 1))
+                        if a != 0:
+                            z = pltpu.roll(z, (64 * a) % VOX, 1)
+                        di = 9 * (a + 1) + 3 * (b + 1) + (c + 1)
+                        stack_ref[di * channels:(di + 1) * channels, :] = z
             st = stack_ref[...]
             gf = jnp.dot(kmix_ref[...], st, preferred_element_type=jnp.float32)
             gf_ref[s] = gf.astype(jnp.bfloat16)

time: 55.9 us -> 53 us (0.948)
  Pallas kernels: 13.6 us -> 6.52 us
  starting transfers between devices: 5.4 us -> 11.3 us
  waiting for transfers between devices: 22.2 us -> 20.1 us
    pallas_call x1, Pallas kernels: 13.6 us -> 6.52 us  [local_conv(): pl.pallas_call(make_kernel(blocks, channels, slots), out_shape=(jax.Shape...]
    ppermute x4, starting transfers between devices: 0.21 us -> 6.15 us  [butterfly_sum(): x = x + lax.ppermute(x, axis, [(i, i ^ bit) for i in range(n)])]
    ppermute x4, waiting for transfers between devices: 17.8 us -> 15.7 us  [butterfly_sum(): x = x + lax.ppermute(x, axis, [(i, i ^ bit) for i in range(n)])]
where the time goes in v2:
time: 53 us; the launch traced here: 52.4 us
  waiting for transfers between devices  20.1 us (38%)
  starting transfers between devices  11.3 us (21%)
  blocking collectives  8.33 us (16%)
  Pallas kernels  6.52 us (12%)
  local copies, waits for them, and re-layouts  3.72 us (7%)
  between operations  1.38 us (3%)
  other arithmetic  1.05 us (2%)
    ppermute x4, waiting for transfers between devices, butterfly_sum(): x = x + lax.ppermute(x, axis, [(i, i ^ bit) for i in range(n)])  15.7 us
    all_gather x1, blocking collectives, on_device(): gathered = lax.all_gather(packed, ('split', 'sub'), axis=0, tiled=True)  8.33 us
    pallas_call x1, Pallas kernels, local_conv(): pl.pallas_call(make_kernel(blocks, channels, slots), out_shape=(jax.Shape...  6.52 us
    ppermute x4, starting transfers between devices, butterfly_sum(): x = x + lax.ppermute(x, axis, [(i, i ^ bit) for i in range(n)])  6.15 us
    ppermute x2, starting transfers between devices, from_behind(): return lax.ppermute(block, axis, route)  5.19 us
    ppermute x2, waiting for transfers between devices, from_behind(): return lax.ppermute(block, axis, route)  4.33 us
    unnamed x8, local copies, waits for them, and re-layouts  2.24 us
  transfers between devices with their start and end apart: 6, of which 6 were waited for; matrix products, arithmetic and copies ran while one was open for 2% of the time, Pallas kernels for 0%

profile of v2, /device:TPU:0, one launch (start us, length us, event | category | flops | bytes accessed | tf_op | source)
XLA Modules:
  0.0 52.4 jit_solution(7940756952724913105)
XLA Ops:
  0.6 1.2 %copy.16 = bf16[4,32,512]{1,2,0:T(8,128)(2,1)S(1)} copy(bf16[4,32,512]{2,1,0:T(8,128)(2,1)} %g_ref.1) | data formatting | bytes 262144 | tf_op args[0]
  1.8 0.2 fusion
  2.0 5.1 %collective-permute-start.1 = (bf16[4,32,64]{1,2,0:T(8,128)(2,1)S(1)}, bf16[4,32,64]{1,2,0:T(8,128)(2,1)S(1)}, u32[]{:S(2)}, u32[]{:S(2)}) collective-permute-start(bf16[4,32,64]{1,2,0:T(8,128)(2,1)S(1)} %bitcast.12), channel_id=1, source_target_pairs={{4,0},{8,4},{12,8},{0,12},{5,1},{9,5},{13,9},{1,13},{6,2},{10,6},{... | collective-permute-start | bytes 49160 | tf_op jit(solution)/shard_map/ppermute | solution.py:18
  7.2 0.1 collective-permute-start
  7.9 0.1 copy.19
  8.0 0.9 %reshape.14.kmix_ref = bf16[32,864]{1,0:T(8,128)(2,1)} reshape(bf16[32,27,32]{2,1,0:T(8,128)(2,1)S(1)} %copy.19) | data formatting | bytes 110592 | tf_op jit(solution)/shard_map/reshape | solution.py:161
  8.9 0.3 collective-permute-done.1
  9.2 0.1 copy.18
  9.3 4.0 %collective-permute-done = bf16[4,32,64]{1,2,0:T(8,128)(2,1)S(1)} collective-permute-done((bf16[4,32,64]{1,2,0:T(8,128)(2,1)S(1)}, bf16[4,32,64]{1,2,0:T(8,128)(2,1)S(1)}, u32[]{:S(2)}, u32[]{:S(2)}) %collective-permute-start) | collective-permute-done | bytes 16416 | tf_op jit(solution)/shard_map/ppermute | solution.py:18
  13.3 0.1 copy.17
  13.4 0.1 pad_maximum_fusion
  13.5 8.3 %all_gather.3.gath_ref = bf16[16,32,640]{2,1,0:T(8,128)(2,1)} all-gather(bf16[4,32,640]{2,1,0:T(8,128)(2,1)S(1)} %pad_maximum_fusion), channel_id=1, replica_groups=mesh['groups'=2,'brick'=4,'split'=2,'sub'=2] {'split','sub'}, dimensions={0}, use_global_device_ids=true | all-gather | bytes 819200 | tf_op jit(solution)/shard_map/all_gather | solution.py:160
  21.8 6.5 %shard_map.68 = (bf16[4,32,512]{2,1,0:T(8,128)(2,1)}, f32[32,864]{1,0:T(8,128)}) custom-call(s32[4,26]{1,0:T(4,128)} %nbr_ref.1, s32[1]{0:T(128)S(6)} %copy.27.cnt_ref, bf16[4,32,512]{2,1,0:T(8,128)(2,1)} %g_ref.1, bf16[4,32,512]{2,1,0:T(8,128)(2,1)} %f_ref.1, bf16[16,32,640]{2,1,0:T(8,128)(2,1)} %all_gather.3.gath_ref, bf16[32,864]{1,0:T(8,128)(2,1)} %reshape.14.kmix_ref), custom_call_target="tpu_custom_call" | custom-call | tf_op jit(solution)/shard_map/pallas_call | solution.py:136
  28.3 0.3 collective-permute-start.2
  28.7 1.2 %collective-permute-done.2 = f32[32,864]{1,0:T(8,128)S(1)} collective-permute-done((f32[32,864]{1,0:T(8,128)}, f32[32,864]{1,0:T(8,128)S(1)}, u32[]{:S(2)}, u32[]{:S(2)}) %collective-permute-start.2) | collective-permute-done | bytes 110624 | tf_op jit(solution)/shard_map/ppermute | solution.py:29
  29.9 0.9 %add.12 = f32[32,864]{1,0:T(8,128)S(1)} add(f32[32,864]{1,0:T(8,128)} %get-tuple-element.5, f32[32,864]{1,0:T(8,128)S(1)} %collective-permute-done.2) | non-fusion elementwise | flops 27648 | bytes 331776 | tf_op jit(solution)/shard_map/add | solution.py:29
  30.8 5.1 %collective-permute-start.3 = (f32[32,864]{1,0:T(8,128)S(1)}, f32[32,864]{1,0:T(8,128)S(1)}, u32[]{:S(2)}, u32[]{:S(2)}) collective-permute-start(f32[32,864]{1,0:T(8,128)S(1)} %add.12), channel_id=1, source_target_pairs={{0,2},{2,0},{1,3},{3,1},{4,6},{6,4},{5,7},{7,5},{8,10},{10,8},{9,1... | collective-permute-start | bytes 331784 | tf_op jit(solution)/shard_map/ppermute | solution.py:29
  35.9 3.5 %collective-permute-done.3 = f32[32,864]{1,0:T(8,128)S(1)} collective-permute-done((f32[32,864]{1,0:T(8,128)S(1)}, f32[32,864]{1,0:T(8,128)S(1)}, u32[]{:S(2)}, u32[]{:S(2)}) %collective-permute-start.3) | collective-permute-done | bytes 110624 | tf_op jit(solution)/shard_map/ppermute | solution.py:29
  39.4 0.6 %collective-permute-start.4 = (f32[32,864]{1,0:T(8,128)S(1)}, f32[32,864]{1,0:T(8,128)S(1)}, u32[]{:S(2)}, u32[]{:S(2)}) collective-permute-start(f32[32,864]{1,0:T(8,128)S(1)} %add.13), channel_id=1, source_target_pairs={{0,4},{4,0},{8,12},{12,8},{1,5},{5,1},{9,13},{13,9},{2,6},{6,2},{1... | collective-permute-start | bytes 331784 | tf_op jit(solution)/shard_map/ppermute | solution.py:29
  40.0 4.3 %collective-permute-done.4 = f32[32,864]{1,0:T(8,128)S(1)} collective-permute-done((f32[32,864]{1,0:T(8,128)S(1)}, f32[32,864]{1,0:T(8,128)S(1)}, u32[]{:S(2)}, u32[]{:S(2)}) %collective-permute-start.4) | collective-permute-done | bytes 110624 | tf_op jit(solution)/shard_map/ppermute | solution.py:29
  44.3 0.1 collective-permute-start.5
  44.4 6.8 %collective-permute-done.5 = f32[32,864]{1,0:T(8,128)S(1)} collective-permute-done((f32[32,864]{1,0:T(8,128)S(1)}, f32[32,864]{1,0:T(8,128)S(1)}, u32[]{:S(2)}, u32[]{:S(2)}) %collective-permute-start.5) | collective-permute-done | bytes 110624 | tf_op jit(solution)/shard_map/ppermute | solution.py:29
  51.2 0.2 mul.14
  51.4 1.0 %copy.20 = f32[27,32,32]{2,1,0:T(8,128)} copy(f32[27,32,32]{2,0,1:T(8,128)S(1)} %bitcast.9) | data formatting | bytes 221184
  (9 shorter events, 0.1 us)
Async XLA Ops:
  2.0 5.9 %copy-start.1 = (bf16[27,32,32]{2,1,0:T(8,128)(2,1)S(1)}, bf16[27,32,32]{2,1,0:T(8,128)(2,1)}, u32[]{:S(2)}) copy-start(bf16[27,32,32]{2,1,0:T(8,128)(2,1)} %param.7) | copy-start | bytes 165892
  2.0 7.2 %collective-permute-start.1 = (bf16[4,32,64]{1,2,0:T(8,128)(2,1)S(1)}, bf16[4,32,64]{1,2,0:T(8,128)(2,1)S(1)}, u32[]{:S(2)}, u32[]{:S(2)}) collective-permute-start(bf16[4,32,64]{1,2,0:T(8,128)(2,1)S(1)} %bitcast.12), channel_id=1, source_target_pairs={{4,0},{8,4},{12,8},{0,12},{5,1},{9,5},{13,9},{1,13},{6,2},{10,6},{... | collective-permute-start | bytes 49160 | tf_op jit(solution)/shard_map/ppermute | solution.py:18
  7.2 6.1 %collective-permute-start = (bf16[4,32,64]{1,2,0:T(8,128)(2,1)S(1)}, bf16[4,32,64]{1,2,0:T(8,128)(2,1)S(1)}, u32[]{:S(2)}, u32[]{:S(2)}) collective-permute-start(bf16[4,32,64]{1,2,0:T(8,128)(2,1)S(1)} %bitcast.13), channel_id=1, source_target_pairs={{12,0},{0,4},{4,8},{8,12},{13,1},{1,5},{5,9},{9,13},{14,2},{2,6},{... | collective-permute-start | bytes 49160 | tf_op jit(solution)/shard_map/ppermute | solution.py:18
  8.9 4.5 %copy-start = (bf16[4,32,512]{2,1,0:T(8,128)(2,1)S(1)}, bf16[4,32,512]{2,1,0:T(8,128)(2,1)}, u32[]{:S(2)}) copy-start(bf16[4,32,512]{2,1,0:T(8,128)(2,1)} %g_ref.1) | copy-start | bytes 393220
  28.3 1.5 %collective-permute-start.2 = (f32[32,864]{1,0:T(8,128)}, f32[32,864]{1,0:T(8,128)S(1)}, u32[]{:S(2)}, u32[]{:S(2)}) collective-permute-start(f32[32,864]{1,0:T(8,128)} %get-tuple-element.5), channel_id=1, source_target_pairs={{0,1},{1,0},{2,3},{3,2},{4,5},{5,4},{6,7},{7,6},{8,9},{9,8},{10,11... | collective-permute-start | bytes 331784 | tf_op jit(solution)/shard_map/ppermute | solution.py:29
  30.8 8.6 %collective-permute-start.3 = (f32[32,864]{1,0:T(8,128)S(1)}, f32[32,864]{1,0:T(8,128)S(1)}, u32[]{:S(2)}, u32[]{:S(2)}) collective-permute-start(f32[32,864]{1,0:T(8,128)S(1)} %add.12), channel_id=1, source_target_pairs={{0,2},{2,0},{1,3},{3,1},{4,6},{6,4},{5,7},{7,5},{8,10},{10,8},{9,1... | collective-permute-start | bytes 331784 | tf_op jit(solution)/shard_map/ppermute | solution.py:29
  39.4 4.9 %collective-permute-start.4 = (f32[32,864]{1,0:T(8,128)S(1)}, f32[32,864]{1,0:T(8,128)S(1)}, u32[]{:S(2)}, u32[]{:S(2)}) collective-permute-start(f32[32,864]{1,0:T(8,128)S(1)} %add.13), channel_id=1, source_target_pairs={{0,4},{4,0},{8,12},{12,8},{1,5},{5,1},{9,13},{13,9},{2,6},{6,2},{1... | collective-permute-start | bytes 331784 | tf_op jit(solution)/shard_map/ppermute | solution.py:29
  44.3 6.9 %collective-permute-start.5 = (f32[32,864]{1,0:T(8,128)S(1)}, f32[32,864]{1,0:T(8,128)S(1)}, u32[]{:S(2)}, u32[]{:S(2)}) collective-permute-start(f32[32,864]{1,0:T(8,128)S(1)} %add.14), channel_id=1, source_target_pairs={{0,8},{4,12},{8,0},{12,4},{1,9},{5,13},{9,1},{13,5},{2,10},{6,14},... | collective-permute-start | bytes 331784 | tf_op jit(solution)/shard_map/ppermute | solution.py:29

commit v3 on v2

--- a/solution.py
+++ b/solution.py
@@ -42,9 +42,12 @@
     return sorted(found, key=lambda e: sum(1 for t in e if t != 0))
 
 
-def make_kernel(blocks, channels, slots):
-    def kernel(nbr_ref, cnt_ref, g_ref, f_ref, gath_ref, kmix_ref, gf_ref, wg_ref,
-               same_ref, lay_ref, stack_ref):
+def make_kernel(blocks, channels, peers):
+    slots = blocks * peers
+
+    def kernel(nbr_ref, cnt_ref, me_ref, g_ref, f_ref, kmix_ref, *rest):
+        recv_refs = rest[:peers]
+        gf_ref, wg_ref, same_ref, lay_ref, stack_ref = rest[peers:]
         lane = lax.broadcasted_iota(jnp.int32, (channels, VOX), 1)
         coord = (lane // 64, (lane // 8) % 8, lane % 8)
 
@@ -58,16 +61,18 @@
         lay_ref[0, slots] = jnp.zeros((channels, VOX), jnp.bfloat16)
         lay_ref[1, slots] = jnp.zeros((channels, VOX), jnp.bfloat16)
 
-        def fill(q, carry):
-            row = gath_ref[q]
-            same_ref[q] = row[:, 0:VOX]
-            for t in range(2):
-                layer = row[:, VOX + 64 * t:VOX + 64 * (t + 1)]
-                wide = jnp.dot(layer, spread, preferred_element_type=jnp.float32)
-                lay_ref[t, q] = wide.astype(jnp.bfloat16)
-            return carry
+        for k in range(peers):
+            def fill(s, carry, k=k):
+                row = recv_refs[k][s]
+                q = (jnp.bitwise_xor(me_ref[0], k)) * blocks + s
+                same_ref[q] = row[:, 0:VOX]
+                for t in range(2):
+                    layer = row[:, VOX + 64 * t:VOX + 64 * (t + 1)]
+                    wide = jnp.dot(layer, spread, preferred_element_type=jnp.float32)
+                    lay_ref[t, q] = wide.astype(jnp.bfloat16)
+                return carry
 
-        lax.fori_loop(0, slots, fill, 0)
+            lax.fori_loop(0, blocks, fill, 0)
 
         gf_ref[...] = jnp.zeros_like(gf_ref)
         wg_ref[...] = jnp.zeros_like(wg_ref)
@@ -128,25 +133,26 @@
     return kernel
 
 
-def local_conv(neighbours, block_count, grad_out, features, gathered, kmix):
+def local_conv(neighbours, block_count, me, grad_out, features, kmix, received):
     blocks, channels = grad_out.shape[0], grad_out.shape[1]
-    slots = gathered.shape[0]
+    peers = len(received)
+    slots = blocks * peers
     smem = pl.BlockSpec(memory_space=pltpu.SMEM)
     vmem = pl.BlockSpec(memory_space=pltpu.VMEM)
     return pl.pallas_call(
-        make_kernel(blocks, channels, slots),
+        make_kernel(blocks, channels, peers),
         out_shape=(
             jax.ShapeDtypeStruct((blocks, channels, VOX), jnp.bfloat16),
             jax.ShapeDtypeStruct((channels, 27 * channels), jnp.float32),
         ),
-        in_specs=[smem, smem, vmem, vmem, vmem, vmem],
+        in_specs=[smem, smem, smem, vmem, vmem, vmem] + [vmem] * peers,
         out_specs=(vmem, vmem),
         scratch_shapes=[
             pltpu.VMEM((slots + 1, channels, VOX), jnp.bfloat16),
             pltpu.VMEM((2, slots + 1, channels, VOX), jnp.bfloat16),
             pltpu.VMEM((27 * channels, VOX), jnp.bfloat16),
         ],
-    )(neighbours, block_count, grad_out, features, gathered, kmix)
+    )(neighbours, block_count, me, grad_out, features, kmix, *received)
 
 
 def on_device(grad_out, features, kernel, block_count, neighbours):
@@ -157,9 +163,17 @@
     from_below = from_behind(highest, "brick", 1)
     from_above = from_behind(lowest, "brick", -1)
     packed = jnp.concatenate([grad_out, from_below, from_above], axis=2)
-    gathered = lax.all_gather(packed, ("split", "sub"), axis=0, tiled=True)
+    peers = lax.axis_size("split") * lax.axis_size("sub")
+    assert peers & (peers - 1) == 0
+    received = [packed] + [
+        lax.ppermute(packed, ("split", "sub"), [(i, i ^ k) for i in range(peers)])
+        for k in range(1, peers)
+    ]
+    me = (lax.axis_index("split") * lax.axis_size("sub") + lax.axis_index("sub")).astype(jnp.int32)
     kmix = jnp.transpose(kernel, (1, 0, 2)).reshape(channels, 27 * channels)
-    grad_features, wg = local_conv(neighbours, block_count, grad_out, features, gathered, kmix)
+    grad_features, wg = local_conv(
+        neighbours, block_count, me.reshape(1), grad_out, features, kmix, received
+    )
     wg = butterfly_sum(wg, ("sub", "split", "brick"))
     scaling = 1.0 / math.sqrt(
         lax.axis_size("brick") * lax.axis_size("split") * lax.axis_size("sub") * blocks * VOX

time: 53 us -> 52.4 us (0.989); the launches traced: 52.4 us -> 52.4 us
  blocking collectives: 8.33 us -> 0 us
  Pallas kernels: 6.52 us -> 11.1 us
  waiting for transfers between devices: 20.1 us -> 23.5 us
  local copies, waits for them, and re-layouts: 3.72 us -> 4.46 us
    all_gather x1 -> x0, blocking collectives: 8.33 us -> none  [on_device(): gathered = lax.all_gather(packed, ('split', 'sub'), axis=0, tiled=True)]
    ppermute x0 -> x3, waiting for transfers between devices: none -> 6.51 us  [on_device(): lax.ppermute(packed, ('split', 'sub'), [(i, i ^ k) for i in range(peers)])]
    pallas_call x1, Pallas kernels: 6.52 us -> 11.1 us  [local_conv(): pl.pallas_call(make_kernel(blocks, channels, peers), out_shape=(jax.Shape...]
    ppermute x4, starting transfers between devices: 6.15 us -> 3.81 us  [butterfly_sum(): x = x + lax.ppermute(x, axis, [(i, i ^ bit) for i in range(n)])]
    ppermute x2, waiting for transfers between devices: 4.33 us -> 2.14 us  [from_behind(): return lax.ppermute(block, axis, route)]
    ppermute x0 -> x3, starting transfers between devices: none -> 1.92 us  [on_device(): lax.ppermute(packed, ('split', 'sub'), [(i, i ^ k) for i in range(peers)])]
    ppermute x4, waiting for transfers between devices: 15.7 us -> 14.8 us  [butterfly_sum(): x = x + lax.ppermute(x, axis, [(i, i ^ bit) for i in range(n)])]
    unnamed x8 -> x16, local copies, waits for them, and re-layouts: 2.24 us -> 2.97 us
  transfers between devices with their start and end apart: 6 -> 9, of which waited for: 6 -> 8; matrix products, arithmetic and copies ran while one was open for 2% -> 2% of each run, Pallas kernels for 0% -> 0%
where the time goes in v3:
time: 52.4 us
  waiting for transfers between devices  23.5 us (45%)
  Pallas kernels  11.1 us (21%)
  starting transfers between devices  10.9 us (21%)
  local copies, waits for them, and re-layouts  4.46 us (9%)
  between operations  1.41 us (3%)
  other arithmetic  1.05 us (2%)
    ppermute x4, waiting for transfers between devices, butterfly_sum(): x = x + lax.ppermute(x, axis, [(i, i ^ bit) for i in range(n)])  14.8 us
    pallas_call x1, Pallas kernels, local_conv(): pl.pallas_call(make_kernel(blocks, channels, peers), out_shape=(jax.Shape...  11.1 us
    ppermute x3, waiting for transfers between devices, on_device(): lax.ppermute(packed, ('split', 'sub'), [(i, i ^ k) for i in range(peers)])  6.51 us
    ppermute x2, starting transfers between devices, from_behind(): return lax.ppermute(block, axis, route)  5.21 us
    ppermute x4, starting transfers between devices, butterfly_sum(): x = x + lax.ppermute(x, axis, [(i, i ^ bit) for i in range(n)])  3.81 us
    unnamed x16, local copies, waits for them, and re-layouts  2.97 us
    ppermute x2, waiting for transfers between devices, from_behind(): return lax.ppermute(block, axis, route)  2.14 us
    ppermute x3, starting transfers between devices, on_device(): lax.ppermute(packed, ('split', 'sub'), [(i, i ^ k) for i in range(peers)])  1.92 us
  transfers between devices with their start and end apart: 9, of which 8 were waited for; matrix products, arithmetic and copies ran while one was open for 2% of the time, Pallas kernels for 0%

profile of v3, /device:TPU:0, one launch (start us, length us, event | category | flops | bytes accessed | tf_op | source)
XLA Modules:
  0.0 52.4 jit_solution(13733899530785855971)
XLA Ops:
  0.6 1.2 %copy.12 = bf16[4,32,512]{1,2,0:T(8,128)(2,1)S(1)} copy(bf16[4,32,512]{2,1,0:T(8,128)(2,1)} %g_ref.1) | data formatting | bytes 262144 | tf_op args[0]
  1.8 0.2 fusion
  2.1 3.1 %collective-permute-start = (bf16[4,32,64]{2,1,0:T(8,128)(2,1)S(1)}, bf16[4,32,64]{2,1,0:T(8,128)(2,1)S(1)}, u32[]{:S(2)}, u32[]{:S(2)}) collective-permute-start(bf16[4,32,64]{2,1,0:T(8,128)(2,1)S(1)} %copy.13), channel_id=1, source_target_pairs={{12,0},{0,4},{4,8},{8,12},{13,1},{1,5},{5,9},{9,13},{14,2},{2,6},{... | collective-permute-start | bytes 49160 | tf_op jit(solution)/shard_map/ppermute | solution.py:18
  5.2 0.1 copy.14
  5.3 2.1 %collective-permute-start.1 = (bf16[4,32,64]{2,1,0:T(8,128)(2,1)S(1)}, bf16[4,32,64]{2,1,0:T(8,128)(2,1)S(1)}, u32[]{:S(2)}, u32[]{:S(2)}) collective-permute-start(bf16[4,32,64]{2,1,0:T(8,128)(2,1)S(1)} %copy.14), channel_id=1, source_target_pairs={{4,0},{8,4},{12,8},{0,12},{5,1},{9,5},{13,9},{1,13},{6,2},{10,6},{... | collective-permute-start | bytes 49160 | tf_op jit(solution)/shard_map/ppermute | solution.py:18
  7.4 1.8 %collective-permute-done = bf16[4,32,64]{2,1,0:T(8,128)(2,1)S(1)} collective-permute-done((bf16[4,32,64]{2,1,0:T(8,128)(2,1)S(1)}, bf16[4,32,64]{2,1,0:T(8,128)(2,1)S(1)}, u32[]{:S(2)}, u32[]{:S(2)}) %collective-permute-start) | collective-permute-done | bytes 16416 | tf_op jit(solution)/shard_map/ppermute | solution.py:18
  9.3 0.3 collective-permute-done.1
  9.8 1.6 %collective-permute-start.3 = (bf16[4,32,640]{2,1,0:T(8,128)(2,1)S(1)}, bf16[4,32,640]{2,1,0:T(8,128)(2,1)S(1)}, u32[]{:S(2)}, u32[]{:S(2)}) collective-permute-start(bf16[4,32,640]{2,1,0:T(8,128)(2,1)S(1)} %pad_maximum_fusion.rest_0_), channel_id=1, source_target_pairs={{0,2},{1,3},{2,0},{3,1},{4,6},{5,7},{6,4},{7,5},{8,10},{9,11},{10,... | collective-permute-start | bytes 491528 | tf_op jit(solution)/shard_map/ppermute | solution.py:169
  11.4 0.2 collective-permute-start.2
  12.3 0.1 copy.11
  12.4 0.9 %reshape.17.kmix_ref = bf16[32,864]{1,0:T(8,128)(2,1)} reshape(bf16[32,27,32]{2,1,0:T(8,128)(2,1)S(1)} %copy.11) | data formatting | bytes 110592 | tf_op jit(solution)/shard_map/reshape | solution.py:173
  13.3 2.9 %collective-permute-done.4.rest_3_ = bf16[4,32,640]{2,1,0:T(8,128)(2,1)S(1)} collective-permute-done((bf16[4,32,640]{2,1,0:T(8,128)(2,1)S(1)}, bf16[4,32,640]{2,1,0:T(8,128)(2,1)S(1)}, u32[]{:S(2)}, u32[]{:S(2)}) %collective-permute-start.4) | collective-permute-done | bytes 163872 | tf_op jit(solution)/shard_map/ppermute | solution.py:169
  16.1 3.6 %collective-permute-done.3.rest_2_ = bf16[4,32,640]{2,1,0:T(8,128)(2,1)S(1)} collective-permute-done((bf16[4,32,640]{2,1,0:T(8,128)(2,1)S(1)}, bf16[4,32,640]{2,1,0:T(8,128)(2,1)S(1)}, u32[]{:S(2)}, u32[]{:S(2)}) %collective-permute-start.3) | collective-permute-done | bytes 163872 | tf_op jit(solution)/shard_map/ppermute | solution.py:169
  19.8 0.7 %copy-done.4 = bf16[4,32,640]{2,1,0:T(8,128)(2,1)} copy-done((bf16[4,32,640]{2,1,0:T(8,128)(2,1)}, bf16[4,32,640]{2,1,0:T(8,128)(2,1)S(1)}, u32[]{:S(2)}) %copy-start.4) | copy-done | bytes 163864
  20.5 11.1 %shard_map.68 = (bf16[4,32,512]{2,1,0:T(8,128)(2,1)}, f32[32,864]{1,0:T(8,128)}) custom-call(s32[4,26]{1,0:T(4,128)} %nbr_ref.1, s32[1]{0:T(128)S(6)} %copy.22.cnt_ref, s32[1]{0:T(128)} %bitcast.me_ref, bf16[4,32,512]{2,1,0:T(8,128)(2,1)} %g_ref.1, bf16[4,32,512]{2,1,0:T(8,128)(2,1)} %f_ref.1, bf16[32,864]{1,0:T(8,128)(2,1)} %reshape.17.kmix_ref, ...), custom_call_target="tpu_custom_call" | custom-call | tf_op jit(solution)/shard_map/pallas_call | solution.py:142
  31.6 1.5 %collective-permute-done.5 = f32[32,864]{1,0:T(8,128)S(1)} collective-permute-done((f32[32,864]{1,0:T(8,128)}, f32[32,864]{1,0:T(8,128)S(1)}, u32[]{:S(2)}, u32[]{:S(2)}) %collective-permute-start.5) | collective-permute-done | bytes 110624 | tf_op jit(solution)/shard_map/ppermute | solution.py:29
  33.1 0.9 %add.16 = f32[32,864]{1,0:T(8,128)S(1)} add(f32[32,864]{1,0:T(8,128)} %get-tuple-element.5, f32[32,864]{1,0:T(8,128)S(1)} %collective-permute-done.5) | non-fusion elementwise | flops 27648 | bytes 331776 | tf_op jit(solution)/shard_map/add | solution.py:29
  34.1 5.2 %collective-permute-done.6 = f32[32,864]{1,0:T(8,128)S(1)} collective-permute-done((f32[32,864]{1,0:T(8,128)S(1)}, f32[32,864]{1,0:T(8,128)S(1)}, u32[]{:S(2)}, u32[]{:S(2)}) %collective-permute-start.6) | collective-permute-done | bytes 110624 | tf_op jit(solution)/shard_map/ppermute | solution.py:29
  39.3 1.4 %collective-permute-start.7 = (f32[32,864]{1,0:T(8,128)S(1)}, f32[32,864]{1,0:T(8,128)S(1)}, u32[]{:S(2)}, u32[]{:S(2)}) collective-permute-start(f32[32,864]{1,0:T(8,128)S(1)} %add.17), channel_id=1, source_target_pairs={{0,4},{4,0},{8,12},{12,8},{1,5},{5,1},{9,13},{13,9},{2,6},{6,2},{1... | collective-permute-start | bytes 331784 | tf_op jit(solution)/shard_map/ppermute | solution.py:29
  40.7 3.5 %collective-permute-done.7 = f32[32,864]{1,0:T(8,128)S(1)} collective-permute-done((f32[32,864]{1,0:T(8,128)S(1)}, f32[32,864]{1,0:T(8,128)S(1)}, u32[]{:S(2)}, u32[]{:S(2)}) %collective-permute-start.7) | collective-permute-done | bytes 110624 | tf_op jit(solution)/shard_map/ppermute | solution.py:29
  44.2 2.4 %collective-permute-start.8 = (f32[32,864]{1,0:T(8,128)S(1)}, f32[32,864]{1,0:T(8,128)S(1)}, u32[]{:S(2)}, u32[]{:S(2)}) collective-permute-start(f32[32,864]{1,0:T(8,128)S(1)} %add.18), channel_id=1, source_target_pairs={{0,8},{4,12},{8,0},{12,4},{1,9},{5,13},{9,1},{13,5},{2,10},{6,14},... | collective-permute-start | bytes 331784 | tf_op jit(solution)/shard_map/ppermute | solution.py:29
  46.6 4.6 %collective-permute-done.8 = f32[32,864]{1,0:T(8,128)S(1)} collective-permute-done((f32[32,864]{1,0:T(8,128)S(1)}, f32[32,864]{1,0:T(8,128)S(1)}, u32[]{:S(2)}, u32[]{:S(2)}) %collective-permute-start.8) | collective-permute-done | bytes 110624 | tf_op jit(solution)/shard_map/ppermute | solution.py:29
  51.2 0.2 mul.18
  51.4 1.0 %copy.15 = f32[27,32,32]{2,1,0:T(8,128)} copy(f32[27,32,32]{2,0,1:T(8,128)S(1)} %bitcast.10) | data formatting | bytes 221184
  (22 shorter events, 0.5 us)
Async XLA Ops:
  2.1 7.2 %collective-permute-start = (bf16[4,32,64]{2,1,0:T(8,128)(2,1)S(1)}, bf16[4,32,64]{2,1,0:T(8,128)(2,1)S(1)}, u32[]{:S(2)}, u32[]{:S(2)}) collective-permute-start(bf16[4,32,64]{2,1,0:T(8,128)(2,1)S(1)} %copy.13), channel_id=1, source_target_pairs={{12,0},{0,4},{4,8},{8,12},{13,1},{1,5},{5,9},{9,13},{14,2},{2,6},{... | collective-permute-start | bytes 49160 | tf_op jit(solution)/shard_map/ppermute | solution.py:18
  5.2 4.4 %copy-start = (bf16[4,32,512]{2,1,0:T(8,128)(2,1)S(1)}, bf16[4,32,512]{2,1,0:T(8,128)(2,1)}, u32[]{:S(2)}) copy-start(bf16[4,32,512]{2,1,0:T(8,128)(2,1)} %g_ref.1) | copy-start | bytes 393220
  5.2 7.0 %copy-start.2 = (bf16[27,32,32]{2,1,0:T(8,128)(2,1)S(1)}, bf16[27,32,32]{2,1,0:T(8,128)(2,1)}, u32[]{:S(2)}) copy-start(bf16[27,32,32]{2,1,0:T(8,128)(2,1)} %param.7) | copy-start | bytes 165892
  5.3 4.2 %collective-permute-start.1 = (bf16[4,32,64]{2,1,0:T(8,128)(2,1)S(1)}, bf16[4,32,64]{2,1,0:T(8,128)(2,1)S(1)}, u32[]{:S(2)}, u32[]{:S(2)}) collective-permute-start(bf16[4,32,64]{2,1,0:T(8,128)(2,1)S(1)} %copy.14), channel_id=1, source_target_pairs={{4,0},{8,4},{12,8},{0,12},{5,1},{9,5},{13,9},{1,13},{6,2},{10,6},{... | collective-permute-start | bytes 49160 | tf_op jit(solution)/shard_map/ppermute | solution.py:18
  9.7 2.7 %copy-start.1 = (bf16[4,32,640]{2,1,0:T(8,128)(2,1)}, bf16[4,32,640]{2,1,0:T(8,128)(2,1)S(1)}, u32[]{:S(2)}) copy-start(bf16[4,32,640]{2,1,0:T(8,128)(2,1)S(1)} %pad_maximum_fusion.rest_0_) | copy-start | bytes 491524
  9.7 6.4 %collective-permute-start.4 = (bf16[4,32,640]{2,1,0:T(8,128)(2,1)S(1)}, bf16[4,32,640]{2,1,0:T(8,128)(2,1)S(1)}, u32[]{:S(2)}, u32[]{:S(2)}) collective-permute-start(bf16[4,32,640]{2,1,0:T(8,128)(2,1)S(1)} %pad_maximum_fusion.rest_0_), channel_id=1, source_target_pairs={{0,3},{1,2},{2,1},{3,0},{4,7},{5,6},{6,5},{7,4},{8,11},{9,10},{10,... | collective-permute-start | bytes 491528 | tf_op jit(solution)/shard_map/ppermute | solution.py:169
  9.8 10.0 %collective-permute-start.3 = (bf16[4,32,640]{2,1,0:T(8,128)(2,1)S(1)}, bf16[4,32,640]{2,1,0:T(8,128)(2,1)S(1)}, u32[]{:S(2)}, u32[]{:S(2)}) collective-permute-start(bf16[4,32,640]{2,1,0:T(8,128)(2,1)S(1)} %pad_maximum_fusion.rest_0_), channel_id=1, source_target_pairs={{0,2},{1,3},{2,0},{3,1},{4,6},{5,7},{6,4},{7,5},{8,10},{9,11},{10,... | collective-permute-start | bytes 491528 | tf_op jit(solution)/shard_map/ppermute | solution.py:169
  11.4 8.4 %collective-permute-start.2 = (bf16[4,32,640]{2,1,0:T(8,128)(2,1)S(1)}, bf16[4,32,640]{2,1,0:T(8,128)(2,1)S(1)}, u32[]{:S(2)}, u32[]{:S(2)}) collective-permute-start(bf16[4,32,640]{2,1,0:T(8,128)(2,1)S(1)} %pad_maximum_fusion.rest_0_), channel_id=1, source_target_pairs={{0,1},{1,0},{2,3},{3,2},{4,5},{5,4},{6,7},{7,6},{8,9},{9,8},{10,11... | collective-permute-start | bytes 491528 | tf_op jit(solution)/shard_map/ppermute | solution.py:169
  16.1 3.6 %copy-start.3 = (bf16[4,32,640]{2,1,0:T(8,128)(2,1)}, bf16[4,32,640]{2,1,0:T(8,128)(2,1)S(1)}, u32[]{:S(2)}) copy-start(bf16[4,32,640]{2,1,0:T(8,128)(2,1)S(1)} %collective-permute-done.4.rest_3_) | copy-start | bytes 491524
  19.8 0.7 %copy-start.4 = (bf16[4,32,640]{2,1,0:T(8,128)(2,1)}, bf16[4,32,640]{2,1,0:T(8,128)(2,1)S(1)}, u32[]{:S(2)}) copy-start(bf16[4,32,640]{2,1,0:T(8,128)(2,1)S(1)} %collective-permute-done.3.rest_2_) | copy-start | bytes 491524
  19.8 0.7 %copy-start.5 = (bf16[4,32,640]{2,1,0:T(8,128)(2,1)}, bf16[4,32,640]{2,1,0:T(8,128)(2,1)S(1)}, u32[]{:S(2)}) copy-start(bf16[4,32,640]{2,1,0:T(8,128)(2,1)S(1)} %collective-permute-done.2.rest_1_) | copy-start | bytes 491524
  31.6 1.5 %collective-permute-start.5 = (f32[32,864]{1,0:T(8,128)}, f32[32,864]{1,0:T(8,128)S(1)}, u32[]{:S(2)}, u32[]{:S(2)}) collective-permute-start(f32[32,864]{1,0:T(8,128)} %get-tuple-element.5), channel_id=1, source_target_pairs={{0,1},{1,0},{2,3},{3,2},{4,5},{5,4},{6,7},{7,6},{8,9},{9,8},{10,11... | collective-permute-start | bytes 331784 | tf_op jit(solution)/shard_map/ppermute | solution.py:29
  34.0 5.3 %collective-permute-start.6 = (f32[32,864]{1,0:T(8,128)S(1)}, f32[32,864]{1,0:T(8,128)S(1)}, u32[]{:S(2)}, u32[]{:S(2)}) collective-permute-start(f32[32,864]{1,0:T(8,128)S(1)} %add.16), channel_id=1, source_target_pairs={{0,2},{2,0},{1,3},{3,1},{4,6},{6,4},{5,7},{7,5},{8,10},{10,8},{9,1... | collective-permute-start | bytes 331784 | tf_op jit(solution)/shard_map/ppermute | solution.py:29
  39.3 4.9 %collective-permute-start.7 = (f32[32,864]{1,0:T(8,128)S(1)}, f32[32,864]{1,0:T(8,128)S(1)}, u32[]{:S(2)}, u32[]{:S(2)}) collective-permute-start(f32[32,864]{1,0:T(8,128)S(1)} %add.17), channel_id=1, source_target_pairs={{0,4},{4,0},{8,12},{12,8},{1,5},{5,1},{9,13},{13,9},{2,6},{6,2},{1... | collective-permute-start | bytes 331784 | tf_op jit(solution)/shard_map/ppermute | solution.py:29
  44.2 7.0 %collective-permute-start.8 = (f32[32,864]{1,0:T(8,128)S(1)}, f32[32,864]{1,0:T(8,128)S(1)}, u32[]{:S(2)}, u32[]{:S(2)}) collective-permute-start(f32[32,864]{1,0:T(8,128)S(1)} %add.18), channel_id=1, source_target_pairs={{0,8},{4,12},{8,0},{12,4},{1,9},{5,13},{9,1},{13,5},{2,10},{6,14},... | collective-permute-start | bytes 331784 | tf_op jit(solution)/shard_map/ppermute | solution.py:29

commit v4 on v3

--- a/solution.py
+++ b/solution.py
@@ -42,12 +42,57 @@
     return sorted(found, key=lambda e: sum(1 for t in e if t != 0))
 
 
-def make_kernel(blocks, channels, peers):
+def face_selector(rows, cols, transpose):
+    v, j = (cols, rows) if transpose else (rows, cols)
+    face, r = j // 64, j % 64
+    hi, lo = r // 8, r % 8
+    target = jnp.where(face == 0, r, 448 + r)
+    target = jnp.where(face == 2, hi * 64 + lo, target)
+    target = jnp.where(face == 3, hi * 64 + 56 + lo, target)
+    hit = v == target
+    if transpose:
+        inner = (v // 64 != 0) & (v // 64 != 7)
+        hit = hit & ((face < 2) | inner)
+    return hit.astype(jnp.bfloat16)
+
+
+def pack_kernel(g_ref, faces_ref, low_ref, high_ref):
+    rows = lax.broadcasted_iota(jnp.int32, (VOX, 256), 0)
+    cols = lax.broadcasted_iota(jnp.int32, (VOX, 256), 1)
+    pick = face_selector(rows, cols, False)
+    lrows = lax.broadcasted_iota(jnp.int32, (VOX, 128), 0)
+    lcols = lax.broadcasted_iota(jnp.int32, (VOX, 128), 1)
+    layer_pick = (lrows == (lcols % 64) * 8 + 7 * (lcols // 64)).astype(jnp.bfloat16)
+    for s in range(g_ref.shape[0]):
+        g = g_ref[s]
+        faces_ref[s] = jnp.dot(g, pick, preferred_element_type=jnp.float32).astype(jnp.bfloat16)
+        layers = jnp.dot(g, layer_pick, preferred_element_type=jnp.float32).astype(jnp.bfloat16)
+        low_ref[s] = layers[:, 0:64]
+        high_ref[s] = layers[:, 64:128]
+
+
+def pack(grad_out):
+    blocks, channels = grad_out.shape[0], grad_out.shape[1]
+    vmem = pl.BlockSpec(memory_space=pltpu.VMEM)
+    return pl.pallas_call(
+        pack_kernel,
+        out_shape=(
+            jax.ShapeDtypeStruct((blocks, channels, 256), jnp.bfloat16),
+            jax.ShapeDtypeStruct((blocks, channels, 64), jnp.bfloat16),
+            jax.ShapeDtypeStruct((blocks, channels, 64), jnp.bfloat16),
+        ),
+        in_specs=[vmem],
+        out_specs=(vmem, vmem, vmem),
+    )(grad_out)
+
+
+def make_kernel(blocks, channels, peers, scaling):
     slots = blocks * peers
 
     def kernel(nbr_ref, cnt_ref, me_ref, g_ref, f_ref, kmix_ref, *rest):
-        recv_refs = rest[:peers]
-        gf_ref, wg_ref, same_ref, lay_ref, stack_ref = rest[peers:]
+        face_refs = rest[:peers]
+        layer_refs = rest[peers:2 * peers]
+        gf_ref, wg_ref, same_ref, lay_ref, stack_ref, acc_ref = rest[2 * peers:]
         lane = lax.broadcasted_iota(jnp.int32, (channels, VOX), 1)
         coord = (lane // 64, (lane // 8) % 8, lane % 8)
 
@@ -61,13 +106,19 @@
         lay_ref[0, slots] = jnp.zeros((channels, VOX), jnp.bfloat16)
         lay_ref[1, slots] = jnp.zeros((channels, VOX), jnp.bfloat16)
 
+        place = face_selector(
+            lax.broadcasted_iota(jnp.int32, (256, VOX), 0),
+            lax.broadcasted_iota(jnp.int32, (256, VOX), 1),
+            True,
+        )
         for k in range(peers):
             def fill(s, carry, k=k):
-                row = recv_refs[k][s]
                 q = (jnp.bitwise_xor(me_ref[0], k)) * blocks + s
-                same_ref[q] = row[:, 0:VOX]
+                wide = jnp.dot(face_refs[k][s], place, preferred_element_type=jnp.float32)
+                same_ref[q] = wide.astype(jnp.bfloat16)
+                row = layer_refs[k][s]
                 for t in range(2):
-                    layer = row[:, VOX + 64 * t:VOX + 64 * (t + 1)]
+                    layer = row[:, 64 * t:64 * (t + 1)]
                     wide = jnp.dot(layer, spread, preferred_element_type=jnp.float32)
                     lay_ref[t, q] = wide.astype(jnp.bfloat16)
                 return carry
@@ -75,7 +126,7 @@
             lax.fori_loop(0, blocks, fill, 0)
 
         gf_ref[...] = jnp.zeros_like(gf_ref)
-        wg_ref[...] = jnp.zeros_like(wg_ref)
+        acc_ref[...] = jnp.zeros_like(acc_ref)
 
         def body(s, carry):
             own = g_ref[s]
@@ -123,62 +174,67 @@
             st = stack_ref[...]
             gf = jnp.dot(kmix_ref[...], st, preferred_element_type=jnp.float32)
             gf_ref[s] = gf.astype(jnp.bfloat16)
-            wg_ref[...] += lax.dot_general(
+            acc_ref[...] += lax.dot_general(
                 f_ref[s], st, (((1,), (1,)), ((), ())), preferred_element_type=jnp.float32
             )
             return carry
 
         lax.fori_loop(0, jnp.minimum(cnt_ref[0], blocks), body, 0)
+        for d in range(27):
+            wg_ref[d] = acc_ref[:, d * channels:(d + 1) * channels] * scaling
 
     return kernel
 
 
-def local_conv(neighbours, block_count, me, grad_out, features, kmix, received):
+def local_conv(neighbours, block_count, me, grad_out, features, kmix, faces, layers, scaling):
     blocks, channels = grad_out.shape[0], grad_out.shape[1]
-    peers = len(received)
+    peers = len(faces)
     slots = blocks * peers
     smem = pl.BlockSpec(memory_space=pltpu.SMEM)
     vmem = pl.BlockSpec(memory_space=pltpu.VMEM)
     return pl.pallas_call(
-        make_kernel(blocks, channels, peers),
+        make_kernel(blocks, channels, peers, scaling),
         out_shape=(
             jax.ShapeDtypeStruct((blocks, channels, VOX), jnp.bfloat16),
-            jax.ShapeDtypeStruct((channels, 27 * channels), jnp.float32),
+            jax.ShapeDtypeStruct((27, channels, channels), jnp.float32),
         ),
-        in_specs=[smem, smem, smem, vmem, vmem, vmem] + [vmem] * peers,
+        in_specs=[smem, smem, smem, vmem, vmem, vmem] + [vmem] * (2 * peers),
         out_specs=(vmem, vmem),
         scratch_shapes=[
             pltpu.VMEM((slots + 1, channels, VOX), jnp.bfloat16),
             pltpu.VMEM((2, slots + 1, channels, VOX), jnp.bfloat16),
             pltpu.VMEM((27 * channels, VOX), jnp.bfloat16),
+            pltpu.VMEM((channels, 27 * channels), jnp.float32),
         ],
-    )(neighbours, block_count, me, grad_out, features, kmix, *received)
+    )(neighbours, block_count, me, grad_out, features, kmix, *faces, *layers)
 
 
 def on_device(grad_out, features, kernel, block_count, neighbours):
     blocks, channels = grad_out.shape[0], grad_out.shape[1]
-    cubes = grad_out.reshape(blocks, channels, 8, 8, 8)
-    lowest = cubes[:, :, :, :, 0].reshape(blocks, channels, 64)
-    highest = cubes[:, :, :, :, 7].reshape(blocks, channels, 64)
+    faces, lowest, highest = pack(grad_out)
+    peers = lax.axis_size("split") * lax.axis_size("sub")
+    assert peers & (peers - 1) == 0
+
+    def spread_in_brick(x):
+        return [x] + [
+            lax.ppermute(x, ("split", "sub"), [(i, i ^ k) for i in range(peers)])
+            for k in range(1, peers)
+        ]
+
     from_below = from_behind(highest, "brick", 1)
     from_above = from_behind(lowest, "brick", -1)
-    packed = jnp.concatenate([grad_out, from_below, from_above], axis=2)
-    peers = lax.axis_size("split") * lax.axis_size("sub")
-    assert peers & (peers - 1) == 0
-    received = [packed] + [
-        lax.ppermute(packed, ("split", "sub"), [(i, i ^ k) for i in range(peers)])
-        for k in range(1, peers)
-    ]
+    all_faces = spread_in_brick(faces)
+    all_layers = spread_in_brick(jnp.concatenate([from_below, from_above], axis=2))
     me = (lax.axis_index("split") * lax.axis_size("sub") + lax.axis_index("sub")).astype(jnp.int32)
     kmix = jnp.transpose(kernel, (1, 0, 2)).reshape(channels, 27 * channels)
-    grad_features, wg = local_conv(
-        neighbours, block_count, me.reshape(1), grad_out, features, kmix, received
-    )
-    wg = butterfly_sum(wg, ("sub", "split", "brick"))
     scaling = 1.0 / math.sqrt(
         lax.axis_size("brick") * lax.axis_size("split") * lax.axis_size("sub") * blocks * VOX
     )
-    totals = jnp.transpose(wg.reshape(channels, 27, channels), (1, 0, 2)) * scaling
+    grad_features, wg = local_conv(
+        neighbours, block_count, me.reshape(1), grad_out, features, kmix,
+        all_faces, all_layers, scaling,
+    )
+    totals = butterfly_sum(wg, ("sub", "split", "brick"))
     return (grad_features, totals)
 
 

time: 52.4 us -> 78.4 us (1.50)
  waiting for transfers between devices: 23.5 us -> 45.9 us
  starting transfers between devices: 10.9 us -> 18.6 us
  local copies, waits for them, and re-layouts: 4.46 us -> 1.61 us
  Pallas kernels: 11.1 us -> 8.64 us
  other arithmetic: 1.05 us -> 2.11 us
    ppermute x4, waiting for transfers between devices: 14.8 us -> 41.8 us  [butterfly_sum(): x = x + lax.ppermute(x, axis, [(i, i ^ bit) for i in range(n)])]
    ppermute x4, starting transfers between devices: 3.81 us -> 9.49 us  [butterfly_sum(): x = x + lax.ppermute(x, axis, [(i, i ^ bit) for i in range(n)])]
    ppermute x3 -> x6, waiting for transfers between devices: 6.51 us -> 1.65 us  [spread_in_brick(): lax.ppermute(x, ('split', 'sub'), [(i, i ^ k) for i in range(peers)])]
    pallas_call x1 -> x2, Pallas kernels: 11.1 us -> 8.64 us  [the longest x1 6.66 us: local_conv(): pl.pallas_call(make_kernel(blocks, channels, peers, scaling), out_shape=(...]
    unnamed x16, local copies, waits for them, and re-layouts: 2.97 us -> 0.65 us
    ppermute x3 -> x6, starting transfers between devices: 1.92 us -> 4.06 us  [spread_in_brick(): lax.ppermute(x, ('split', 'sub'), [(i, i ^ k) for i in range(peers)])]
    add x3 -> x4, other arithmetic: 0.95 us -> 2.03 us  [butterfly_sum(): x = x + lax.ppermute(x, axis, [(i, i ^ bit) for i in range(n)])]
  transfers between devices with their start and end apart: 9 -> 12, of which waited for: 8 -> 7; matrix products, arithmetic and copies ran while one was open for 2% -> 1% of each run, Pallas kernels for 0% -> 0%
where the time goes in v4:
time: 78.4 us; the launch traced here: 78.3 us
  waiting for transfers between devices  45.9 us (59%)
  starting transfers between devices  18.6 us (24%)
  Pallas kernels  8.64 us (11%)
  other arithmetic  2.11 us (3%)
  local copies, waits for them, and re-layouts  1.61 us (2%)
  between operations  1.41 us (2%)
    ppermute x4, waiting for transfers between devices, butterfly_sum(): x = x + lax.ppermute(x, axis, [(i, i ^ bit) for i in range(n)])  41.8 us
    ppermute x4, starting transfers between devices, butterfly_sum(): x = x + lax.ppermute(x, axis, [(i, i ^ bit) for i in range(n)])  9.49 us
    pallas_call x1, Pallas kernels, local_conv(): pl.pallas_call(make_kernel(blocks, channels, peers, scaling), out_shape=(...  6.66 us
    ppermute x2, starting transfers between devices, from_behind(): return lax.ppermute(block, axis, route)  5.08 us
    ppermute x6, starting transfers between devices, spread_in_brick(): lax.ppermute(x, ('split', 'sub'), [(i, i ^ k) for i in range(peers)])  4.06 us
    ppermute x2, waiting for transfers between devices, from_behind(): return lax.ppermute(block, axis, route)  2.45 us
    add x4, other arithmetic, butterfly_sum(): x = x + lax.ppermute(x, axis, [(i, i ^ bit) for i in range(n)])  2.03 us
    pallas_call x1, Pallas kernels, pack(): pl.pallas_call(pack_kernel, out_shape=(jax.ShapeDtypeStruct((blocks, chan...  1.98 us
  transfers between devices with their start and end apart: 12, of which 7 were waited for; matrix products, arithmetic and copies ran while one was open for 1% of the time, Pallas kernels for 0%

profile of v4, /device:TPU:0, one launch (start us, length us, event | category | flops | bytes accessed | tf_op | source)
XLA Modules:
  0.0 78.3 jit_solution(13198871216590443320)
XLA Ops:
  0.6 2.0 %shard_map.68 = (bf16[4,32,256]{2,1,0:T(8,128)(2,1)}, bf16[4,32,64]{2,1,0:T(8,128)(2,1)}, bf16[4,32,64]{2,1,0:T(8,128)(2,1)}) custom-call(bf16[4,32,512]{2,1,0:T(8,128)(2,1)} %g_ref.3), custom_call_target="tpu_custom_call" | custom-call | tf_op jit(solution)/shard_map/pallas_call | solution.py:77
  2.6 3.1 %collective-permute-start.3 = (bf16[4,32,64]{2,1,0:T(8,128)(2,1)}, bf16[4,32,64]{2,1,0:T(8,128)(2,1)S(1)}, u32[]{:S(2)}, u32[]{:S(2)}) collective-permute-start(bf16[4,32,64]{2,1,0:T(8,128)(2,1)} %get-tuple-element.8), channel_id=1, source_target_pairs={{12,0},{0,4},{4,8},{8,12},{13,1},{1,5},{5,9},{9,13},{14,2},{2,6},{... | collective-permute-start | bytes 49160 | tf_op jit(solution)/shard_map/ppermute | solution.py:18
  5.7 2.0 %collective-permute-start.4 = (bf16[4,32,64]{2,1,0:T(8,128)(2,1)}, bf16[4,32,64]{2,1,0:T(8,128)(2,1)S(1)}, u32[]{:S(2)}, u32[]{:S(2)}) collective-permute-start(bf16[4,32,64]{2,1,0:T(8,128)(2,1)} %get-tuple-element.9), channel_id=1, source_target_pairs={{4,0},{8,4},{12,8},{0,12},{5,1},{9,5},{13,9},{1,13},{6,2},{10,6},{... | collective-permute-start | bytes 49160 | tf_op jit(solution)/shard_map/ppermute | solution.py:18
  7.7 2.2 %collective-permute-done.3 = bf16[4,32,64]{2,1,0:T(8,128)(2,1)S(1)} collective-permute-done((bf16[4,32,64]{2,1,0:T(8,128)(2,1)}, bf16[4,32,64]{2,1,0:T(8,128)(2,1)S(1)}, u32[]{:S(2)}, u32[]{:S(2)}) %collective-permute-start.3) | collective-permute-done | bytes 16416 | tf_op jit(solution)/shard_map/ppermute | solution.py:18
  9.9 0.2 collective-permute-done.4
  10.3 1.7 %collective-permute-start.2 = (bf16[4,32,256]{2,1,0:T(8,128)(2,1)}, bf16[4,32,256]{2,1,0:T(8,128)(2,1)S(1)}, u32[]{:S(2)}, u32[]{:S(2)}) collective-permute-start(bf16[4,32,256]{2,1,0:T(8,128)(2,1)} %get-tuple-element.7.rest_0_), channel_id=1, source_target_pairs={{0,3},{1,2},{2,1},{3,0},{4,7},{5,6},{6,5},{7,4},{8,11},{9,10},{10,... | collective-permute-start | bytes 196616 | tf_op jit(solution)/shard_map/ppermute | solution.py:220
  12.1 1.5 %collective-permute-start.1 = (bf16[4,32,256]{2,1,0:T(8,128)(2,1)}, bf16[4,32,256]{2,1,0:T(8,128)(2,1)S(1)}, u32[]{:S(2)}, u32[]{:S(2)}) collective-permute-start(bf16[4,32,256]{2,1,0:T(8,128)(2,1)} %get-tuple-element.7.rest_0_), channel_id=1, source_target_pairs={{0,2},{1,3},{2,0},{3,1},{4,6},{5,7},{6,4},{7,5},{8,10},{9,11},{10,... | collective-permute-start | bytes 196616 | tf_op jit(solution)/shard_map/ppermute | solution.py:220
  13.6 0.5 collective-permute-start.6
  14.1 0.2 collective-permute-start.5
  15.0 0.1 copy.8
  15.1 0.9 %reshape.11.kmix_ref = bf16[32,864]{1,0:T(8,128)(2,1)} reshape(bf16[32,27,32]{2,1,0:T(8,128)(2,1)S(1)} %copy.8) | data formatting | bytes 110592 | tf_op jit(solution)/shard_map/reshape | solution.py:229
  16.0 1.6 %collective-permute-done.6.rest_6_ = bf16[4,32,128]{2,1,0:T(8,128)(2,1)S(1)} collective-permute-done((bf16[4,32,128]{2,1,0:T(8,128)(2,1)S(1)}, bf16[4,32,128]{2,1,0:T(8,128)(2,1)S(1)}, u32[]{:S(2)}, u32[]{:S(2)}) %collective-permute-start.6) | collective-permute-done | bytes 32800 | tf_op jit(solution)/shard_map/ppermute | solution.py:220
  17.7 0.5 copy-done.6
  18.3 6.7 %shard_map.69 = (bf16[4,32,512]{2,1,0:T(8,128)(2,1)}, f32[27,32,32]{2,1,0:T(8,128)}) custom-call(s32[4,26]{1,0:T(4,128)} %nbr_ref.1, s32[1]{0:T(128)S(6)} %copy.9.cnt_ref, s32[1]{0:T(128)} %bitcast.me_ref, bf16[4,32,512]{2,1,0:T(8,128)(2,1)} %g_ref.3, bf16[4,32,512]{2,1,0:T(8,128)(2,1)} %f_ref.1, bf16[32,864]{1,0:T(8,128)(2,1)} %reshape.11.kmix_ref, ...), custom_call_target="tpu_custom_call" | custom-call | tf_op jit(solution)/shard_map/pallas_call | solution.py:195
  25.0 1.4 %collective-permute-start.8 = (f32[27,32,32]{2,1,0:T(8,128)}, f32[27,32,32]{2,1,0:T(8,128)S(1)}, u32[]{:S(2)}, u32[]{:S(2)}) collective-permute-start(f32[27,32,32]{2,1,0:T(8,128)} %get-tuple-element.11), channel_id=1, source_target_pairs={{0,1},{1,0},{2,3},{3,2},{4,5},{5,4},{6,7},{7,6},{8,9},{9,8},{10,11... | collective-permute-start | bytes 331784 | tf_op jit(solution)/shard_map/ppermute | solution.py:29
  26.3 1.6 %collective-permute-done.8 = f32[27,32,32]{2,1,0:T(8,128)S(1)} collective-permute-done((f32[27,32,32]{2,1,0:T(8,128)}, f32[27,32,32]{2,1,0:T(8,128)S(1)}, u32[]{:S(2)}, u32[]{:S(2)}) %collective-permute-start.8) | collective-permute-done | bytes 110624 | tf_op jit(solution)/shard_map/ppermute | solution.py:29
  28.0 1.1 %add.16 = f32[27,32,32]{2,1,0:T(8,128)S(1)} add(f32[27,32,32]{2,1,0:T(8,128)} %get-tuple-element.11, f32[27,32,32]{2,1,0:T(8,128)S(1)} %collective-permute-done.8) | non-fusion elementwise | flops 27648 | bytes 331776 | tf_op jit(solution)/shard_map/add | solution.py:29
  29.1 4.6 %collective-permute-start.9 = (f32[27,32,32]{2,1,0:T(8,128)S(1)}, f32[27,32,32]{2,1,0:T(8,128)S(1)}, u32[]{:S(2)}, u32[]{:S(2)}) collective-permute-start(f32[27,32,32]{2,1,0:T(8,128)S(1)} %add.16), channel_id=1, source_target_pairs={{0,2},{2,0},{1,3},{3,1},{4,6},{6,4},{5,7},{7,5},{8,10},{10,8},{9,1... | collective-permute-start | bytes 331784 | tf_op jit(solution)/shard_map/ppermute | solution.py:29
  33.7 10.5 %collective-permute-done.9 = f32[27,32,32]{2,1,0:T(8,128)S(1)} collective-permute-done((f32[27,32,32]{2,1,0:T(8,128)S(1)}, f32[27,32,32]{2,1,0:T(8,128)S(1)}, u32[]{:S(2)}, u32[]{:S(2)}) %collective-permute-start.9) | collective-permute-done | bytes 110624 | tf_op jit(solution)/shard_map/ppermute | solution.py:29
  44.2 0.5 collective-permute-start.10
  44.7 11.2 %collective-permute-done.10 = f32[27,32,32]{2,1,0:T(8,128)S(1)} collective-permute-done((f32[27,32,32]{2,1,0:T(8,128)S(1)}, f32[27,32,32]{2,1,0:T(8,128)S(1)}, u32[]{:S(2)}, u32[]{:S(2)}) %collective-permute-start.10) | collective-permute-done | bytes 110624 | tf_op jit(solution)/shard_map/ppermute | solution.py:29
  56.0 3.0 %collective-permute-start.11 = (f32[27,32,32]{2,1,0:T(8,128)S(1)}, f32[27,32,32]{2,1,0:T(8,128)S(1)}, u32[]{:S(2)}, u32[]{:S(2)}) collective-permute-start(f32[27,32,32]{2,1,0:T(8,128)S(1)} %add.18), channel_id=1, source_target_pairs={{0,8},{4,12},{8,0},{12,4},{1,9},{5,13},{9,1},{13,5},{2,10},{6,14},... | collective-permute-start | bytes 331784 | tf_op jit(solution)/shard_map/ppermute | solution.py:29
  59.0 18.5 %collective-permute-done.11 = f32[27,32,32]{2,1,0:T(8,128)S(1)} collective-permute-done((f32[27,32,32]{2,1,0:T(8,128)S(1)}, f32[27,32,32]{2,1,0:T(8,128)S(1)}, u32[]{:S(2)}, u32[]{:S(2)}) %collective-permute-start.11) | collective-permute-done | bytes 110624 | tf_op jit(solution)/shard_map/ppermute | solution.py:29
  77.5 0.8 %add.19 = f32[27,32,32]{2,1,0:T(8,128)} add(f32[27,32,32]{2,1,0:T(8,128)S(1)} %add.18, f32[27,32,32]{2,1,0:T(8,128)S(1)} %collective-permute-done.11) | non-fusion elementwise | flops 27648 | bytes 331776 | tf_op jit(solution)/shard_map/add | solution.py:29
  (25 shorter events, 0.4 us)
Async XLA Ops:
  0.6 14.3 %copy-start = (bf16[27,32,32]{2,1,0:T(8,128)(2,1)S(1)}, bf16[27,32,32]{2,1,0:T(8,128)(2,1)}, u32[]{:S(2)}) copy-start(bf16[27,32,32]{2,1,0:T(8,128)(2,1)} %param.7) | copy-start | bytes 165892
  2.6 7.3 %collective-permute-start.3 = (bf16[4,32,64]{2,1,0:T(8,128)(2,1)}, bf16[4,32,64]{2,1,0:T(8,128)(2,1)S(1)}, u32[]{:S(2)}, u32[]{:S(2)}) collective-permute-start(bf16[4,32,64]{2,1,0:T(8,128)(2,1)} %get-tuple-element.8), channel_id=1, source_target_pairs={{12,0},{0,4},{4,8},{8,12},{13,1},{1,5},{5,9},{9,13},{14,2},{2,6},{... | collective-permute-start | bytes 49160 | tf_op jit(solution)/shard_map/ppermute | solution.py:18
  5.7 4.5 %collective-permute-start.4 = (bf16[4,32,64]{2,1,0:T(8,128)(2,1)}, bf16[4,32,64]{2,1,0:T(8,128)(2,1)S(1)}, u32[]{:S(2)}, u32[]{:S(2)}) collective-permute-start(bf16[4,32,64]{2,1,0:T(8,128)(2,1)} %get-tuple-element.9), channel_id=1, source_target_pairs={{4,0},{8,4},{12,8},{0,12},{5,1},{9,5},{13,9},{1,13},{6,2},{10,6},{... | collective-permute-start | bytes 49160 | tf_op jit(solution)/shard_map/ppermute | solution.py:18
  10.2 4.9 %copy-start.1 = (bf16[4,32,128]{2,1,0:T(8,128)(2,1)}, bf16[4,32,128]{2,1,0:T(8,128)(2,1)S(1)}, u32[]{:S(2)}) copy-start(bf16[4,32,128]{2,1,0:T(8,128)(2,1)S(1)} %pad_maximum_fusion.rest_4_) | copy-start | bytes 98308
  10.2 3.8 %collective-permute-start.7 = (bf16[4,32,128]{2,1,0:T(8,128)(2,1)S(1)}, bf16[4,32,128]{2,1,0:T(8,128)(2,1)S(1)}, u32[]{:S(2)}, u32[]{:S(2)}) collective-permute-start(bf16[4,32,128]{2,1,0:T(8,128)(2,1)S(1)} %pad_maximum_fusion.rest_4_), channel_id=1, source_target_pairs={{0,3},{1,2},{2,1},{3,0},{4,7},{5,6},{6,5},{7,4},{8,11},{9,10},{10,... | collective-permute-start | bytes 98312 | tf_op jit(solution)/shard_map/ppermute | solution.py:220
  10.3 7.3 %collective-permute-start.2 = (bf16[4,32,256]{2,1,0:T(8,128)(2,1)}, bf16[4,32,256]{2,1,0:T(8,128)(2,1)S(1)}, u32[]{:S(2)}, u32[]{:S(2)}) collective-permute-start(bf16[4,32,256]{2,1,0:T(8,128)(2,1)} %get-tuple-element.7.rest_0_), channel_id=1, source_target_pairs={{0,3},{1,2},{2,1},{3,0},{4,7},{5,6},{6,5},{7,4},{8,11},{9,10},{10,... | collective-permute-start | bytes 196616 | tf_op jit(solution)/shard_map/ppermute | solution.py:220
  12.1 5.6 %collective-permute-start.1 = (bf16[4,32,256]{2,1,0:T(8,128)(2,1)}, bf16[4,32,256]{2,1,0:T(8,128)(2,1)S(1)}, u32[]{:S(2)}, u32[]{:S(2)}) collective-permute-start(bf16[4,32,256]{2,1,0:T(8,128)(2,1)} %get-tuple-element.7.rest_0_), channel_id=1, source_target_pairs={{0,2},{1,3},{2,0},{3,1},{4,6},{5,7},{6,4},{7,5},{8,10},{9,11},{10,... | collective-permute-start | bytes 196616 | tf_op jit(solution)/shard_map/ppermute | solution.py:220
  13.5 4.1 %collective-permute-start = (bf16[4,32,256]{2,1,0:T(8,128)(2,1)}, bf16[4,32,256]{2,1,0:T(8,128)(2,1)S(1)}, u32[]{:S(2)}, u32[]{:S(2)}) collective-permute-start(bf16[4,32,256]{2,1,0:T(8,128)(2,1)} %get-tuple-element.7.rest_0_), channel_id=1, source_target_pairs={{0,1},{1,0},{2,3},{3,2},{4,5},{5,4},{6,7},{7,6},{8,9},{9,8},{10,11... | collective-permute-start | bytes 196616 | tf_op jit(solution)/shard_map/ppermute | solution.py:220
  13.6 4.1 %collective-permute-start.6 = (bf16[4,32,128]{2,1,0:T(8,128)(2,1)S(1)}, bf16[4,32,128]{2,1,0:T(8,128)(2,1)S(1)}, u32[]{:S(2)}, u32[]{:S(2)}) collective-permute-start(bf16[4,32,128]{2,1,0:T(8,128)(2,1)S(1)} %pad_maximum_fusion.rest_4_), channel_id=1, source_target_pairs={{0,2},{1,3},{2,0},{3,1},{4,6},{5,7},{6,4},{7,5},{8,10},{9,11},{10,... | collective-permute-start | bytes 98312 | tf_op jit(solution)/shard_map/ppermute | solution.py:220
  14.1 1.0 %copy-start.5 = (bf16[4,32,128]{2,1,0:T(8,128)(2,1)}, bf16[4,32,128]{2,1,0:T(8,128)(2,1)S(1)}, u32[]{:S(2)}) copy-start(bf16[4,32,128]{2,1,0:T(8,128)(2,1)S(1)} %collective-permute-done.7.rest_7_) | copy-start | bytes 98308
  14.1 3.5 %collective-permute-start.5 = (bf16[4,32,128]{2,1,0:T(8,128)(2,1)S(1)}, bf16[4,32,128]{2,1,0:T(8,128)(2,1)S(1)}, u32[]{:S(2)}, u32[]{:S(2)}) collective-permute-start(bf16[4,32,128]{2,1,0:T(8,128)(2,1)S(1)} %pad_maximum_fusion.rest_4_), channel_id=1, source_target_pairs={{0,1},{1,0},{2,3},{3,2},{4,5},{5,4},{6,7},{7,6},{8,9},{9,8},{10,11... | collective-permute-start | bytes 98312 | tf_op jit(solution)/shard_map/ppermute | solution.py:220
  17.6 0.6 copy-start.6
  17.6 0.6 copy-start.7
  17.6 0.6 copy-start.2
  17.6 0.6 copy-start.3
  17.7 0.6 copy-start.4
  25.0 3.0 %collective-permute-start.8 = (f32[27,32,32]{2,1,0:T(8,128)}, f32[27,32,32]{2,1,0:T(8,128)S(1)}, u32[]{:S(2)}, u32[]{:S(2)}) collective-permute-start(f32[27,32,32]{2,1,0:T(8,128)} %get-tuple-element.11), channel_id=1, source_target_pairs={{0,1},{1,0},{2,3},{3,2},{4,5},{5,4},{6,7},{7,6},{8,9},{9,8},{10,11... | collective-permute-start | bytes 331784 | tf_op jit(solution)/shard_map/ppermute | solution.py:29
  29.1 15.1 %collective-permute-start.9 = (f32[27,32,32]{2,1,0:T(8,128)S(1)}, f32[27,32,32]{2,1,0:T(8,128)S(1)}, u32[]{:S(2)}, u32[]{:S(2)}) collective-permute-start(f32[27,32,32]{2,1,0:T(8,128)S(1)} %add.16), channel_id=1, source_target_pairs={{0,2},{2,0},{1,3},{3,1},{4,6},{6,4},{5,7},{7,5},{8,10},{10,8},{9,1... | collective-permute-start | bytes 331784 | tf_op jit(solution)/shard_map/ppermute | solution.py:29
  44.2 11.7 %collective-permute-start.10 = (f32[27,32,32]{2,1,0:T(8,128)S(1)}, f32[27,32,32]{2,1,0:T(8,128)S(1)}, u32[]{:S(2)}, u32[]{:S(2)}) collective-permute-start(f32[27,32,32]{2,1,0:T(8,128)S(1)} %add.17), channel_id=1, source_target_pairs={{0,4},{4,0},{8,12},{12,8},{1,5},{5,1},{9,13},{13,9},{2,6},{6,2},{1... | collective-permute-start | bytes 331784 | tf_op jit(solution)/shard_map/ppermute | solution.py:29
  56.0 21.5 %collective-permute-start.11 = (f32[27,32,32]{2,1,0:T(8,128)S(1)}, f32[27,32,32]{2,1,0:T(8,128)S(1)}, u32[]{:S(2)}, u32[]{:S(2)}) collective-permute-start(f32[27,32,32]{2,1,0:T(8,128)S(1)} %add.18), channel_id=1, source_target_pairs={{0,8},{4,12},{8,0},{12,4},{1,9},{5,13},{9,1},{13,5},{2,10},{6,14},... | collective-permute-start | bytes 331784 | tf_op jit(solution)/shard_map/ppermute | solution.py:29

commit v5 on v4

--- a/solution.py
+++ b/solution.py
@@ -90,9 +90,8 @@
     slots = blocks * peers
 
     def kernel(nbr_ref, cnt_ref, me_ref, g_ref, f_ref, kmix_ref, *rest):
-        face_refs = rest[:peers]
-        layer_refs = rest[peers:2 * peers]
-        gf_ref, wg_ref, same_ref, lay_ref, stack_ref, acc_ref = rest[2 * peers:]
+        shared_refs = rest[:peers]
+        gf_ref, wg_ref, same_ref, lay_ref, stack_ref, acc_ref = rest[peers:]
         lane = lax.broadcasted_iota(jnp.int32, (channels, VOX), 1)
         coord = (lane // 64, (lane // 8) % 8, lane % 8)
 
@@ -114,11 +113,11 @@
         for k in range(peers):
             def fill(s, carry, k=k):
                 q = (jnp.bitwise_xor(me_ref[0], k)) * blocks + s
-                wide = jnp.dot(face_refs[k][s], place, preferred_element_type=jnp.float32)
+                row = shared_refs[k][s]
+                wide = jnp.dot(row[:, 0:256], place, preferred_element_type=jnp.float32)
                 same_ref[q] = wide.astype(jnp.bfloat16)
-                row = layer_refs[k][s]
                 for t in range(2):
-                    layer = row[:, 64 * t:64 * (t + 1)]
+                    layer = row[:, 256 + 64 * t:256 + 64 * (t + 1)]
                     wide = jnp.dot(layer, spread, preferred_element_type=jnp.float32)
                     lay_ref[t, q] = wide.astype(jnp.bfloat16)
                 return carry
@@ -180,15 +179,14 @@
             return carry
 
         lax.fori_loop(0, jnp.minimum(cnt_ref[0], blocks), body, 0)
-        for d in range(27):
-            wg_ref[d] = acc_ref[:, d * channels:(d + 1) * channels] * scaling
+        wg_ref[...] = acc_ref[...] * scaling
 
     return kernel
 
 
-def local_conv(neighbours, block_count, me, grad_out, features, kmix, faces, layers, scaling):
+def local_conv(neighbours, block_count, me, grad_out, features, kmix, shared, scaling):
     blocks, channels = grad_out.shape[0], grad_out.shape[1]
-    peers = len(faces)
+    peers = len(shared)
     slots = blocks * peers
     smem = pl.BlockSpec(memory_space=pltpu.SMEM)
     vmem = pl.BlockSpec(memory_space=pltpu.VMEM)
@@ -196,9 +194,9 @@
         make_kernel(blocks, channels, peers, scaling),
         out_shape=(
             jax.ShapeDtypeStruct((blocks, channels, VOX), jnp.bfloat16),
-            jax.ShapeDtypeStruct((27, channels, channels), jnp.float32),
+            jax.ShapeDtypeStruct((channels, 27 * channels), jnp.float32),
         ),
-        in_specs=[smem, smem, smem, vmem, vmem, vmem] + [vmem] * (2 * peers),
+        in_specs=[smem, smem, smem, vmem, vmem, vmem] + [vmem] * peers,
         out_specs=(vmem, vmem),
         scratch_shapes=[
             pltpu.VMEM((slots + 1, channels, VOX), jnp.bfloat16),
@@ -206,7 +204,7 @@
             pltpu.VMEM((27 * channels, VOX), jnp.bfloat16),
             pltpu.VMEM((channels, 27 * channels), jnp.float32),
         ],
-    )(neighbours, block_count, me, grad_out, features, kmix, *faces, *layers)
+    )(neighbours, block_count, me, grad_out, features, kmix, *shared)
 
 
 def on_device(grad_out, features, kernel, block_count, neighbours):
@@ -223,8 +221,7 @@
 
     from_below = from_behind(highest, "brick", 1)
     from_above = from_behind(lowest, "brick", -1)
-    all_faces = spread_in_brick(faces)
-    all_layers = spread_in_brick(jnp.concatenate([from_below, from_above], axis=2))
+    shared = spread_in_brick(jnp.concatenate([faces, from_below, from_above], axis=2))
     me = (lax.axis_index("split") * lax.axis_size("sub") + lax.axis_index("sub")).astype(jnp.int32)
     kmix = jnp.transpose(kernel, (1, 0, 2)).reshape(channels, 27 * channels)
     scaling = 1.0 / math.sqrt(
@@ -232,9 +229,10 @@
     )
     grad_features, wg = local_conv(
         neighbours, block_count, me.reshape(1), grad_out, features, kmix,
-        all_faces, all_layers, scaling,
-    )
-    totals = butterfly_sum(wg, ("sub", "split", "brick"))
+        shared, scaling,
+    )
+    wg = butterfly_sum(wg, ("sub", "split", "brick"))
+    totals = jnp.transpose(wg.reshape(channels, 27, channels), (1, 0, 2))
     return (grad_features, totals)
 
 

time: 78.4 us -> 50.8 us (0.65)
  waiting for transfers between devices: 45.9 us -> 21 us
  starting transfers between devices: 18.6 us -> 15.2 us
  local copies, waits for them, and re-layouts: 1.61 us -> 2.83 us
    ppermute x4, waiting for transfers between devices: 41.8 us -> 14.8 us  [butterfly_sum(): x = x + lax.ppermute(x, axis, [(i, i ^ bit) for i in range(n)])]
    ppermute x6 -> x3, starting transfers between devices: 4.06 us -> 1.92 us  [spread_in_brick(): lax.ppermute(x, ('split', 'sub'), [(i, i ^ k) for i in range(peers)])]
    ppermute x6 -> x3, waiting for transfers between devices: 1.65 us -> 3.7 us  [spread_in_brick(): lax.ppermute(x, ('split', 'sub'), [(i, i ^ k) for i in range(peers)])]
    ppermute x4, starting transfers between devices: 9.49 us -> 8.24 us  [butterfly_sum(): x = x + lax.ppermute(x, axis, [(i, i ^ bit) for i in range(n)])]
    add x4, other arithmetic: 2.03 us -> 0.96 us  [butterfly_sum(): x = x + lax.ppermute(x, axis, [(i, i ^ bit) for i in range(n)])]
    unnamed x16 -> x11, local copies, waits for them, and re-layouts: 0.65 us -> 1.7 us
    concatenate x1, other arithmetic: 0.08 us -> 0.92 us  [on_device(): jnp.concatenate([faces, from_below, from_above], axis=2)]
  transfers between devices with their start and end apart: 12 -> 9, of which waited for: 7 -> 8; matrix products, arithmetic and copies ran while one was open for 1% -> 2% of each run, Pallas kernels for 0% -> 0%
where the time goes in v5:
time: 50.8 us
  waiting for transfers between devices  21 us (41%)
  starting transfers between devices  15.2 us (30%)
  Pallas kernels  8.48 us (17%)
  local copies, waits for them, and re-layouts  2.83 us (6%)
  other arithmetic  1.88 us (4%)
  between operations  1.38 us (3%)
    ppermute x4, waiting for transfers between devices, butterfly_sum(): x = x + lax.ppermute(x, axis, [(i, i ^ bit) for i in range(n)])  14.8 us
    ppermute x4, starting transfers between devices, butterfly_sum(): x = x + lax.ppermute(x, axis, [(i, i ^ bit) for i in range(n)])  8.24 us
    pallas_call x1, Pallas kernels, local_conv(): pl.pallas_call(make_kernel(blocks, channels, peers, scaling), out_shape=(...  6.51 us
    ppermute x2, starting transfers between devices, from_behind(): return lax.ppermute(block, axis, route)  5.08 us
    ppermute x3, waiting for transfers between devices, spread_in_brick(): lax.ppermute(x, ('split', 'sub'), [(i, i ^ k) for i in range(peers)])  3.7 us
    ppermute x2, waiting for transfers between devices, from_behind(): return lax.ppermute(block, axis, route)  2.45 us
    pallas_call x1, Pallas kernels, pack(): pl.pallas_call(pack_kernel, out_shape=(jax.ShapeDtypeStruct((blocks, chan...  1.96 us
    ppermute x3, starting transfers between devices, spread_in_brick(): lax.ppermute(x, ('split', 'sub'), [(i, i ^ k) for i in range(peers)])  1.92 us
  transfers between devices with their start and end apart: 9, of which 8 were waited for; matrix products, arithmetic and copies ran while one was open for 2% of the time, Pallas kernels for 0%

profile of v5, /device:TPU:0, one launch (start us, length us, event | category | flops | bytes accessed | tf_op | source)
XLA Modules:
  0.0 50.8 jit_solution(8512712409086102020)
XLA Ops:
  0.6 2.0 %shard_map.68 = (bf16[4,32,256]{2,1,0:T(8,128)(2,1)}, bf16[4,32,64]{2,1,0:T(8,128)(2,1)}, bf16[4,32,64]{2,1,0:T(8,128)(2,1)}) custom-call(bf16[4,32,512]{2,1,0:T(8,128)(2,1)} %g_ref.3), custom_call_target="tpu_custom_call" | custom-call | tf_op jit(solution)/shard_map/pallas_call | solution.py:77
  2.6 3.1 %collective-permute-start = (bf16[4,32,64]{2,1,0:T(8,128)(2,1)}, bf16[4,32,64]{2,1,0:T(8,128)(2,1)S(1)}, u32[]{:S(2)}, u32[]{:S(2)}) collective-permute-start(bf16[4,32,64]{2,1,0:T(8,128)(2,1)} %get-tuple-element.8), channel_id=1, source_target_pairs={{12,0},{0,4},{4,8},{8,12},{13,1},{1,5},{5,9},{9,13},{14,2},{2,6},{... | collective-permute-start | bytes 49160 | tf_op jit(solution)/shard_map/ppermute | solution.py:18
  5.7 2.0 %collective-permute-start.1 = (bf16[4,32,64]{2,1,0:T(8,128)(2,1)}, bf16[4,32,64]{2,1,0:T(8,128)(2,1)S(1)}, u32[]{:S(2)}, u32[]{:S(2)}) collective-permute-start(bf16[4,32,64]{2,1,0:T(8,128)(2,1)} %get-tuple-element.9), channel_id=1, source_target_pairs={{4,0},{8,4},{12,8},{0,12},{5,1},{9,5},{13,9},{1,13},{6,2},{10,6},{... | collective-permute-start | bytes 49160 | tf_op jit(solution)/shard_map/ppermute | solution.py:18
  7.7 2.2 %collective-permute-done = bf16[4,32,64]{2,1,0:T(8,128)(2,1)S(1)} collective-permute-done((bf16[4,32,64]{2,1,0:T(8,128)(2,1)}, bf16[4,32,64]{2,1,0:T(8,128)(2,1)S(1)}, u32[]{:S(2)}, u32[]{:S(2)}) %collective-permute-start) | collective-permute-done | bytes 16416 | tf_op jit(solution)/shard_map/ppermute | solution.py:18
  9.9 0.2 collective-permute-done.1
  10.1 0.9 %pad_maximum_fusion.rest_0_ = bf16[4,32,384]{2,1,0:T(8,128)(2,1)S(1)} fusion(bf16[4,32,64]{2,1,0:T(8,128)(2,1)S(1)} %collective-permute-done.1, bf16[4,32,64]{2,1,0:T(8,128)(2,1)S(1)} %collective-permute-done, bf16[4,32,256]{2,1,0:T(8,128)(2,1)} %get-tuple-element.7), kind=kLoop, calls=%fused_computation | loop fusion | flops 294912 | bytes 196608 | tf_op jit(solution)/shard_map/concatenate | solution.py:224
  11.1 1.6 %collective-permute-start.3 = (bf16[4,32,384]{2,1,0:T(8,128)(2,1)S(1)}, bf16[4,32,384]{2,1,0:T(8,128)(2,1)S(1)}, u32[]{:S(2)}, u32[]{:S(2)}) collective-permute-start(bf16[4,32,384]{2,1,0:T(8,128)(2,1)S(1)} %pad_maximum_fusion.rest_0_), channel_id=1, source_target_pairs={{0,2},{1,3},{2,0},{3,1},{4,6},{5,7},{6,4},{7,5},{8,10},{9,11},{10,... | collective-permute-start | bytes 294920 | tf_op jit(solution)/shard_map/ppermute | solution.py:218
  12.7 0.3 collective-permute-start.2
  13.7 0.1 copy.9
  13.8 0.9 %reshape.14.kmix_ref = bf16[32,864]{1,0:T(8,128)(2,1)} reshape(bf16[32,27,32]{2,1,0:T(8,128)(2,1)S(1)} %copy.9) | data formatting | bytes 110592 | tf_op jit(solution)/shard_map/reshape | solution.py:226
  14.6 1.5 %collective-permute-done.4.rest_3_ = bf16[4,32,384]{2,1,0:T(8,128)(2,1)S(1)} collective-permute-done((bf16[4,32,384]{2,1,0:T(8,128)(2,1)S(1)}, bf16[4,32,384]{2,1,0:T(8,128)(2,1)S(1)}, u32[]{:S(2)}, u32[]{:S(2)}) %collective-permute-start.4) | collective-permute-done | bytes 98336 | tf_op jit(solution)/shard_map/ppermute | solution.py:218
  16.2 2.2 %collective-permute-done.3.rest_2_ = bf16[4,32,384]{2,1,0:T(8,128)(2,1)S(1)} collective-permute-done((bf16[4,32,384]{2,1,0:T(8,128)(2,1)S(1)}, bf16[4,32,384]{2,1,0:T(8,128)(2,1)S(1)}, u32[]{:S(2)}, u32[]{:S(2)}) %collective-permute-start.3) | collective-permute-done | bytes 98336 | tf_op jit(solution)/shard_map/ppermute | solution.py:218
  18.3 0.6 %copy-done.3 = bf16[4,32,384]{2,1,0:T(8,128)(2,1)} copy-done((bf16[4,32,384]{2,1,0:T(8,128)(2,1)}, bf16[4,32,384]{2,1,0:T(8,128)(2,1)S(1)}, u32[]{:S(2)}) %copy-start.3) | copy-done | bytes 98328
  19.0 6.5 %shard_map.69 = (bf16[4,32,512]{2,1,0:T(8,128)(2,1)}, f32[32,864]{1,0:T(8,128)}) custom-call(s32[4,26]{1,0:T(4,128)} %nbr_ref.1, s32[1]{0:T(128)S(6)} %copy.11.cnt_ref, s32[1]{0:T(128)} %bitcast.me_ref, bf16[4,32,512]{2,1,0:T(8,128)(2,1)} %g_ref.3, bf16[4,32,512]{2,1,0:T(8,128)(2,1)} %f_ref.1, bf16[32,864]{1,0:T(8,128)(2,1)} %reshape.14.kmix_ref, ...), custom_call_target="tpu_custom_call" | custom-call | tf_op jit(solution)/shard_map/pallas_call | solution.py:193
  25.5 4.6 %collective-permute-start.5 = (f32[32,864]{1,0:T(8,128)}, f32[32,864]{1,0:T(8,128)S(1)}, u32[]{:S(2)}, u32[]{:S(2)}) collective-permute-start(f32[32,864]{1,0:T(8,128)} %get-tuple-element.11), channel_id=1, source_target_pairs={{0,1},{1,0},{2,3},{3,2},{4,5},{5,4},{6,7},{7,6},{8,9},{9,8},{10,11... | collective-permute-start | bytes 331784 | tf_op jit(solution)/shard_map/ppermute | solution.py:29
  30.1 1.2 %collective-permute-done.5 = f32[32,864]{1,0:T(8,128)S(1)} collective-permute-done((f32[32,864]{1,0:T(8,128)}, f32[32,864]{1,0:T(8,128)S(1)}, u32[]{:S(2)}, u32[]{:S(2)}) %collective-permute-start.5) | collective-permute-done | bytes 110624 | tf_op jit(solution)/shard_map/ppermute | solution.py:29
  31.3 0.9 %add.16 = f32[32,864]{1,0:T(8,128)S(1)} add(f32[32,864]{1,0:T(8,128)} %get-tuple-element.11, f32[32,864]{1,0:T(8,128)S(1)} %collective-permute-done.5) | non-fusion elementwise | flops 27648 | bytes 331776 | tf_op jit(solution)/shard_map/add | solution.py:29
  32.3 5.4 %collective-permute-done.6 = f32[32,864]{1,0:T(8,128)S(1)} collective-permute-done((f32[32,864]{1,0:T(8,128)S(1)}, f32[32,864]{1,0:T(8,128)S(1)}, u32[]{:S(2)}, u32[]{:S(2)}) %collective-permute-start.6) | collective-permute-done | bytes 110624 | tf_op jit(solution)/shard_map/ppermute | solution.py:29
  37.7 1.3 %collective-permute-start.7 = (f32[32,864]{1,0:T(8,128)S(1)}, f32[32,864]{1,0:T(8,128)S(1)}, u32[]{:S(2)}, u32[]{:S(2)}) collective-permute-start(f32[32,864]{1,0:T(8,128)S(1)} %add.17), channel_id=1, source_target_pairs={{0,4},{4,0},{8,12},{12,8},{1,5},{5,1},{9,13},{13,9},{2,6},{6,2},{1... | collective-permute-start | bytes 331784 | tf_op jit(solution)/shard_map/ppermute | solution.py:29
  39.0 3.6 %collective-permute-done.7 = f32[32,864]{1,0:T(8,128)S(1)} collective-permute-done((f32[32,864]{1,0:T(8,128)S(1)}, f32[32,864]{1,0:T(8,128)S(1)}, u32[]{:S(2)}, u32[]{:S(2)}) %collective-permute-start.7) | collective-permute-done | bytes 110624 | tf_op jit(solution)/shard_map/ppermute | solution.py:29
  42.6 2.3 %collective-permute-start.8 = (f32[32,864]{1,0:T(8,128)S(1)}, f32[32,864]{1,0:T(8,128)S(1)}, u32[]{:S(2)}, u32[]{:S(2)}) collective-permute-start(f32[32,864]{1,0:T(8,128)S(1)} %add.18), channel_id=1, source_target_pairs={{0,8},{4,12},{8,0},{12,4},{1,9},{5,13},{9,1},{13,5},{2,10},{6,14},... | collective-permute-start | bytes 331784 | tf_op jit(solution)/shard_map/ppermute | solution.py:29
  44.9 4.7 %collective-permute-done.8 = f32[32,864]{1,0:T(8,128)S(1)} collective-permute-done((f32[32,864]{1,0:T(8,128)S(1)}, f32[32,864]{1,0:T(8,128)S(1)}, u32[]{:S(2)}, u32[]{:S(2)}) %collective-permute-start.8) | collective-permute-done | bytes 110624 | tf_op jit(solution)/shard_map/ppermute | solution.py:29
  49.6 0.2 reshape.15
  49.7 1.0 %copy.10 = f32[27,32,32]{2,1,0:T(8,128)} copy(f32[27,32,32]{2,0,1:T(8,128)S(1)} %bitcast.3) | data formatting | bytes 221184
  (15 shorter events, 0.2 us)
Async XLA Ops:
  0.6 13.0 %copy-start.1 = (bf16[27,32,32]{2,1,0:T(8,128)(2,1)S(1)}, bf16[27,32,32]{2,1,0:T(8,128)(2,1)}, u32[]{:S(2)}) copy-start(bf16[27,32,32]{2,1,0:T(8,128)(2,1)} %param.7) | copy-start | bytes 165892
  2.6 7.3 %collective-permute-start = (bf16[4,32,64]{2,1,0:T(8,128)(2,1)}, bf16[4,32,64]{2,1,0:T(8,128)(2,1)S(1)}, u32[]{:S(2)}, u32[]{:S(2)}) collective-permute-start(bf16[4,32,64]{2,1,0:T(8,128)(2,1)} %get-tuple-element.8), channel_id=1, source_target_pairs={{12,0},{0,4},{4,8},{8,12},{13,1},{1,5},{5,9},{9,13},{14,2},{2,6},{... | collective-permute-start | bytes 49160 | tf_op jit(solution)/shard_map/ppermute | solution.py:18
  5.7 4.5 %collective-permute-start.1 = (bf16[4,32,64]{2,1,0:T(8,128)(2,1)}, bf16[4,32,64]{2,1,0:T(8,128)(2,1)S(1)}, u32[]{:S(2)}, u32[]{:S(2)}) collective-permute-start(bf16[4,32,64]{2,1,0:T(8,128)(2,1)} %get-tuple-element.9), channel_id=1, source_target_pairs={{4,0},{8,4},{12,8},{0,12},{5,1},{9,5},{13,9},{1,13},{6,2},{10,6},{... | collective-permute-start | bytes 49160 | tf_op jit(solution)/shard_map/ppermute | solution.py:18
  11.1 2.7 %copy-start = (bf16[4,32,384]{2,1,0:T(8,128)(2,1)}, bf16[4,32,384]{2,1,0:T(8,128)(2,1)S(1)}, u32[]{:S(2)}) copy-start(bf16[4,32,384]{2,1,0:T(8,128)(2,1)S(1)} %pad_maximum_fusion.rest_0_) | copy-start | bytes 294916
  11.1 5.1 %collective-permute-start.4 = (bf16[4,32,384]{2,1,0:T(8,128)(2,1)S(1)}, bf16[4,32,384]{2,1,0:T(8,128)(2,1)S(1)}, u32[]{:S(2)}, u32[]{:S(2)}) collective-permute-start(bf16[4,32,384]{2,1,0:T(8,128)(2,1)S(1)} %pad_maximum_fusion.rest_0_), channel_id=1, source_target_pairs={{0,3},{1,2},{2,1},{3,0},{4,7},{5,6},{6,5},{7,4},{8,11},{9,10},{10,... | collective-permute-start | bytes 294920 | tf_op jit(solution)/shard_map/ppermute | solution.py:218
  11.1 7.2 %collective-permute-start.3 = (bf16[4,32,384]{2,1,0:T(8,128)(2,1)S(1)}, bf16[4,32,384]{2,1,0:T(8,128)(2,1)S(1)}, u32[]{:S(2)}, u32[]{:S(2)}) collective-permute-start(bf16[4,32,384]{2,1,0:T(8,128)(2,1)S(1)} %pad_maximum_fusion.rest_0_), channel_id=1, source_target_pairs={{0,2},{1,3},{2,0},{3,1},{4,6},{5,7},{6,4},{7,5},{8,10},{9,11},{10,... | collective-permute-start | bytes 294920 | tf_op jit(solution)/shard_map/ppermute | solution.py:218
  12.7 5.6 %collective-permute-start.2 = (bf16[4,32,384]{2,1,0:T(8,128)(2,1)S(1)}, bf16[4,32,384]{2,1,0:T(8,128)(2,1)S(1)}, u32[]{:S(2)}, u32[]{:S(2)}) collective-permute-start(bf16[4,32,384]{2,1,0:T(8,128)(2,1)S(1)} %pad_maximum_fusion.rest_0_), channel_id=1, source_target_pairs={{0,1},{1,0},{2,3},{3,2},{4,5},{5,4},{6,7},{7,6},{8,9},{9,8},{10,11... | collective-permute-start | bytes 294920 | tf_op jit(solution)/shard_map/ppermute | solution.py:218
  16.2 2.2 %copy-start.2 = (bf16[4,32,384]{2,1,0:T(8,128)(2,1)}, bf16[4,32,384]{2,1,0:T(8,128)(2,1)S(1)}, u32[]{:S(2)}) copy-start(bf16[4,32,384]{2,1,0:T(8,128)(2,1)S(1)} %collective-permute-done.4.rest_3_) | copy-start | bytes 294916
  18.3 0.6 %copy-start.3 = (bf16[4,32,384]{2,1,0:T(8,128)(2,1)}, bf16[4,32,384]{2,1,0:T(8,128)(2,1)S(1)}, u32[]{:S(2)}) copy-start(bf16[4,32,384]{2,1,0:T(8,128)(2,1)S(1)} %collective-permute-done.3.rest_2_) | copy-start | bytes 294916
  18.3 0.7 %copy-start.4 = (bf16[4,32,384]{2,1,0:T(8,128)(2,1)}, bf16[4,32,384]{2,1,0:T(8,128)(2,1)S(1)}, u32[]{:S(2)}) copy-start(bf16[4,32,384]{2,1,0:T(8,128)(2,1)S(1)} %collective-permute-done.2.rest_1_) | copy-start | bytes 294916
  25.5 5.8 %collective-permute-start.5 = (f32[32,864]{1,0:T(8,128)}, f32[32,864]{1,0:T(8,128)S(1)}, u32[]{:S(2)}, u32[]{:S(2)}) collective-permute-start(f32[32,864]{1,0:T(8,128)} %get-tuple-element.11), channel_id=1, source_target_pairs={{0,1},{1,0},{2,3},{3,2},{4,5},{5,4},{6,7},{7,6},{8,9},{9,8},{10,11... | collective-permute-start | bytes 331784 | tf_op jit(solution)/shard_map/ppermute | solution.py:29
  32.2 5.5 %collective-permute-start.6 = (f32[32,864]{1,0:T(8,128)S(1)}, f32[32,864]{1,0:T(8,128)S(1)}, u32[]{:S(2)}, u32[]{:S(2)}) collective-permute-start(f32[32,864]{1,0:T(8,128)S(1)} %add.16), channel_id=1, source_target_pairs={{0,2},{2,0},{1,3},{3,1},{4,6},{6,4},{5,7},{7,5},{8,10},{10,8},{9,1... | collective-permute-start | bytes 331784 | tf_op jit(solution)/shard_map/ppermute | solution.py:29
  37.7 4.9 %collective-permute-start.7 = (f32[32,864]{1,0:T(8,128)S(1)}, f32[32,864]{1,0:T(8,128)S(1)}, u32[]{:S(2)}, u32[]{:S(2)}) collective-permute-start(f32[32,864]{1,0:T(8,128)S(1)} %add.17), channel_id=1, source_target_pairs={{0,4},{4,0},{8,12},{12,8},{1,5},{5,1},{9,13},{13,9},{2,6},{6,2},{1... | collective-permute-start | bytes 331784 | tf_op jit(solution)/shard_map/ppermute | solution.py:29
  42.6 7.0 %collective-permute-start.8 = (f32[32,864]{1,0:T(8,128)S(1)}, f32[32,864]{1,0:T(8,128)S(1)}, u32[]{:S(2)}, u32[]{:S(2)}) collective-permute-start(f32[32,864]{1,0:T(8,128)S(1)} %add.18), channel_id=1, source_target_pairs={{0,8},{4,12},{8,0},{12,4},{1,9},{5,13},{9,1},{13,5},{2,10},{6,14},... | collective-permute-start | bytes 331784 | tf_op jit(solution)/shard_map/ppermute | solution.py:29

commit v6 on v5

--- a/solution.py
+++ b/solution.py
@@ -1,4 +1,6 @@
 import math
+
+import numpy as np
 
 import jax
 import jax.numpy as jnp
@@ -42,36 +44,37 @@
     return sorted(found, key=lambda e: sum(1 for t in e if t != 0))
 
 
-def face_selector(rows, cols, transpose):
-    v, j = (cols, rows) if transpose else (rows, cols)
-    face, r = j // 64, j % 64
-    hi, lo = r // 8, r % 8
-    target = jnp.where(face == 0, r, 448 + r)
-    target = jnp.where(face == 2, hi * 64 + lo, target)
-    target = jnp.where(face == 3, hi * 64 + 56 + lo, target)
-    hit = v == target
-    if transpose:
-        inner = (v // 64 != 0) & (v // 64 != 7)
-        hit = hit & ((face < 2) | inner)
-    return hit.astype(jnp.bfloat16)
-
-
-def pack_kernel(g_ref, faces_ref, low_ref, high_ref):
-    rows = lax.broadcasted_iota(jnp.int32, (VOX, 256), 0)
-    cols = lax.broadcasted_iota(jnp.int32, (VOX, 256), 1)
-    pick = face_selector(rows, cols, False)
-    lrows = lax.broadcasted_iota(jnp.int32, (VOX, 128), 0)
-    lcols = lax.broadcasted_iota(jnp.int32, (VOX, 128), 1)
-    layer_pick = (lrows == (lcols % 64) * 8 + 7 * (lcols // 64)).astype(jnp.bfloat16)
-    for s in range(g_ref.shape[0]):
-        g = g_ref[s]
-        faces_ref[s] = jnp.dot(g, pick, preferred_element_type=jnp.float32).astype(jnp.bfloat16)
-        layers = jnp.dot(g, layer_pick, preferred_element_type=jnp.float32).astype(jnp.bfloat16)
-        low_ref[s] = layers[:, 0:64]
-        high_ref[s] = layers[:, 64:128]
-
-
-def pack(grad_out):
+def selectors():
+    v = np.arange(VOX)
+    x, y, z = v // 64, (v // 8) % 8, v % 8
+    pick = np.zeros((VOX, 384), np.float32)
+    place = np.zeros((256, VOX), np.float32)
+    for face, (axis, side) in enumerate(((0, 0), (0, 7), (1, 0), (1, 7))):
+        coord = (x, y)[axis]
+        other = y if axis == 0 else x
+        on = np.nonzero(coord == side)[0]
+        cols = face * 64 + other[on] * 8 + z[on]
+        pick[on, cols] = 1.0
+        keep = on if axis == 0 else on[(x[on] != 0) & (x[on] != 7)]
+        place[face * 64 + other[keep] * 8 + z[keep], keep] = 1.0
+    for t, side in enumerate((0, 7)):
+        on = np.nonzero(z == side)[0]
+        pick[on, 256 + 64 * t + x[on] * 8 + y[on]] = 1.0
+    spread = (v[None, :] // 8 == np.arange(64)[:, None]).astype(np.float32)
+    as_bf16 = lambda a: jnp.asarray(a, jnp.bfloat16)
+    return as_bf16(pick), as_bf16(place), as_bf16(spread)
+
+
+def pack_kernel(g_ref, pick_ref, faces_ref, low_ref, high_ref):
+    blocks, channels = g_ref.shape[0], g_ref.shape[1]
+    g = g_ref[...].reshape(blocks * channels, VOX)
+    out = jnp.dot(g, pick_ref[...], preferred_element_type=jnp.float32).astype(jnp.bfloat16)
+    faces_ref[...] = out[:, 0:256].reshape(blocks, channels, 256)
+    low_ref[...] = out[:, 256:320].reshape(blocks, channels, 64)
+    high_ref[...] = out[:, 320:384].reshape(blocks, channels, 64)
+
+
+def pack(grad_out, pick):
     blocks, channels = grad_out.shape[0], grad_out.shape[1]
     vmem = pl.BlockSpec(memory_space=pltpu.VMEM)
     return pl.pallas_call(
@@ -81,15 +84,15 @@
             jax.ShapeDtypeStruct((blocks, channels, 64), jnp.bfloat16),
             jax.ShapeDtypeStruct((blocks, channels, 64), jnp.bfloat16),
         ),
-        in_specs=[vmem],
+        in_specs=[vmem, vmem],
         out_specs=(vmem, vmem, vmem),
-    )(grad_out)
+    )(grad_out, pick)
 
 
 def make_kernel(blocks, channels, peers, scaling):
     slots = blocks * peers
 
-    def kernel(nbr_ref, cnt_ref, me_ref, g_ref, f_ref, kmix_ref, *rest):
+    def kernel(nbr_ref, cnt_ref, me_ref, g_ref, f_ref, kmix_ref, place_ref, spread_ref, *rest):
         shared_refs = rest[:peers]
         gf_ref, wg_ref, same_ref, lay_ref, stack_ref, acc_ref = rest[peers:]
         lane = lax.broadcasted_iota(jnp.int32, (channels, VOX), 1)
@@ -98,31 +101,20 @@
         def boundary(axis, sign):
             return coord[axis] == (7 if sign < 0 else 0)
 
-        rows = lax.broadcasted_iota(jnp.int32, (64, VOX), 0)
-        cols = lax.broadcasted_iota(jnp.int32, (64, VOX), 1)
-        spread = (cols // 8 == rows).astype(jnp.bfloat16)
         same_ref[slots] = jnp.zeros((channels, VOX), jnp.bfloat16)
         lay_ref[0, slots] = jnp.zeros((channels, VOX), jnp.bfloat16)
         lay_ref[1, slots] = jnp.zeros((channels, VOX), jnp.bfloat16)
-
-        place = face_selector(
-            lax.broadcasted_iota(jnp.int32, (256, VOX), 0),
-            lax.broadcasted_iota(jnp.int32, (256, VOX), 1),
-            True,
-        )
+        place = place_ref[...]
+        spread = spread_ref[...]
         for k in range(peers):
-            def fill(s, carry, k=k):
-                q = (jnp.bitwise_xor(me_ref[0], k)) * blocks + s
-                row = shared_refs[k][s]
-                wide = jnp.dot(row[:, 0:256], place, preferred_element_type=jnp.float32)
-                same_ref[q] = wide.astype(jnp.bfloat16)
-                for t in range(2):
-                    layer = row[:, 256 + 64 * t:256 + 64 * (t + 1)]
-                    wide = jnp.dot(layer, spread, preferred_element_type=jnp.float32)
-                    lay_ref[t, q] = wide.astype(jnp.bfloat16)
-                return carry
-
-            lax.fori_loop(0, blocks, fill, 0)
+            first = pl.ds(jnp.bitwise_xor(me_ref[0], k) * blocks, blocks)
+            rows = shared_refs[k][...].reshape(blocks * channels, 384)
+            wide = jnp.dot(rows[:, 0:256], place, preferred_element_type=jnp.float32)
+            same_ref[first] = wide.astype(jnp.bfloat16).reshape(blocks, channels, VOX)
+            for t in range(2):
+                layer = rows[:, 256 + 64 * t:256 + 64 * (t + 1)]
+                wide = jnp.dot(layer, spread, preferred_element_type=jnp.float32)
+                lay_ref[t, first] = wide.astype(jnp.bfloat16).reshape(blocks, channels, VOX)
 
         gf_ref[...] = jnp.zeros_like(gf_ref)
         acc_ref[...] = jnp.zeros_like(acc_ref)
@@ -184,7 +176,7 @@
     return kernel
 
 
-def local_conv(neighbours, block_count, me, grad_out, features, kmix, shared, scaling):
+def local_conv(neighbours, block_count, me, grad_out, features, kmix, place, spread, shared, scaling):
     blocks, channels = grad_out.shape[0], grad_out.shape[1]
     peers = len(shared)
     slots = blocks * peers
@@ -196,7 +188,7 @@
             jax.ShapeDtypeStruct((blocks, channels, VOX), jnp.bfloat16),
             jax.ShapeDtypeStruct((channels, 27 * channels), jnp.float32),
         ),
-        in_specs=[smem, smem, smem, vmem, vmem, vmem] + [vmem] * peers,
+        in_specs=[smem, smem, smem, vmem, vmem, vmem, vmem, vmem] + [vmem] * peers,
         out_specs=(vmem, vmem),
         scratch_shapes=[
             pltpu.VMEM((slots + 1, channels, VOX), jnp.bfloat16),
@@ -204,12 +196,13 @@
             pltpu.VMEM((27 * channels, VOX), jnp.bfloat16),
             pltpu.VMEM((channels, 27 * channels), jnp.float32),
         ],
-    )(neighbours, block_count, me, grad_out, features, kmix, *shared)
+    )(neighbours, block_count, me, grad_out, features, kmix, place, spread, *shared)
 
 
 def on_device(grad_out, features, kernel, block_count, neighbours):
     blocks, channels = grad_out.shape[0], grad_out.shape[1]
-    faces, lowest, highest = pack(grad_out)
+    pick, place, spread = selectors()
+    faces, lowest, highest = pack(grad_out, pick)
     peers = lax.axis_size("split") * lax.axis_size("sub")
     assert peers & (peers - 1) == 0
 
@@ -228,7 +221,7 @@
         lax.axis_size("brick") * lax.axis_size("split") * lax.axis_size("sub") * blocks * VOX
     )
     grad_features, wg = local_conv(
-        neighbours, block_count, me.reshape(1), grad_out, features, kmix,
+        neighbours, block_count, me.reshape(1), grad_out, features, kmix, place, spread,
         shared, scaling,
     )
     wg = butterfly_sum(wg, ("sub", "split", "brick"))

time: 50.8 us -> 47.1 us (0.927)
  starting transfers between devices: 15.2 us -> 13.7 us
  Pallas kernels: 8.48 us -> 7.48 us
  waiting for transfers between devices: 21 us -> 20 us
    ppermute x4, starting transfers between devices: 8.24 us -> 6.7 us  [butterfly_sum(): x = x + lax.ppermute(x, axis, [(i, i ^ bit) for i in range(n)])]
    pallas_call x1, Pallas kernels: 6.51 us -> 5.53 us  [local_conv(): pl.pallas_call(make_kernel(blocks, channels, peers, scaling), out_shape=(...]
    ppermute x4, waiting for transfers between devices: 14.8 us -> 13.9 us  [butterfly_sum(): x = x + lax.ppermute(x, axis, [(i, i ^ bit) for i in range(n)])]
where the time goes in v6:
time: 47.1 us; the launch traced here: 47.3 us
  waiting for transfers between devices  20 us (42%)
  starting transfers between devices  13.7 us (29%)
  Pallas kernels  7.48 us (16%)
  local copies, waits for them, and re-layouts  2.83 us (6%)
  other arithmetic  1.88 us (4%)
  between operations  1.36 us (3%)
    ppermute x4, waiting for transfers between devices, butterfly_sum(): x = x + lax.ppermute(x, axis, [(i, i ^ bit) for i in range(n)])  13.9 us
    ppermute x4, starting transfers between devices, butterfly_sum(): x = x + lax.ppermute(x, axis, [(i, i ^ bit) for i in range(n)])  6.7 us
    pallas_call x1, Pallas kernels, local_conv(): pl.pallas_call(make_kernel(blocks, channels, peers, scaling), out_shape=(...  5.53 us
    ppermute x2, starting transfers between devices, from_behind(): return lax.ppermute(block, axis, route)  5.12 us
    ppermute x3, waiting for transfers between devices, spread_in_brick(): lax.ppermute(x, ('split', 'sub'), [(i, i ^ k) for i in range(peers)])  3.7 us
    ppermute x2, waiting for transfers between devices, from_behind(): return lax.ppermute(block, axis, route)  2.41 us
    pallas_call x1, Pallas kernels, pack(): pl.pallas_call(pack_kernel, out_shape=(jax.ShapeDtypeStruct((blocks, chan...  1.95 us
    ppermute x3, starting transfers between devices, spread_in_brick(): lax.ppermute(x, ('split', 'sub'), [(i, i ^ k) for i in range(peers)])  1.92 us
  transfers between devices with their start and end apart: 9, of which 8 were waited for; matrix products, arithmetic and copies ran while one was open for 2% of the time, Pallas kernels for 0%

profile of v6, /device:TPU:0, one launch (start us, length us, event | category | flops | bytes accessed | tf_op | source)
XLA Modules:
  0.0 47.3 jit_solution(3686129415615376105)
XLA Ops:
  0.6 1.9 %shard_map.95 = (bf16[4,32,256]{2,1,0:T(8,128)(2,1)}, bf16[4,32,64]{2,1,0:T(8,128)(2,1)}, bf16[4,32,64]{2,1,0:T(8,128)(2,1)}) custom-call(bf16[4,32,512]{2,1,0:T(8,128)(2,1)} %g_ref.3, bf16[512,384]{1,0:T(8,128)(2,1)} %constant.14.clone.pick_ref), custom_call_target="tpu_custom_call" | custom-call | tf_op jit(solution)/shard_map/pallas_call | solution.py:80
  2.6 3.1 %collective-permute-start = (bf16[4,32,64]{2,1,0:T(8,128)(2,1)}, bf16[4,32,64]{2,1,0:T(8,128)(2,1)S(1)}, u32[]{:S(2)}, u32[]{:S(2)}) collective-permute-start(bf16[4,32,64]{2,1,0:T(8,128)(2,1)} %get-tuple-element.8), channel_id=1, source_target_pairs={{12,0},{0,4},{4,8},{8,12},{13,1},{1,5},{5,9},{9,13},{14,2},{2,6},{... | collective-permute-start | bytes 49160 | tf_op jit(solution)/shard_map/ppermute | solution.py:20
  5.6 2.1 %collective-permute-start.1 = (bf16[4,32,64]{2,1,0:T(8,128)(2,1)}, bf16[4,32,64]{2,1,0:T(8,128)(2,1)S(1)}, u32[]{:S(2)}, u32[]{:S(2)}) collective-permute-start(bf16[4,32,64]{2,1,0:T(8,128)(2,1)} %get-tuple-element.9), channel_id=1, source_target_pairs={{4,0},{8,4},{12,8},{0,12},{5,1},{9,5},{13,9},{1,13},{6,2},{10,6},{... | collective-permute-start | bytes 49160 | tf_op jit(solution)/shard_map/ppermute | solution.py:20
  7.7 2.2 %collective-permute-done = bf16[4,32,64]{2,1,0:T(8,128)(2,1)S(1)} collective-permute-done((bf16[4,32,64]{2,1,0:T(8,128)(2,1)}, bf16[4,32,64]{2,1,0:T(8,128)(2,1)S(1)}, u32[]{:S(2)}, u32[]{:S(2)}) %collective-permute-start) | collective-permute-done | bytes 16416 | tf_op jit(solution)/shard_map/ppermute | solution.py:20
  9.9 0.2 collective-permute-done.1
  10.1 0.9 %pad_maximum_fusion.rest_0_ = bf16[4,32,384]{2,1,0:T(8,128)(2,1)S(1)} fusion(bf16[4,32,64]{2,1,0:T(8,128)(2,1)S(1)} %collective-permute-done.1, bf16[4,32,64]{2,1,0:T(8,128)(2,1)S(1)} %collective-permute-done, bf16[4,32,256]{2,1,0:T(8,128)(2,1)} %get-tuple-element.7), kind=kLoop, calls=%fused_computation | loop fusion | flops 294912 | bytes 196608 | tf_op jit(solution)/shard_map/concatenate | solution.py:217
  11.1 1.6 %collective-permute-start.3 = (bf16[4,32,384]{2,1,0:T(8,128)(2,1)S(1)}, bf16[4,32,384]{2,1,0:T(8,128)(2,1)S(1)}, u32[]{:S(2)}, u32[]{:S(2)}) collective-permute-start(bf16[4,32,384]{2,1,0:T(8,128)(2,1)S(1)} %pad_maximum_fusion.rest_0_), channel_id=1, source_target_pairs={{0,2},{1,3},{2,0},{3,1},{4,6},{5,7},{6,4},{7,5},{8,10},{9,11},{10,... | collective-permute-start | bytes 294920 | tf_op jit(solution)/shard_map/ppermute | solution.py:211
  12.7 0.3 collective-permute-start.2
  13.6 0.1 copy.12
  13.7 0.9 %reshape.14.kmix_ref = bf16[32,864]{1,0:T(8,128)(2,1)} reshape(bf16[32,27,32]{2,1,0:T(8,128)(2,1)S(1)} %copy.12) | data formatting | bytes 110592 | tf_op jit(solution)/shard_map/reshape | solution.py:219
  14.6 1.5 %collective-permute-done.4.rest_3_ = bf16[4,32,384]{2,1,0:T(8,128)(2,1)S(1)} collective-permute-done((bf16[4,32,384]{2,1,0:T(8,128)(2,1)S(1)}, bf16[4,32,384]{2,1,0:T(8,128)(2,1)S(1)}, u32[]{:S(2)}, u32[]{:S(2)}) %collective-permute-start.4) | collective-permute-done | bytes 98336 | tf_op jit(solution)/shard_map/ppermute | solution.py:211
  16.2 2.1 %collective-permute-done.3.rest_2_ = bf16[4,32,384]{2,1,0:T(8,128)(2,1)S(1)} collective-permute-done((bf16[4,32,384]{2,1,0:T(8,128)(2,1)S(1)}, bf16[4,32,384]{2,1,0:T(8,128)(2,1)S(1)}, u32[]{:S(2)}, u32[]{:S(2)}) %collective-permute-start.3) | collective-permute-done | bytes 98336 | tf_op jit(solution)/shard_map/ppermute | solution.py:211
  18.3 0.6 %copy-done.3 = bf16[4,32,384]{2,1,0:T(8,128)(2,1)} copy-done((bf16[4,32,384]{2,1,0:T(8,128)(2,1)}, bf16[4,32,384]{2,1,0:T(8,128)(2,1)S(1)}, u32[]{:S(2)}) %copy-start.3) | copy-done | bytes 98328
  19.0 5.5 %shard_map.96 = (bf16[4,32,512]{2,1,0:T(8,128)(2,1)}, f32[32,864]{1,0:T(8,128)}) custom-call(s32[4,26]{1,0:T(4,128)} %nbr_ref.1, s32[1]{0:T(128)S(6)} %copy.14.cnt_ref, s32[1]{0:T(128)} %bitcast.me_ref, bf16[4,32,512]{2,1,0:T(8,128)(2,1)} %g_ref.3, bf16[4,32,512]{2,1,0:T(8,128)(2,1)} %f_ref.1, bf16[32,864]{1,0:T(8,128)(2,1)} %reshape.14.kmix_ref, ...), custom_call_target="tpu_custom_call" | custom-call | tf_op jit(solution)/shard_map/pallas_call | solution.py:185
  24.6 1.5 %collective-permute-done.5 = f32[32,864]{1,0:T(8,128)S(1)} collective-permute-done((f32[32,864]{1,0:T(8,128)}, f32[32,864]{1,0:T(8,128)S(1)}, u32[]{:S(2)}, u32[]{:S(2)}) %collective-permute-start.5) | collective-permute-done | bytes 110624 | tf_op jit(solution)/shard_map/ppermute | solution.py:31
  26.0 0.9 %add.16 = f32[32,864]{1,0:T(8,128)S(1)} add(f32[32,864]{1,0:T(8,128)} %get-tuple-element.11, f32[32,864]{1,0:T(8,128)S(1)} %collective-permute-done.5) | non-fusion elementwise | flops 27648 | bytes 331776 | tf_op jit(solution)/shard_map/add | solution.py:31
  27.0 3.1 %collective-permute-start.6 = (f32[32,864]{1,0:T(8,128)S(1)}, f32[32,864]{1,0:T(8,128)S(1)}, u32[]{:S(2)}, u32[]{:S(2)}) collective-permute-start(f32[32,864]{1,0:T(8,128)S(1)} %add.16), channel_id=1, source_target_pairs={{0,2},{2,0},{1,3},{3,1},{4,6},{6,4},{5,7},{7,5},{8,10},{10,8},{9,1... | collective-permute-start | bytes 331784 | tf_op jit(solution)/shard_map/ppermute | solution.py:31
  30.1 3.7 %collective-permute-done.6 = f32[32,864]{1,0:T(8,128)S(1)} collective-permute-done((f32[32,864]{1,0:T(8,128)S(1)}, f32[32,864]{1,0:T(8,128)S(1)}, u32[]{:S(2)}, u32[]{:S(2)}) %collective-permute-start.6) | collective-permute-done | bytes 110624 | tf_op jit(solution)/shard_map/ppermute | solution.py:31
  33.8 1.1 %collective-permute-start.7 = (f32[32,864]{1,0:T(8,128)S(1)}, f32[32,864]{1,0:T(8,128)S(1)}, u32[]{:S(2)}, u32[]{:S(2)}) collective-permute-start(f32[32,864]{1,0:T(8,128)S(1)} %add.17), channel_id=1, source_target_pairs={{0,4},{4,0},{8,12},{12,8},{1,5},{5,1},{9,13},{13,9},{2,6},{6,2},{1... | collective-permute-start | bytes 331784 | tf_op jit(solution)/shard_map/ppermute | solution.py:31
  34.8 3.8 %collective-permute-done.7 = f32[32,864]{1,0:T(8,128)S(1)} collective-permute-done((f32[32,864]{1,0:T(8,128)S(1)}, f32[32,864]{1,0:T(8,128)S(1)}, u32[]{:S(2)}, u32[]{:S(2)}) %collective-permute-start.7) | collective-permute-done | bytes 110624 | tf_op jit(solution)/shard_map/ppermute | solution.py:31
  38.7 2.4 %collective-permute-start.8 = (f32[32,864]{1,0:T(8,128)S(1)}, f32[32,864]{1,0:T(8,128)S(1)}, u32[]{:S(2)}, u32[]{:S(2)}) collective-permute-start(f32[32,864]{1,0:T(8,128)S(1)} %add.18), channel_id=1, source_target_pairs={{0,8},{4,12},{8,0},{12,4},{1,9},{5,13},{9,1},{13,5},{2,10},{6,14},... | collective-permute-start | bytes 331784 | tf_op jit(solution)/shard_map/ppermute | solution.py:31
  41.1 5.0 %collective-permute-done.8 = f32[32,864]{1,0:T(8,128)S(1)} collective-permute-done((f32[32,864]{1,0:T(8,128)S(1)}, f32[32,864]{1,0:T(8,128)S(1)}, u32[]{:S(2)}, u32[]{:S(2)}) %collective-permute-start.8) | collective-permute-done | bytes 110624 | tf_op jit(solution)/shard_map/ppermute | solution.py:31
  46.1 0.2 reshape.15
  46.3 1.0 %copy.13 = f32[27,32,32]{2,1,0:T(8,128)} copy(f32[27,32,32]{2,0,1:T(8,128)S(1)} %bitcast.3) | data formatting | bytes 221184
  (15 shorter events, 0.2 us)
Async XLA Ops:
  2.6 11.0 %copy-start.1 = (bf16[27,32,32]{2,1,0:T(8,128)(2,1)S(1)}, bf16[27,32,32]{2,1,0:T(8,128)(2,1)}, u32[]{:S(2)}) copy-start(bf16[27,32,32]{2,1,0:T(8,128)(2,1)} %param.10) | copy-start | bytes 165892
  2.6 7.3 %collective-permute-start = (bf16[4,32,64]{2,1,0:T(8,128)(2,1)}, bf16[4,32,64]{2,1,0:T(8,128)(2,1)S(1)}, u32[]{:S(2)}, u32[]{:S(2)}) collective-permute-start(bf16[4,32,64]{2,1,0:T(8,128)(2,1)} %get-tuple-element.8), channel_id=1, source_target_pairs={{12,0},{0,4},{4,8},{8,12},{13,1},{1,5},{5,9},{9,13},{14,2},{2,6},{... | collective-permute-start | bytes 49160 | tf_op jit(solution)/shard_map/ppermute | solution.py:20
  5.6 4.5 %collective-permute-start.1 = (bf16[4,32,64]{2,1,0:T(8,128)(2,1)}, bf16[4,32,64]{2,1,0:T(8,128)(2,1)S(1)}, u32[]{:S(2)}, u32[]{:S(2)}) collective-permute-start(bf16[4,32,64]{2,1,0:T(8,128)(2,1)} %get-tuple-element.9), channel_id=1, source_target_pairs={{4,0},{8,4},{12,8},{0,12},{5,1},{9,5},{13,9},{1,13},{6,2},{10,6},{... | collective-permute-start | bytes 49160 | tf_op jit(solution)/shard_map/ppermute | solution.py:20
  11.0 2.7 %copy-start = (bf16[4,32,384]{2,1,0:T(8,128)(2,1)}, bf16[4,32,384]{2,1,0:T(8,128)(2,1)S(1)}, u32[]{:S(2)}) copy-start(bf16[4,32,384]{2,1,0:T(8,128)(2,1)S(1)} %pad_maximum_fusion.rest_0_) | copy-start | bytes 294916
  11.0 5.1 %collective-permute-start.4 = (bf16[4,32,384]{2,1,0:T(8,128)(2,1)S(1)}, bf16[4,32,384]{2,1,0:T(8,128)(2,1)S(1)}, u32[]{:S(2)}, u32[]{:S(2)}) collective-permute-start(bf16[4,32,384]{2,1,0:T(8,128)(2,1)S(1)} %pad_maximum_fusion.rest_0_), channel_id=1, source_target_pairs={{0,3},{1,2},{2,1},{3,0},{4,7},{5,6},{6,5},{7,4},{8,11},{9,10},{10,... | collective-permute-start | bytes 294920 | tf_op jit(solution)/shard_map/ppermute | solution.py:211
  11.1 7.2 %collective-permute-start.3 = (bf16[4,32,384]{2,1,0:T(8,128)(2,1)S(1)}, bf16[4,32,384]{2,1,0:T(8,128)(2,1)S(1)}, u32[]{:S(2)}, u32[]{:S(2)}) collective-permute-start(bf16[4,32,384]{2,1,0:T(8,128)(2,1)S(1)} %pad_maximum_fusion.rest_0_), channel_id=1, source_target_pairs={{0,2},{1,3},{2,0},{3,1},{4,6},{5,7},{6,4},{7,5},{8,10},{9,11},{10,... | collective-permute-start | bytes 294920 | tf_op jit(solution)/shard_map/ppermute | solution.py:211
  12.7 5.6 %collective-permute-start.2 = (bf16[4,32,384]{2,1,0:T(8,128)(2,1)S(1)}, bf16[4,32,384]{2,1,0:T(8,128)(2,1)S(1)}, u32[]{:S(2)}, u32[]{:S(2)}) collective-permute-start(bf16[4,32,384]{2,1,0:T(8,128)(2,1)S(1)} %pad_maximum_fusion.rest_0_), channel_id=1, source_target_pairs={{0,1},{1,0},{2,3},{3,2},{4,5},{5,4},{6,7},{7,6},{8,9},{9,8},{10,11... | collective-permute-start | bytes 294920 | tf_op jit(solution)/shard_map/ppermute | solution.py:211
  16.2 2.2 %copy-start.2 = (bf16[4,32,384]{2,1,0:T(8,128)(2,1)}, bf16[4,32,384]{2,1,0:T(8,128)(2,1)S(1)}, u32[]{:S(2)}) copy-start(bf16[4,32,384]{2,1,0:T(8,128)(2,1)S(1)} %collective-permute-done.4.rest_3_) | copy-start | bytes 294916
  18.3 0.6 %copy-start.3 = (bf16[4,32,384]{2,1,0:T(8,128)(2,1)}, bf16[4,32,384]{2,1,0:T(8,128)(2,1)S(1)}, u32[]{:S(2)}) copy-start(bf16[4,32,384]{2,1,0:T(8,128)(2,1)S(1)} %collective-permute-done.3.rest_2_) | copy-start | bytes 294916
  18.3 0.7 %copy-start.4 = (bf16[4,32,384]{2,1,0:T(8,128)(2,1)}, bf16[4,32,384]{2,1,0:T(8,128)(2,1)S(1)}, u32[]{:S(2)}) copy-start(bf16[4,32,384]{2,1,0:T(8,128)(2,1)S(1)} %collective-permute-done.2.rest_1_) | copy-start | bytes 294916
  24.5 1.5 %collective-permute-start.5 = (f32[32,864]{1,0:T(8,128)}, f32[32,864]{1,0:T(8,128)S(1)}, u32[]{:S(2)}, u32[]{:S(2)}) collective-permute-start(f32[32,864]{1,0:T(8,128)} %get-tuple-element.11), channel_id=1, source_target_pairs={{0,1},{1,0},{2,3},{3,2},{4,5},{5,4},{6,7},{7,6},{8,9},{9,8},{10,11... | collective-permute-start | bytes 331784 | tf_op jit(solution)/shard_map/ppermute | solution.py:31
  27.0 6.8 %collective-permute-start.6 = (f32[32,864]{1,0:T(8,128)S(1)}, f32[32,864]{1,0:T(8,128)S(1)}, u32[]{:S(2)}, u32[]{:S(2)}) collective-permute-start(f32[32,864]{1,0:T(8,128)S(1)} %add.16), channel_id=1, source_target_pairs={{0,2},{2,0},{1,3},{3,1},{4,6},{6,4},{5,7},{7,5},{8,10},{10,8},{9,1... | collective-permute-start | bytes 331784 | tf_op jit(solution)/shard_map/ppermute | solution.py:31
  33.8 4.9 %collective-permute-start.7 = (f32[32,864]{1,0:T(8,128)S(1)}, f32[32,864]{1,0:T(8,128)S(1)}, u32[]{:S(2)}, u32[]{:S(2)}) collective-permute-start(f32[32,864]{1,0:T(8,128)S(1)} %add.17), channel_id=1, source_target_pairs={{0,4},{4,0},{8,12},{12,8},{1,5},{5,1},{9,13},{13,9},{2,6},{6,2},{1... | collective-permute-start | bytes 331784 | tf_op jit(solution)/shard_map/ppermute | solution.py:31
  38.7 7.4 %collective-permute-start.8 = (f32[32,864]{1,0:T(8,128)S(1)}, f32[32,864]{1,0:T(8,128)S(1)}, u32[]{:S(2)}, u32[]{:S(2)}) collective-permute-start(f32[32,864]{1,0:T(8,128)S(1)} %add.18), channel_id=1, source_target_pairs={{0,8},{4,12},{8,0},{12,4},{1,9},{5,13},{9,1},{13,5},{2,10},{6,14},... | collective-permute-start | bytes 331784 | tf_op jit(solution)/shard_map/ppermute | solution.py:31

commit v7 on v6

--- a/solution.py
+++ b/solution.py
@@ -20,16 +20,28 @@
     return lax.ppermute(block, axis, route)
 
 
-def butterfly_sum(x, axes):
+def butterfly_sum(x, axes, finish):
+    rounds = []
     for axis in axes:
         n = lax.axis_size(axis)
         if n & (n - 1):
-            x = lax.psum(x, axis)
+            rounds.append((axis, None))
             continue
         bit = 1
         while bit < n:
-            x = x + lax.ppermute(x, axis, [(i, i ^ bit) for i in range(n)])
+            rounds.append((axis, bit))
             bit *= 2
+    for step, (axis, bit) in enumerate(rounds):
+        last = step == len(rounds) - 1
+        if bit is None:
+            x = lax.psum(x, axis)
+            if last:
+                x = finish(x)
+            continue
+        other = lax.ppermute(x, axis, [(i, i ^ bit) for i in range(lax.axis_size(axis))])
+        x = finish(x) + finish(other) if last else x + other
+    if not rounds:
+        x = finish(x)
     return x
 
 
@@ -93,8 +105,9 @@
     slots = blocks * peers
 
     def kernel(nbr_ref, cnt_ref, me_ref, g_ref, f_ref, kmix_ref, place_ref, spread_ref, *rest):
-        shared_refs = rest[:peers]
-        gf_ref, wg_ref, same_ref, lay_ref, stack_ref, acc_ref = rest[peers:]
+        face_refs = rest[:peers]
+        layer_refs = rest[peers:2 * peers]
+        gf_ref, wg_ref, same_ref, lay_ref, stack_ref, acc_ref = rest[2 * peers:]
         lane = lax.broadcasted_iota(jnp.int32, (channels, VOX), 1)
         coord = (lane // 64, (lane // 8) % 8, lane % 8)
 
@@ -108,11 +121,12 @@
         spread = spread_ref[...]
         for k in range(peers):
             first = pl.ds(jnp.bitwise_xor(me_ref[0], k) * blocks, blocks)
-            rows = shared_refs[k][...].reshape(blocks * channels, 384)
-            wide = jnp.dot(rows[:, 0:256], place, preferred_element_type=jnp.float32)
+            rows = face_refs[k][...].reshape(blocks * channels, 256)
+            wide = jnp.dot(rows, place, preferred_element_type=jnp.float32)
             same_ref[first] = wide.astype(jnp.bfloat16).reshape(blocks, channels, VOX)
+            rows = layer_refs[k][...].reshape(blocks * channels, 128)
             for t in range(2):
-                layer = rows[:, 256 + 64 * t:256 + 64 * (t + 1)]
+                layer = rows[:, 64 * t:64 * (t + 1)]
                 wide = jnp.dot(layer, spread, preferred_element_type=jnp.float32)
                 lay_ref[t, first] = wide.astype(jnp.bfloat16).reshape(blocks, channels, VOX)
 
@@ -178,7 +192,7 @@
 
 def local_conv(neighbours, block_count, me, grad_out, features, kmix, place, spread, shared, scaling):
     blocks, channels = grad_out.shape[0], grad_out.shape[1]
-    peers = len(shared)
+    peers = len(shared) // 2
     slots = blocks * peers
     smem = pl.BlockSpec(memory_space=pltpu.SMEM)
     vmem = pl.BlockSpec(memory_space=pltpu.VMEM)
@@ -188,7 +202,7 @@
             jax.ShapeDtypeStruct((blocks, channels, VOX), jnp.bfloat16),
             jax.ShapeDtypeStruct((channels, 27 * channels), jnp.float32),
         ),
-        in_specs=[smem, smem, smem, vmem, vmem, vmem, vmem, vmem] + [vmem] * peers,
+        in_specs=[smem, smem, smem, vmem, vmem, vmem, vmem, vmem] + [vmem] * (2 * peers),
         out_specs=(vmem, vmem),
         scratch_shapes=[
             pltpu.VMEM((slots + 1, channels, VOX), jnp.bfloat16),
@@ -214,7 +228,9 @@
 
     from_below = from_behind(highest, "brick", 1)
     from_above = from_behind(lowest, "brick", -1)
-    shared = spread_in_brick(jnp.concatenate([faces, from_below, from_above], axis=2))
+    shared = spread_in_brick(faces) + spread_in_brick(
+        jnp.concatenate([from_below, from_above], axis=2)
+    )
     me = (lax.axis_index("split") * lax.axis_size("sub") + lax.axis_index("sub")).astype(jnp.int32)
     kmix = jnp.transpose(kernel, (1, 0, 2)).reshape(channels, 27 * channels)
     scaling = 1.0 / math.sqrt(
@@ -224,8 +240,11 @@
         neighbours, block_count, me.reshape(1), grad_out, features, kmix, place, spread,
         shared, scaling,
     )
-    wg = butterfly_sum(wg, ("sub", "split", "brick"))
-    totals = jnp.transpose(wg.reshape(channels, 27, channels), (1, 0, 2))
+    totals = butterfly_sum(
+        wg,
+        ("sub", "split", "brick"),
+        lambda t: jnp.transpose(t.reshape(channels, 27, channels), (1, 0, 2)),
+    )
     return (grad_features, totals)
 
 

time: 47.1 us -> 45.9 us (0.975)
  starting transfers between devices: 13.7 us -> 19.6 us
  waiting for transfers between devices: 20 us -> 14.9 us
  Pallas kernels: 7.48 us -> 5.95 us
  other arithmetic: 1.88 us -> 1.04 us
    ppermute x4, starting transfers between devices: 6.7 us -> 10.5 us  [butterfly_sum(): lax.ppermute(x, axis, [(i, i ^ bit) for i in range(lax.axis_size(axis))])]
    ppermute x4, waiting for transfers between devices: 13.9 us -> 10.9 us  [butterfly_sum(): lax.ppermute(x, axis, [(i, i ^ bit) for i in range(lax.axis_size(axis))])]
    ppermute x3 -> x6, waiting for transfers between devices: 3.7 us -> 1.54 us  [spread_in_brick(): lax.ppermute(x, ('split', 'sub'), [(i, i ^ k) for i in range(peers)])]
    ppermute x3 -> x6, starting transfers between devices: 1.92 us -> 4.05 us  [spread_in_brick(): lax.ppermute(x, ('split', 'sub'), [(i, i ^ k) for i in range(peers)])]
    pallas_call x1, Pallas kernels: 5.53 us -> 3.96 us  [local_conv(): pl.pallas_call(make_kernel(blocks, channels, peers, scaling), out_shape=(...]
    concatenate x1, other arithmetic: 0.92 us -> 0.08 us  [on_device(): jnp.concatenate([from_below, from_above], axis=2)]
    unnamed x11 -> x19, local copies, waits for them, and re-layouts: 1.7 us -> 1.68 us
  transfers between devices with their start and end apart: 9 -> 12, of which waited for: 8 -> 7; matrix products, arithmetic and copies ran while one was open for 2% -> 2% of each run, Pallas kernels for 0% -> 0%
where the time goes in v7:
time: 45.9 us; the launch traced here: 45.8 us
  starting transfers between devices  19.6 us (43%)
  waiting for transfers between devices  14.9 us (32%)
  Pallas kernels  5.95 us (13%)
  local copies, waits for them, and re-layouts  2.82 us (6%)
  between operations  1.43 us (3%)
  other arithmetic  1.04 us (2%)
    ppermute x4, waiting for transfers between devices, butterfly_sum(): lax.ppermute(x, axis, [(i, i ^ bit) for i in range(lax.axis_size(axis))])  10.9 us
    ppermute x4, starting transfers between devices, butterfly_sum(): lax.ppermute(x, axis, [(i, i ^ bit) for i in range(lax.axis_size(axis))])  10.5 us
    ppermute x2, starting transfers between devices, from_behind(): return lax.ppermute(block, axis, route)  5.11 us
    ppermute x6, starting transfers between devices, spread_in_brick(): lax.ppermute(x, ('split', 'sub'), [(i, i ^ k) for i in range(peers)])  4.05 us
    pallas_call x1, Pallas kernels, local_conv(): pl.pallas_call(make_kernel(blocks, channels, peers, scaling), out_shape=(...  3.96 us
    ppermute x2, waiting for transfers between devices, from_behind(): return lax.ppermute(block, axis, route)  2.42 us
    pallas_call x1, Pallas kernels, pack(): pl.pallas_call(pack_kernel, out_shape=(jax.ShapeDtypeStruct((blocks, chan...  1.99 us
    unnamed x19, local copies, waits for them, and re-layouts  1.68 us
  transfers between devices with their start and end apart: 12, of which 7 were waited for; matrix products, arithmetic and copies ran while one was open for 2% of the time, Pallas kernels for 0%

profile of v7, /device:TPU:0, one launch (start us, length us, event | category | flops | bytes accessed | tf_op | source)
XLA Modules:
  0.0 45.8 jit_solution(5089598805843860099)
XLA Ops:
  0.6 2.0 %shard_map.95 = (bf16[4,32,256]{2,1,0:T(8,128)(2,1)}, bf16[4,32,64]{2,1,0:T(8,128)(2,1)}, bf16[4,32,64]{2,1,0:T(8,128)(2,1)}) custom-call(bf16[4,32,512]{2,1,0:T(8,128)(2,1)} %g_ref.3, bf16[512,384]{1,0:T(8,128)(2,1)} %constant.14.clone.pick_ref), custom_call_target="tpu_custom_call" | custom-call | tf_op jit(solution)/shard_map/pallas_call | solution.py:92
  2.6 3.1 %collective-permute-start.3 = (bf16[4,32,64]{2,1,0:T(8,128)(2,1)}, bf16[4,32,64]{2,1,0:T(8,128)(2,1)S(1)}, u32[]{:S(2)}, u32[]{:S(2)}) collective-permute-start(bf16[4,32,64]{2,1,0:T(8,128)(2,1)} %get-tuple-element.8), channel_id=1, source_target_pairs={{12,0},{0,4},{4,8},{8,12},{13,1},{1,5},{5,9},{9,13},{14,2},{2,6},{... | collective-permute-start | bytes 49160 | tf_op jit(solution)/shard_map/ppermute | solution.py:20
  5.7 2.1 %collective-permute-start.4 = (bf16[4,32,64]{2,1,0:T(8,128)(2,1)}, bf16[4,32,64]{2,1,0:T(8,128)(2,1)S(1)}, u32[]{:S(2)}, u32[]{:S(2)}) collective-permute-start(bf16[4,32,64]{2,1,0:T(8,128)(2,1)} %get-tuple-element.9), channel_id=1, source_target_pairs={{4,0},{8,4},{12,8},{0,12},{5,1},{9,5},{13,9},{1,13},{6,2},{10,6},{... | collective-permute-start | bytes 49160 | tf_op jit(solution)/shard_map/ppermute | solution.py:20
  7.7 2.2 %collective-permute-done.3 = bf16[4,32,64]{2,1,0:T(8,128)(2,1)S(1)} collective-permute-done((bf16[4,32,64]{2,1,0:T(8,128)(2,1)}, bf16[4,32,64]{2,1,0:T(8,128)(2,1)S(1)}, u32[]{:S(2)}, u32[]{:S(2)}) %collective-permute-start.3) | collective-permute-done | bytes 16416 | tf_op jit(solution)/shard_map/ppermute | solution.py:20
  9.9 0.2 collective-permute-done.4
  10.4 1.7 %collective-permute-start.2 = (bf16[4,32,256]{2,1,0:T(8,128)(2,1)S(1)}, bf16[4,32,256]{2,1,0:T(8,128)(2,1)S(1)}, u32[]{:S(2)}, u32[]{:S(2)}) collective-permute-start(bf16[4,32,256]{2,1,0:T(8,128)(2,1)S(1)} %copy-done.2), channel_id=1, source_target_pairs={{0,3},{1,2},{2,1},{3,0},{4,7},{5,6},{6,5},{7,4},{8,11},{9,10},{10,... | collective-permute-start | bytes 196616 | tf_op jit(solution)/shard_map/ppermute | solution.py:225
  12.1 1.5 %collective-permute-start.1 = (bf16[4,32,256]{2,1,0:T(8,128)(2,1)S(1)}, bf16[4,32,256]{2,1,0:T(8,128)(2,1)S(1)}, u32[]{:S(2)}, u32[]{:S(2)}) collective-permute-start(bf16[4,32,256]{2,1,0:T(8,128)(2,1)S(1)} %copy-done.2), channel_id=1, source_target_pairs={{0,2},{1,3},{2,0},{3,1},{4,6},{5,7},{6,4},{7,5},{8,10},{9,11},{10,... | collective-permute-start | bytes 196616 | tf_op jit(solution)/shard_map/ppermute | solution.py:225
  13.6 0.5 %collective-permute-start.6 = (bf16[4,32,128]{2,1,0:T(8,128)(2,1)S(1)}, bf16[4,32,128]{2,1,0:T(8,128)(2,1)S(1)}, u32[]{:S(2)}, u32[]{:S(2)}) collective-permute-start(bf16[4,32,128]{2,1,0:T(8,128)(2,1)S(1)} %pad_maximum_fusion.rest_4_), channel_id=1, source_target_pairs={{0,2},{1,3},{2,0},{3,1},{4,6},{5,7},{6,4},{7,5},{8,10},{9,11},{10,... | collective-permute-start | bytes 98312 | tf_op jit(solution)/shard_map/ppermute | solution.py:225
  14.1 0.2 collective-permute-start.5
  15.0 0.1 copy.12
  15.1 0.9 %reshape.14.kmix_ref = bf16[32,864]{1,0:T(8,128)(2,1)} reshape(bf16[32,27,32]{2,1,0:T(8,128)(2,1)S(1)} %copy.12) | data formatting | bytes 110592 | tf_op jit(solution)/shard_map/reshape | solution.py:235
  16.0 1.5 %collective-permute-done.6.rest_6_ = bf16[4,32,128]{2,1,0:T(8,128)(2,1)S(1)} collective-permute-done((bf16[4,32,128]{2,1,0:T(8,128)(2,1)S(1)}, bf16[4,32,128]{2,1,0:T(8,128)(2,1)S(1)}, u32[]{:S(2)}, u32[]{:S(2)}) %collective-permute-start.6) | collective-permute-done | bytes 32800 | tf_op jit(solution)/shard_map/ppermute | solution.py:225
  17.6 0.5 %copy-done.7 = bf16[4,32,128]{2,1,0:T(8,128)(2,1)} copy-done((bf16[4,32,128]{2,1,0:T(8,128)(2,1)}, bf16[4,32,128]{2,1,0:T(8,128)(2,1)S(1)}, u32[]{:S(2)}) %copy-start.7) | copy-done | bytes 32792
  18.2 4.0 %shard_map.96 = (bf16[4,32,512]{2,1,0:T(8,128)(2,1)}, f32[32,864]{1,0:T(8,128)}) custom-call(s32[4,26]{1,0:T(4,128)} %nbr_ref.1, s32[1]{0:T(128)S(6)} %copy.14.cnt_ref, s32[1]{0:T(128)} %bitcast.me_ref, bf16[4,32,512]{2,1,0:T(8,128)(2,1)} %g_ref.3, bf16[4,32,512]{2,1,0:T(8,128)(2,1)} %f_ref.1, bf16[32,864]{1,0:T(8,128)(2,1)} %reshape.14.kmix_ref, ...), custom_call_target="tpu_custom_call" | custom-call | tf_op jit(solution)/shard_map/pallas_call | solution.py:199
  22.2 1.5 %collective-permute-done.8 = f32[32,864]{1,0:T(8,128)S(1)} collective-permute-done((f32[32,864]{1,0:T(8,128)}, f32[32,864]{1,0:T(8,128)S(1)}, u32[]{:S(2)}, u32[]{:S(2)}) %collective-permute-start.8) | collective-permute-done | bytes 110624 | tf_op jit(solution)/shard_map/ppermute | solution.py:41
  23.7 0.9 %add.22 = f32[32,864]{1,0:T(8,128)S(1)} add(f32[32,864]{1,0:T(8,128)} %get-tuple-element.11, f32[32,864]{1,0:T(8,128)S(1)} %collective-permute-done.8) | non-fusion elementwise | flops 27648 | bytes 331776 | tf_op jit(solution)/shard_map/add | solution.py:42
  24.6 5.7 %collective-permute-start.9 = (f32[32,864]{1,0:T(8,128)S(1)}, f32[32,864]{1,0:T(8,128)S(1)}, u32[]{:S(2)}, u32[]{:S(2)}) collective-permute-start(f32[32,864]{1,0:T(8,128)S(1)} %add.22), channel_id=1, source_target_pairs={{0,2},{2,0},{1,3},{3,1},{4,6},{6,4},{5,7},{7,5},{8,10},{10,8},{9,1... | collective-permute-start | bytes 331784 | tf_op jit(solution)/shard_map/ppermute | solution.py:41
  30.4 3.5 %collective-permute-done.9 = f32[32,864]{1,0:T(8,128)S(1)} collective-permute-done((f32[32,864]{1,0:T(8,128)S(1)}, f32[32,864]{1,0:T(8,128)S(1)}, u32[]{:S(2)}, u32[]{:S(2)}) %collective-permute-start.9) | collective-permute-done | bytes 110624 | tf_op jit(solution)/shard_map/ppermute | solution.py:41
  33.8 1.9 %collective-permute-start.10 = (f32[32,864]{1,0:T(8,128)S(1)}, f32[32,864]{1,0:T(8,128)S(1)}, u32[]{:S(2)}, u32[]{:S(2)}) collective-permute-start(f32[32,864]{1,0:T(8,128)S(1)} %add.23), channel_id=1, source_target_pairs={{0,4},{4,0},{8,12},{12,8},{1,5},{5,1},{9,13},{13,9},{2,6},{6,2},{1... | collective-permute-start | bytes 331784 | tf_op jit(solution)/shard_map/ppermute | solution.py:41
  35.7 3.0 %collective-permute-done.10 = f32[32,864]{1,0:T(8,128)S(1)} collective-permute-done((f32[32,864]{1,0:T(8,128)S(1)}, f32[32,864]{1,0:T(8,128)S(1)}, u32[]{:S(2)}, u32[]{:S(2)}) %collective-permute-start.10) | collective-permute-done | bytes 110624 | tf_op jit(solution)/shard_map/ppermute | solution.py:41
  38.7 2.9 %collective-permute-start.11 = (f32[32,864]{1,0:T(8,128)S(1)}, f32[32,864]{1,0:T(8,128)S(1)}, u32[]{:S(2)}, u32[]{:S(2)}) collective-permute-start(f32[32,864]{1,0:T(8,128)S(1)} %add.24), channel_id=1, source_target_pairs={{0,8},{4,12},{8,0},{12,4},{1,9},{5,13},{9,1},{13,5},{2,10},{6,14},... | collective-permute-start | bytes 331784 | tf_op jit(solution)/shard_map/ppermute | solution.py:41
  41.6 3.0 %collective-permute-done.11 = f32[32,864]{1,0:T(8,128)S(1)} collective-permute-done((f32[32,864]{1,0:T(8,128)S(1)}, f32[32,864]{1,0:T(8,128)S(1)}, u32[]{:S(2)}, u32[]{:S(2)}) %collective-permute-start.11) | collective-permute-done | bytes 110624 | tf_op jit(solution)/shard_map/ppermute | solution.py:41
  44.5 0.2 add.26
  44.7 1.0 %copy.13 = f32[27,32,32]{2,1,0:T(8,128)} copy(f32[27,32,32]{2,0,1:T(8,128)S(1)} %bitcast.3) | data formatting | bytes 221184
  (29 shorter events, 0.3 us)
Async XLA Ops:
  0.6 14.4 %copy-start = (bf16[27,32,32]{2,1,0:T(8,128)(2,1)S(1)}, bf16[27,32,32]{2,1,0:T(8,128)(2,1)}, u32[]{:S(2)}) copy-start(bf16[27,32,32]{2,1,0:T(8,128)(2,1)} %param.10) | copy-start | bytes 165892
  2.6 7.7 %copy-start.2 = (bf16[4,32,256]{2,1,0:T(8,128)(2,1)S(1)}, bf16[4,32,256]{2,1,0:T(8,128)(2,1)}, u32[]{:S(2)}) copy-start(bf16[4,32,256]{2,1,0:T(8,128)(2,1)} %get-tuple-element.7.rest_0_) | copy-start | bytes 196612
  2.6 7.3 %collective-permute-start.3 = (bf16[4,32,64]{2,1,0:T(8,128)(2,1)}, bf16[4,32,64]{2,1,0:T(8,128)(2,1)S(1)}, u32[]{:S(2)}, u32[]{:S(2)}) collective-permute-start(bf16[4,32,64]{2,1,0:T(8,128)(2,1)} %get-tuple-element.8), channel_id=1, source_target_pairs={{12,0},{0,4},{4,8},{8,12},{13,1},{1,5},{5,9},{9,13},{14,2},{2,6},{... | collective-permute-start | bytes 49160 | tf_op jit(solution)/shard_map/ppermute | solution.py:20
  5.7 4.5 %collective-permute-start.4 = (bf16[4,32,64]{2,1,0:T(8,128)(2,1)}, bf16[4,32,64]{2,1,0:T(8,128)(2,1)S(1)}, u32[]{:S(2)}, u32[]{:S(2)}) collective-permute-start(bf16[4,32,64]{2,1,0:T(8,128)(2,1)} %get-tuple-element.9), channel_id=1, source_target_pairs={{4,0},{8,4},{12,8},{0,12},{5,1},{9,5},{13,9},{1,13},{6,2},{10,6},{... | collective-permute-start | bytes 49160 | tf_op jit(solution)/shard_map/ppermute | solution.py:20
  10.3 4.9 %copy-start.1 = (bf16[4,32,128]{2,1,0:T(8,128)(2,1)}, bf16[4,32,128]{2,1,0:T(8,128)(2,1)S(1)}, u32[]{:S(2)}) copy-start(bf16[4,32,128]{2,1,0:T(8,128)(2,1)S(1)} %pad_maximum_fusion.rest_4_) | copy-start | bytes 98308
  10.3 3.8 %collective-permute-start.7 = (bf16[4,32,128]{2,1,0:T(8,128)(2,1)S(1)}, bf16[4,32,128]{2,1,0:T(8,128)(2,1)S(1)}, u32[]{:S(2)}, u32[]{:S(2)}) collective-permute-start(bf16[4,32,128]{2,1,0:T(8,128)(2,1)S(1)} %pad_maximum_fusion.rest_4_), channel_id=1, source_target_pairs={{0,3},{1,2},{2,1},{3,0},{4,7},{5,6},{6,5},{7,4},{8,11},{9,10},{10,... | collective-permute-start | bytes 98312 | tf_op jit(solution)/shard_map/ppermute | solution.py:225
  10.4 7.2 %collective-permute-start.2 = (bf16[4,32,256]{2,1,0:T(8,128)(2,1)S(1)}, bf16[4,32,256]{2,1,0:T(8,128)(2,1)S(1)}, u32[]{:S(2)}, u32[]{:S(2)}) collective-permute-start(bf16[4,32,256]{2,1,0:T(8,128)(2,1)S(1)} %copy-done.2), channel_id=1, source_target_pairs={{0,3},{1,2},{2,1},{3,0},{4,7},{5,6},{6,5},{7,4},{8,11},{9,10},{10,... | collective-permute-start | bytes 196616 | tf_op jit(solution)/shard_map/ppermute | solution.py:225
  12.1 5.5 %collective-permute-start.1 = (bf16[4,32,256]{2,1,0:T(8,128)(2,1)S(1)}, bf16[4,32,256]{2,1,0:T(8,128)(2,1)S(1)}, u32[]{:S(2)}, u32[]{:S(2)}) collective-permute-start(bf16[4,32,256]{2,1,0:T(8,128)(2,1)S(1)} %copy-done.2), channel_id=1, source_target_pairs={{0,2},{1,3},{2,0},{3,1},{4,6},{5,7},{6,4},{7,5},{8,10},{9,11},{10,... | collective-permute-start | bytes 196616 | tf_op jit(solution)/shard_map/ppermute | solution.py:225
  13.6 4.0 %collective-permute-start = (bf16[4,32,256]{2,1,0:T(8,128)(2,1)S(1)}, bf16[4,32,256]{2,1,0:T(8,128)(2,1)S(1)}, u32[]{:S(2)}, u32[]{:S(2)}) collective-permute-start(bf16[4,32,256]{2,1,0:T(8,128)(2,1)S(1)} %copy-done.2), channel_id=1, source_target_pairs={{0,1},{1,0},{2,3},{3,2},{4,5},{5,4},{6,7},{7,6},{8,9},{9,8},{10,11... | collective-permute-start | bytes 196616 | tf_op jit(solution)/shard_map/ppermute | solution.py:225
  13.6 4.0 %collective-permute-start.6 = (bf16[4,32,128]{2,1,0:T(8,128)(2,1)S(1)}, bf16[4,32,128]{2,1,0:T(8,128)(2,1)S(1)}, u32[]{:S(2)}, u32[]{:S(2)}) collective-permute-start(bf16[4,32,128]{2,1,0:T(8,128)(2,1)S(1)} %pad_maximum_fusion.rest_4_), channel_id=1, source_target_pairs={{0,2},{1,3},{2,0},{3,1},{4,6},{5,7},{6,4},{7,5},{8,10},{9,11},{10,... | collective-permute-start | bytes 98312 | tf_op jit(solution)/shard_map/ppermute | solution.py:225
  14.1 1.0 %copy-start.6 = (bf16[4,32,128]{2,1,0:T(8,128)(2,1)}, bf16[4,32,128]{2,1,0:T(8,128)(2,1)S(1)}, u32[]{:S(2)}) copy-start(bf16[4,32,128]{2,1,0:T(8,128)(2,1)S(1)} %collective-permute-done.7.rest_7_) | copy-start | bytes 98308
  14.1 3.4 %collective-permute-start.5 = (bf16[4,32,128]{2,1,0:T(8,128)(2,1)S(1)}, bf16[4,32,128]{2,1,0:T(8,128)(2,1)S(1)}, u32[]{:S(2)}, u32[]{:S(2)}) collective-permute-start(bf16[4,32,128]{2,1,0:T(8,128)(2,1)S(1)} %pad_maximum_fusion.rest_4_), channel_id=1, source_target_pairs={{0,1},{1,0},{2,3},{3,2},{4,5},{5,4},{6,7},{7,6},{8,9},{9,8},{10,11... | collective-permute-start | bytes 98312 | tf_op jit(solution)/shard_map/ppermute | solution.py:225
  17.5 0.6 %copy-start.7 = (bf16[4,32,128]{2,1,0:T(8,128)(2,1)}, bf16[4,32,128]{2,1,0:T(8,128)(2,1)S(1)}, u32[]{:S(2)}) copy-start(bf16[4,32,128]{2,1,0:T(8,128)(2,1)S(1)} %collective-permute-done.6.rest_6_) | copy-start | bytes 98308
  17.5 0.6 %copy-start.8 = (bf16[4,32,128]{2,1,0:T(8,128)(2,1)}, bf16[4,32,128]{2,1,0:T(8,128)(2,1)S(1)}, u32[]{:S(2)}) copy-start(bf16[4,32,128]{2,1,0:T(8,128)(2,1)S(1)} %collective-permute-done.5.rest_5_) | copy-start | bytes 98308
  17.5 0.6 %copy-start.3 = (bf16[4,32,256]{2,1,0:T(8,128)(2,1)}, bf16[4,32,256]{2,1,0:T(8,128)(2,1)S(1)}, u32[]{:S(2)}) copy-start(bf16[4,32,256]{2,1,0:T(8,128)(2,1)S(1)} %collective-permute-done.2.rest_3_) | copy-start | bytes 196612
  17.6 0.7 %copy-start.4 = (bf16[4,32,256]{2,1,0:T(8,128)(2,1)}, bf16[4,32,256]{2,1,0:T(8,128)(2,1)S(1)}, u32[]{:S(2)}) copy-start(bf16[4,32,256]{2,1,0:T(8,128)(2,1)S(1)} %collective-permute-done.1.rest_2_) | copy-start | bytes 196612
  17.6 0.6 %copy-start.5 = (bf16[4,32,256]{2,1,0:T(8,128)(2,1)}, bf16[4,32,256]{2,1,0:T(8,128)(2,1)S(1)}, u32[]{:S(2)}) copy-start(bf16[4,32,256]{2,1,0:T(8,128)(2,1)S(1)} %collective-permute-done.rest_1_) | copy-start | bytes 196612
  22.2 1.5 %collective-permute-start.8 = (f32[32,864]{1,0:T(8,128)}, f32[32,864]{1,0:T(8,128)S(1)}, u32[]{:S(2)}, u32[]{:S(2)}) collective-permute-start(f32[32,864]{1,0:T(8,128)} %get-tuple-element.11), channel_id=1, source_target_pairs={{0,1},{1,0},{2,3},{3,2},{4,5},{5,4},{6,7},{7,6},{8,9},{9,8},{10,11... | collective-permute-start | bytes 331784 | tf_op jit(solution)/shard_map/ppermute | solution.py:41
  24.6 9.2 %collective-permute-start.9 = (f32[32,864]{1,0:T(8,128)S(1)}, f32[32,864]{1,0:T(8,128)S(1)}, u32[]{:S(2)}, u32[]{:S(2)}) collective-permute-start(f32[32,864]{1,0:T(8,128)S(1)} %add.22), channel_id=1, source_target_pairs={{0,2},{2,0},{1,3},{3,1},{4,6},{6,4},{5,7},{7,5},{8,10},{10,8},{9,1... | collective-permute-start | bytes 331784 | tf_op jit(solution)/shard_map/ppermute | solution.py:41
  33.8 4.9 %collective-permute-start.10 = (f32[32,864]{1,0:T(8,128)S(1)}, f32[32,864]{1,0:T(8,128)S(1)}, u32[]{:S(2)}, u32[]{:S(2)}) collective-permute-start(f32[32,864]{1,0:T(8,128)S(1)} %add.23), channel_id=1, source_target_pairs={{0,4},{4,0},{8,12},{12,8},{1,5},{5,1},{9,13},{13,9},{2,6},{6,2},{1... | collective-permute-start | bytes 331784 | tf_op jit(solution)/shard_map/ppermute | solution.py:41
  38.7 5.8 %collective-permute-start.11 = (f32[32,864]{1,0:T(8,128)S(1)}, f32[32,864]{1,0:T(8,128)S(1)}, u32[]{:S(2)}, u32[]{:S(2)}) collective-permute-start(f32[32,864]{1,0:T(8,128)S(1)} %add.24), channel_id=1, source_target_pairs={{0,8},{4,12},{8,0},{12,4},{1,9},{5,13},{9,1},{13,5},{2,10},{6,14},... | collective-permute-start | bytes 331784 | tf_op jit(solution)/shard_map/ppermute | solution.py:41

commit v8 on v7

--- a/solution.py
+++ b/solution.py
@@ -108,11 +108,8 @@
         face_refs = rest[:peers]
         layer_refs = rest[peers:2 * peers]
         gf_ref, wg_ref, same_ref, lay_ref, stack_ref, acc_ref = rest[2 * peers:]
-        lane = lax.broadcasted_iota(jnp.int32, (channels, VOX), 1)
-        coord = (lane // 64, (lane // 8) % 8, lane % 8)
-
-        def boundary(axis, sign):
-            return coord[axis] == (7 if sign < 0 else 0)
+        lane = lax.broadcasted_iota(jnp.int32, (channels, 128), 1)
+        half, ycoord, zcoord = lane // 64, (lane // 8) % 8, lane % 8
 
         same_ref[slots] = jnp.zeros((channels, VOX), jnp.bfloat16)
         lay_ref[0, slots] = jnp.zeros((channels, VOX), jnp.bfloat16)
@@ -134,48 +131,56 @@
         acc_ref[...] = jnp.zeros_like(acc_ref)
 
         def body(s, carry):
-            own = g_ref[s]
-
-            def neighbour(e):
+            def own(k):
+                return g_ref[s, :, 128 * k:128 * (k + 1)]
+
+            def neighbour(e, k):
                 q = jnp.minimum(nbr_ref[s, NEIGHBOURS.index(e)], slots)
                 if e[2] == 0:
-                    return same_ref[q]
-                return lay_ref[0 if e[2] < 0 else 1, q]
+                    return same_ref[q, :, 128 * k:128 * (k + 1)]
+                return lay_ref[0 if e[2] < 0 else 1, q, :, 128 * k:128 * (k + 1)]
 
             for a in (-1, 0, 1):
+                kx = 3 if a > 0 else 0
+                mx = half == (1 if a > 0 else 0)
                 for b in (-1, 0, 1):
-                    rx = boundary(0, -a) if a != 0 else None
-                    ry = boundary(1, -b) if b != 0 else None
-                    flat = own
-                    if a != 0:
-                        flat = jnp.where(rx, neighbour((-a, 0, 0)), flat)
-                    if b != 0:
-                        flat = jnp.where(ry, neighbour((0, -b, 0)), flat)
-                    if a != 0 and b != 0:
-                        flat = jnp.where(rx & ry, neighbour((-a, -b, 0)), flat)
+                    my = ycoord == (7 if b > 0 else 0)
+                    flat = []
+                    for k in range(4):
+                        f = own(k)
+                        if a != 0 and k == kx:
+                            f = jnp.where(mx, neighbour((-a, 0, 0), k), f)
+                        if b != 0:
+                            f = jnp.where(my, neighbour((0, -b, 0), k), f)
+                        if a != 0 and b != 0 and k == kx:
+                            f = jnp.where(mx & my, neighbour((-a, -b, 0), k), f)
+                        flat.append(f)
                     for c in (-1, 0, 1):
-                        z = flat
-                        if c != 0:
-                            y = neighbour((0, 0, -c))
-                            if a != 0:
-                                y = jnp.where(rx, neighbour((-a, 0, -c)), y)
+                        chunks = []
+                        for k in range(4):
+                            z = flat[k]
+                            if c != 0:
+                                y = neighbour((0, 0, -c), k)
+                                if a != 0 and k == kx:
+                                    y = jnp.where(mx, neighbour((-a, 0, -c), k), y)
+                                if b != 0:
+                                    y = jnp.where(my, neighbour((0, -b, -c), k), y)
+                                if a != 0 and b != 0 and k == kx:
+                                    y = jnp.where(mx & my, neighbour((-a, -b, -c), k), y)
+                                z = jnp.where(zcoord == (0 if c > 0 else 7), y,
+                                              pltpu.roll(z, c % 128, 1))
                             if b != 0:
-                                y = jnp.where(ry, neighbour((0, -b, -c)), y)
-                            if a != 0 and b != 0:
-                                y = jnp.where(rx & ry, neighbour((-a, -b, -c)), y)
-                            z = jnp.where(boundary(2, -c), y, flat)
-                        if c != 0:
-                            z = jnp.where(coord[2] == (0 if c > 0 else 7),
-                                          pltpu.roll(z, (-7 * c) % VOX, 1),
-                                          pltpu.roll(z, c % VOX, 1))
-                        if b != 0:
-                            z = jnp.where(coord[1] == (0 if b > 0 else 7),
-                                          pltpu.roll(z, (-56 * b) % VOX, 1),
-                                          pltpu.roll(z, (8 * b) % VOX, 1))
+                                z = jnp.where(ycoord == (0 if b > 0 else 7),
+                                              pltpu.roll(z, (-56 * b) % 128, 1),
+                                              pltpu.roll(z, (8 * b) % 128, 1))
+                            chunks.append(z)
                         if a != 0:
-                            z = pltpu.roll(z, (64 * a) % VOX, 1)
+                            turned = [pltpu.roll(z, 64, 1) for z in chunks]
+                            keep = half == (1 if a > 0 else 0)
+                            chunks = [jnp.where(keep, turned[k], turned[(k - a) % 4]) for k in range(4)]
                         di = 9 * (a + 1) + 3 * (b + 1) + (c + 1)
-                        stack_ref[di * channels:(di + 1) * channels, :] = z
+                        for k in range(4):
+                            stack_ref[di * channels:(di + 1) * channels, 128 * k:128 * (k + 1)] = chunks[k]
             st = stack_ref[...]
             gf = jnp.dot(kmix_ref[...], st, preferred_element_type=jnp.float32)
             gf_ref[s] = gf.astype(jnp.bfloat16)

time: 45.9 us -> 46.1 us (level)
  waiting for transfers between devices: 14.9 us -> 19.8 us
  starting transfers between devices: 19.6 us -> 15.3 us
    ppermute x4, waiting for transfers between devices: 10.9 us -> 15.8 us  [butterfly_sum(): lax.ppermute(x, axis, [(i, i ^ bit) for i in range(lax.axis_size(axis))])]
    ppermute x4, starting transfers between devices: 10.5 us -> 6.12 us  [butterfly_sum(): lax.ppermute(x, axis, [(i, i ^ bit) for i in range(lax.axis_size(axis))])]
where the time goes in v8:
time: 46.1 us; the launch traced here: 46 us
  waiting for transfers between devices  19.8 us (43%)
  starting transfers between devices  15.3 us (33%)
  Pallas kernels  5.67 us (12%)
  local copies, waits for them, and re-layouts  2.82 us (6%)
  between operations  1.43 us (3%)
  other arithmetic  1.04 us (2%)
    ppermute x4, waiting for transfers between devices, butterfly_sum(): lax.ppermute(x, axis, [(i, i ^ bit) for i in range(lax.axis_size(axis))])  15.8 us
    ppermute x4, starting transfers between devices, butterfly_sum(): lax.ppermute(x, axis, [(i, i ^ bit) for i in range(lax.axis_size(axis))])  6.12 us
    ppermute x2, starting transfers between devices, from_behind(): return lax.ppermute(block, axis, route)  5.11 us
    ppermute x6, starting transfers between devices, spread_in_brick(): lax.ppermute(x, ('split', 'sub'), [(i, i ^ k) for i in range(peers)])  4.05 us
    pallas_call x1, Pallas kernels, local_conv(): pl.pallas_call(make_kernel(blocks, channels, peers, scaling), out_shape=(...  3.68 us
    ppermute x2, waiting for transfers between devices, from_behind(): return lax.ppermute(block, axis, route)  2.42 us
    pallas_call x1, Pallas kernels, pack(): pl.pallas_call(pack_kernel, out_shape=(jax.ShapeDtypeStruct((blocks, chan...  1.99 us
    unnamed x19, local copies, waits for them, and re-layouts  1.68 us
  transfers between devices with their start and end apart: 12, of which 7 were waited for; matrix products, arithmetic and copies ran while one was open for 2% of the time, Pallas kernels for 0%

profile of v8, /device:TPU:0, one launch (start us, length us, event | category | flops | bytes accessed | tf_op | source)
XLA Modules:
  0.0 46.0 jit_solution(10404711645110421201)
XLA Ops:
  0.6 2.0 %shard_map.95 = (bf16[4,32,256]{2,1,0:T(8,128)(2,1)}, bf16[4,32,64]{2,1,0:T(8,128)(2,1)}, bf16[4,32,64]{2,1,0:T(8,128)(2,1)}) custom-call(bf16[4,32,512]{2,1,0:T(8,128)(2,1)} %g_ref.3, bf16[512,384]{1,0:T(8,128)(2,1)} %constant.14.clone.pick_ref), custom_call_target="tpu_custom_call" | custom-call | tf_op jit(solution)/shard_map/pallas_call | solution.py:92
  2.6 3.1 %collective-permute-start.3 = (bf16[4,32,64]{2,1,0:T(8,128)(2,1)}, bf16[4,32,64]{2,1,0:T(8,128)(2,1)S(1)}, u32[]{:S(2)}, u32[]{:S(2)}) collective-permute-start(bf16[4,32,64]{2,1,0:T(8,128)(2,1)} %get-tuple-element.8), channel_id=1, source_target_pairs={{12,0},{0,4},{4,8},{8,12},{13,1},{1,5},{5,9},{9,13},{14,2},{2,6},{... | collective-permute-start | bytes 49160 | tf_op jit(solution)/shard_map/ppermute | solution.py:20
  5.7 2.1 %collective-permute-start.4 = (bf16[4,32,64]{2,1,0:T(8,128)(2,1)}, bf16[4,32,64]{2,1,0:T(8,128)(2,1)S(1)}, u32[]{:S(2)}, u32[]{:S(2)}) collective-permute-start(bf16[4,32,64]{2,1,0:T(8,128)(2,1)} %get-tuple-element.9), channel_id=1, source_target_pairs={{4,0},{8,4},{12,8},{0,12},{5,1},{9,5},{13,9},{1,13},{6,2},{10,6},{... | collective-permute-start | bytes 49160 | tf_op jit(solution)/shard_map/ppermute | solution.py:20
  7.7 2.2 %collective-permute-done.3 = bf16[4,32,64]{2,1,0:T(8,128)(2,1)S(1)} collective-permute-done((bf16[4,32,64]{2,1,0:T(8,128)(2,1)}, bf16[4,32,64]{2,1,0:T(8,128)(2,1)S(1)}, u32[]{:S(2)}, u32[]{:S(2)}) %collective-permute-start.3) | collective-permute-done | bytes 16416 | tf_op jit(solution)/shard_map/ppermute | solution.py:20
  9.9 0.2 collective-permute-done.4
  10.4 1.7 %collective-permute-start.2 = (bf16[4,32,256]{2,1,0:T(8,128)(2,1)S(1)}, bf16[4,32,256]{2,1,0:T(8,128)(2,1)S(1)}, u32[]{:S(2)}, u32[]{:S(2)}) collective-permute-start(bf16[4,32,256]{2,1,0:T(8,128)(2,1)S(1)} %copy-done.2), channel_id=1, source_target_pairs={{0,3},{1,2},{2,1},{3,0},{4,7},{5,6},{6,5},{7,4},{8,11},{9,10},{10,... | collective-permute-start | bytes 196616 | tf_op jit(solution)/shard_map/ppermute | solution.py:230
  12.1 1.5 %collective-permute-start.1 = (bf16[4,32,256]{2,1,0:T(8,128)(2,1)S(1)}, bf16[4,32,256]{2,1,0:T(8,128)(2,1)S(1)}, u32[]{:S(2)}, u32[]{:S(2)}) collective-permute-start(bf16[4,32,256]{2,1,0:T(8,128)(2,1)S(1)} %copy-done.2), channel_id=1, source_target_pairs={{0,2},{1,3},{2,0},{3,1},{4,6},{5,7},{6,4},{7,5},{8,10},{9,11},{10,... | collective-permute-start | bytes 196616 | tf_op jit(solution)/shard_map/ppermute | solution.py:230
  13.6 0.5 %collective-permute-start.6 = (bf16[4,32,128]{2,1,0:T(8,128)(2,1)S(1)}, bf16[4,32,128]{2,1,0:T(8,128)(2,1)S(1)}, u32[]{:S(2)}, u32[]{:S(2)}) collective-permute-start(bf16[4,32,128]{2,1,0:T(8,128)(2,1)S(1)} %pad_maximum_fusion.rest_4_), channel_id=1, source_target_pairs={{0,2},{1,3},{2,0},{3,1},{4,6},{5,7},{6,4},{7,5},{8,10},{9,11},{10,... | collective-permute-start | bytes 98312 | tf_op jit(solution)/shard_map/ppermute | solution.py:230
  14.1 0.2 collective-permute-start.5
  15.0 0.1 copy.12
  15.1 0.9 %reshape.14.kmix_ref = bf16[32,864]{1,0:T(8,128)(2,1)} reshape(bf16[32,27,32]{2,1,0:T(8,128)(2,1)S(1)} %copy.12) | data formatting | bytes 110592 | tf_op jit(solution)/shard_map/reshape | solution.py:240
  16.0 1.5 %collective-permute-done.6.rest_6_ = bf16[4,32,128]{2,1,0:T(8,128)(2,1)S(1)} collective-permute-done((bf16[4,32,128]{2,1,0:T(8,128)(2,1)S(1)}, bf16[4,32,128]{2,1,0:T(8,128)(2,1)S(1)}, u32[]{:S(2)}, u32[]{:S(2)}) %collective-permute-start.6) | collective-permute-done | bytes 32800 | tf_op jit(solution)/shard_map/ppermute | solution.py:230
  17.6 0.5 %copy-done.7 = bf16[4,32,128]{2,1,0:T(8,128)(2,1)} copy-done((bf16[4,32,128]{2,1,0:T(8,128)(2,1)}, bf16[4,32,128]{2,1,0:T(8,128)(2,1)S(1)}, u32[]{:S(2)}) %copy-start.7) | copy-done | bytes 32792
  18.2 3.7 %shard_map.96 = (bf16[4,32,512]{2,1,0:T(8,128)(2,1)}, f32[32,864]{1,0:T(8,128)}) custom-call(s32[4,26]{1,0:T(4,128)} %nbr_ref.1, s32[1]{0:T(128)S(6)} %copy.14.cnt_ref, s32[1]{0:T(128)} %bitcast.me_ref, bf16[4,32,512]{2,1,0:T(8,128)(2,1)} %g_ref.3, bf16[4,32,512]{2,1,0:T(8,128)(2,1)} %f_ref.1, bf16[32,864]{1,0:T(8,128)(2,1)} %reshape.14.kmix_ref, ...), custom_call_target="tpu_custom_call" | custom-call | tf_op jit(solution)/shard_map/pallas_call | solution.py:204
  21.9 3.5 %collective-permute-start.8 = (f32[32,864]{1,0:T(8,128)}, f32[32,864]{1,0:T(8,128)S(1)}, u32[]{:S(2)}, u32[]{:S(2)}) collective-permute-start(f32[32,864]{1,0:T(8,128)} %get-tuple-element.11), channel_id=1, source_target_pairs={{0,1},{1,0},{2,3},{3,2},{4,5},{5,4},{6,7},{7,6},{8,9},{9,8},{10,11... | collective-permute-start | bytes 331784 | tf_op jit(solution)/shard_map/ppermute | solution.py:41
  25.4 1.2 %collective-permute-done.8 = f32[32,864]{1,0:T(8,128)S(1)} collective-permute-done((f32[32,864]{1,0:T(8,128)}, f32[32,864]{1,0:T(8,128)S(1)}, u32[]{:S(2)}, u32[]{:S(2)}) %collective-permute-start.8) | collective-permute-done | bytes 110624 | tf_op jit(solution)/shard_map/ppermute | solution.py:41
  26.5 0.9 %add.22 = f32[32,864]{1,0:T(8,128)S(1)} add(f32[32,864]{1,0:T(8,128)} %get-tuple-element.11, f32[32,864]{1,0:T(8,128)S(1)} %collective-permute-done.8) | non-fusion elementwise | flops 27648 | bytes 331776 | tf_op jit(solution)/shard_map/add | solution.py:42
  27.5 5.4 %collective-permute-done.9 = f32[32,864]{1,0:T(8,128)S(1)} collective-permute-done((f32[32,864]{1,0:T(8,128)S(1)}, f32[32,864]{1,0:T(8,128)S(1)}, u32[]{:S(2)}, u32[]{:S(2)}) %collective-permute-start.9) | collective-permute-done | bytes 110624 | tf_op jit(solution)/shard_map/ppermute | solution.py:41
  33.0 0.4 collective-permute-start.10
  33.4 4.4 %collective-permute-done.10 = f32[32,864]{1,0:T(8,128)S(1)} collective-permute-done((f32[32,864]{1,0:T(8,128)S(1)}, f32[32,864]{1,0:T(8,128)S(1)}, u32[]{:S(2)}, u32[]{:S(2)}) %collective-permute-start.10) | collective-permute-done | bytes 110624 | tf_op jit(solution)/shard_map/ppermute | solution.py:41
  37.8 2.2 %collective-permute-start.11 = (f32[32,864]{1,0:T(8,128)S(1)}, f32[32,864]{1,0:T(8,128)S(1)}, u32[]{:S(2)}, u32[]{:S(2)}) collective-permute-start(f32[32,864]{1,0:T(8,128)S(1)} %add.24), channel_id=1, source_target_pairs={{0,8},{4,12},{8,0},{12,4},{1,9},{5,13},{9,1},{13,5},{2,10},{6,14},... | collective-permute-start | bytes 331784 | tf_op jit(solution)/shard_map/ppermute | solution.py:41
  40.0 4.8 %collective-permute-done.11 = f32[32,864]{1,0:T(8,128)S(1)} collective-permute-done((f32[32,864]{1,0:T(8,128)S(1)}, f32[32,864]{1,0:T(8,128)S(1)}, u32[]{:S(2)}, u32[]{:S(2)}) %collective-permute-start.11) | collective-permute-done | bytes 110624 | tf_op jit(solution)/shard_map/ppermute | solution.py:41
  44.8 0.2 add.26
  45.0 1.0 %copy.13 = f32[27,32,32]{2,1,0:T(8,128)} copy(f32[27,32,32]{2,0,1:T(8,128)S(1)} %bitcast.3) | data formatting | bytes 221184
  (29 shorter events, 0.4 us)
Async XLA Ops:
  0.6 14.4 %copy-start = (bf16[27,32,32]{2,1,0:T(8,128)(2,1)S(1)}, bf16[27,32,32]{2,1,0:T(8,128)(2,1)}, u32[]{:S(2)}) copy-start(bf16[27,32,32]{2,1,0:T(8,128)(2,1)} %param.10) | copy-start | bytes 165892
  2.6 7.7 %copy-start.2 = (bf16[4,32,256]{2,1,0:T(8,128)(2,1)S(1)}, bf16[4,32,256]{2,1,0:T(8,128)(2,1)}, u32[]{:S(2)}) copy-start(bf16[4,32,256]{2,1,0:T(8,128)(2,1)} %get-tuple-element.7.rest_0_) | copy-start | bytes 196612
  2.6 7.3 %collective-permute-start.3 = (bf16[4,32,64]{2,1,0:T(8,128)(2,1)}, bf16[4,32,64]{2,1,0:T(8,128)(2,1)S(1)}, u32[]{:S(2)}, u32[]{:S(2)}) collective-permute-start(bf16[4,32,64]{2,1,0:T(8,128)(2,1)} %get-tuple-element.8), channel_id=1, source_target_pairs={{12,0},{0,4},{4,8},{8,12},{13,1},{1,5},{5,9},{9,13},{14,2},{2,6},{... | collective-permute-start | bytes 49160 | tf_op jit(solution)/shard_map/ppermute | solution.py:20
  5.7 4.5 %collective-permute-start.4 = (bf16[4,32,64]{2,1,0:T(8,128)(2,1)}, bf16[4,32,64]{2,1,0:T(8,128)(2,1)S(1)}, u32[]{:S(2)}, u32[]{:S(2)}) collective-permute-start(bf16[4,32,64]{2,1,0:T(8,128)(2,1)} %get-tuple-element.9), channel_id=1, source_target_pairs={{4,0},{8,4},{12,8},{0,12},{5,1},{9,5},{13,9},{1,13},{6,2},{10,6},{... | collective-permute-start | bytes 49160 | tf_op jit(solution)/shard_map/ppermute | solution.py:20
  10.3 4.9 %copy-start.1 = (bf16[4,32,128]{2,1,0:T(8,128)(2,1)}, bf16[4,32,128]{2,1,0:T(8,128)(2,1)S(1)}, u32[]{:S(2)}) copy-start(bf16[4,32,128]{2,1,0:T(8,128)(2,1)S(1)} %pad_maximum_fusion.rest_4_) | copy-start | bytes 98308
  10.3 3.8 %collective-permute-start.7 = (bf16[4,32,128]{2,1,0:T(8,128)(2,1)S(1)}, bf16[4,32,128]{2,1,0:T(8,128)(2,1)S(1)}, u32[]{:S(2)}, u32[]{:S(2)}) collective-permute-start(bf16[4,32,128]{2,1,0:T(8,128)(2,1)S(1)} %pad_maximum_fusion.rest_4_), channel_id=1, source_target_pairs={{0,3},{1,2},{2,1},{3,0},{4,7},{5,6},{6,5},{7,4},{8,11},{9,10},{10,... | collective-permute-start | bytes 98312 | tf_op jit(solution)/shard_map/ppermute | solution.py:230
  10.4 7.2 %collective-permute-start.2 = (bf16[4,32,256]{2,1,0:T(8,128)(2,1)S(1)}, bf16[4,32,256]{2,1,0:T(8,128)(2,1)S(1)}, u32[]{:S(2)}, u32[]{:S(2)}) collective-permute-start(bf16[4,32,256]{2,1,0:T(8,128)(2,1)S(1)} %copy-done.2), channel_id=1, source_target_pairs={{0,3},{1,2},{2,1},{3,0},{4,7},{5,6},{6,5},{7,4},{8,11},{9,10},{10,... | collective-permute-start | bytes 196616 | tf_op jit(solution)/shard_map/ppermute | solution.py:230
  12.1 5.5 %collective-permute-start.1 = (bf16[4,32,256]{2,1,0:T(8,128)(2,1)S(1)}, bf16[4,32,256]{2,1,0:T(8,128)(2,1)S(1)}, u32[]{:S(2)}, u32[]{:S(2)}) collective-permute-start(bf16[4,32,256]{2,1,0:T(8,128)(2,1)S(1)} %copy-done.2), channel_id=1, source_target_pairs={{0,2},{1,3},{2,0},{3,1},{4,6},{5,7},{6,4},{7,5},{8,10},{9,11},{10,... | collective-permute-start | bytes 196616 | tf_op jit(solution)/shard_map/ppermute | solution.py:230
  13.6 4.0 %collective-permute-start = (bf16[4,32,256]{2,1,0:T(8,128)(2,1)S(1)}, bf16[4,32,256]{2,1,0:T(8,128)(2,1)S(1)}, u32[]{:S(2)}, u32[]{:S(2)}) collective-permute-start(bf16[4,32,256]{2,1,0:T(8,128)(2,1)S(1)} %copy-done.2), channel_id=1, source_target_pairs={{0,1},{1,0},{2,3},{3,2},{4,5},{5,4},{6,7},{7,6},{8,9},{9,8},{10,11... | collective-permute-start | bytes 196616 | tf_op jit(solution)/shard_map/ppermute | solution.py:230
  13.6 4.0 %collective-permute-start.6 = (bf16[4,32,128]{2,1,0:T(8,128)(2,1)S(1)}, bf16[4,32,128]{2,1,0:T(8,128)(2,1)S(1)}, u32[]{:S(2)}, u32[]{:S(2)}) collective-permute-start(bf16[4,32,128]{2,1,0:T(8,128)(2,1)S(1)} %pad_maximum_fusion.rest_4_), channel_id=1, source_target_pairs={{0,2},{1,3},{2,0},{3,1},{4,6},{5,7},{6,4},{7,5},{8,10},{9,11},{10,... | collective-permute-start | bytes 98312 | tf_op jit(solution)/shard_map/ppermute | solution.py:230
  14.1 1.0 %copy-start.6 = (bf16[4,32,128]{2,1,0:T(8,128)(2,1)}, bf16[4,32,128]{2,1,0:T(8,128)(2,1)S(1)}, u32[]{:S(2)}) copy-start(bf16[4,32,128]{2,1,0:T(8,128)(2,1)S(1)} %collective-permute-done.7.rest_7_) | copy-start | bytes 98308
  14.1 3.4 %collective-permute-start.5 = (bf16[4,32,128]{2,1,0:T(8,128)(2,1)S(1)}, bf16[4,32,128]{2,1,0:T(8,128)(2,1)S(1)}, u32[]{:S(2)}, u32[]{:S(2)}) collective-permute-start(bf16[4,32,128]{2,1,0:T(8,128)(2,1)S(1)} %pad_maximum_fusion.rest_4_), channel_id=1, source_target_pairs={{0,1},{1,0},{2,3},{3,2},{4,5},{5,4},{6,7},{7,6},{8,9},{9,8},{10,11... | collective-permute-start | bytes 98312 | tf_op jit(solution)/shard_map/ppermute | solution.py:230
  17.5 0.6 %copy-start.7 = (bf16[4,32,128]{2,1,0:T(8,128)(2,1)}, bf16[4,32,128]{2,1,0:T(8,128)(2,1)S(1)}, u32[]{:S(2)}) copy-start(bf16[4,32,128]{2,1,0:T(8,128)(2,1)S(1)} %collective-permute-done.6.rest_6_) | copy-start | bytes 98308
  17.5 0.6 %copy-start.8 = (bf16[4,32,128]{2,1,0:T(8,128)(2,1)}, bf16[4,32,128]{2,1,0:T(8,128)(2,1)S(1)}, u32[]{:S(2)}) copy-start(bf16[4,32,128]{2,1,0:T(8,128)(2,1)S(1)} %collective-permute-done.5.rest_5_) | copy-start | bytes 98308
  17.5 0.6 %copy-start.3 = (bf16[4,32,256]{2,1,0:T(8,128)(2,1)}, bf16[4,32,256]{2,1,0:T(8,128)(2,1)S(1)}, u32[]{:S(2)}) copy-start(bf16[4,32,256]{2,1,0:T(8,128)(2,1)S(1)} %collective-permute-done.2.rest_3_) | copy-start | bytes 196612
  17.6 0.7 %copy-start.4 = (bf16[4,32,256]{2,1,0:T(8,128)(2,1)}, bf16[4,32,256]{2,1,0:T(8,128)(2,1)S(1)}, u32[]{:S(2)}) copy-start(bf16[4,32,256]{2,1,0:T(8,128)(2,1)S(1)} %collective-permute-done.1.rest_2_) | copy-start | bytes 196612
  17.6 0.6 %copy-start.5 = (bf16[4,32,256]{2,1,0:T(8,128)(2,1)}, bf16[4,32,256]{2,1,0:T(8,128)(2,1)S(1)}, u32[]{:S(2)}) copy-start(bf16[4,32,256]{2,1,0:T(8,128)(2,1)S(1)} %collective-permute-done.rest_1_) | copy-start | bytes 196612
  21.9 4.6 %collective-permute-start.8 = (f32[32,864]{1,0:T(8,128)}, f32[32,864]{1,0:T(8,128)S(1)}, u32[]{:S(2)}, u32[]{:S(2)}) collective-permute-start(f32[32,864]{1,0:T(8,128)} %get-tuple-element.11), channel_id=1, source_target_pairs={{0,1},{1,0},{2,3},{3,2},{4,5},{5,4},{6,7},{7,6},{8,9},{9,8},{10,11... | collective-permute-start | bytes 331784 | tf_op jit(solution)/shard_map/ppermute | solution.py:41
  27.5 5.5 %collective-permute-start.9 = (f32[32,864]{1,0:T(8,128)S(1)}, f32[32,864]{1,0:T(8,128)S(1)}, u32[]{:S(2)}, u32[]{:S(2)}) collective-permute-start(f32[32,864]{1,0:T(8,128)S(1)} %add.22), channel_id=1, source_target_pairs={{0,2},{2,0},{1,3},{3,1},{4,6},{6,4},{5,7},{7,5},{8,10},{10,8},{9,1... | collective-permute-start | bytes 331784 | tf_op jit(solution)/shard_map/ppermute | solution.py:41
  33.0 4.9 %collective-permute-start.10 = (f32[32,864]{1,0:T(8,128)S(1)}, f32[32,864]{1,0:T(8,128)S(1)}, u32[]{:S(2)}, u32[]{:S(2)}) collective-permute-start(f32[32,864]{1,0:T(8,128)S(1)} %add.23), channel_id=1, source_target_pairs={{0,4},{4,0},{8,12},{12,8},{1,5},{5,1},{9,13},{13,9},{2,6},{6,2},{1... | collective-permute-start | bytes 331784 | tf_op jit(solution)/shard_map/ppermute | solution.py:41
  37.8 7.0 %collective-permute-start.11 = (f32[32,864]{1,0:T(8,128)S(1)}, f32[32,864]{1,0:T(8,128)S(1)}, u32[]{:S(2)}, u32[]{:S(2)}) collective-permute-start(f32[32,864]{1,0:T(8,128)S(1)} %add.24), channel_id=1, source_target_pairs={{0,8},{4,12},{8,0},{12,4},{1,9},{5,13},{9,1},{13,5},{2,10},{6,14},... | collective-permute-start | bytes 331784 | tf_op jit(solution)/shard_map/ppermute | solution.py:41
